TPU v7x, 256 devices: a whole 4x4x8 slice. The times are simulated.
256 devices in a mesh: heads: 4 (over x), seq: 64 (over z, y, core).
Axes of the slice: x: 4, y: 4, z: 8, core: 2. Of those that a mesh axis runs over, the one named last changes fastest.
Arguments:
- queries: bfloat16 [32768, 2048], P('seq', 'heads'), may hold values from -64 to 64
- keys: bfloat16 [32768, 512], P('seq', 'heads'), may hold values from -6 to 6
- values: bfloat16 [32768, 512], P('seq', 'heads'), may hold values from -6 to 6
- vertical: int32 [16, 16], replicated, may hold values from 0 to 511, as said below
- slash: int32 [16, 8], replicated, may hold values from 0 to 15, as said below
- out_weight: bfloat16 [2048, 4096], P('heads'), may hold values from -0.25 to 0.25
Outputs:
- layer_out: bfloat16 [32768, 4096], P('seq', 'heads')
Inputs may be any that keep to these rules, and one draw needn't show every extreme that they name: `vertical`: each row lists 16 distinct blocks; the four rows of one KV head (rows 4g to 4g+3) list 64 distinct blocks in all; at most 2 of those lie within blocks k * 8 to (k + 1) * 8 - 1 for any k, and in every draw some k reaches 2. `slash`: each row lists 8 distinct offsets, 0 among them; some row holds 15 in every draw.
All inputs are finite; a program needn't handle non-finite values.
Results may differ from a plain program's by a relative error of at most 0.0095.
Values may be sent and summed in bfloat16 or wider, within the bound.
No kernel may reach another device: no remote copies, remote signals or barrier semaphores. Data moves between devices by JAX's collectives and lax.ppermute only.
A program may use at most 128 MiB of HBM per device.

v0:
```python
import math

import jax
import jax.numpy as jnp
import numpy as np
from jax import lax
from jax.sharding import Mesh
from jax.sharding import PartitionSpec as P

HEAD_SIZE = 128
BLOCK_TOKENS = 64
SEQ = ("z", "y", "core")


def shift(block, axis, size, distance):
    route = [(i, i + distance) for i in range(size) if 0 <= i + distance < size]
    return lax.ppermute(block, axis, route)


def ring(block, axis, size, distance):
    return lax.ppermute(block, axis, [(i, (i + distance) % size) for i in range(size)])


def spread(table, rows, cols):
    return jnp.repeat(jnp.repeat(table, rows, axis=-2), cols, axis=-1)


def make_local(sizes):
    heads_n, z_n, y_n, core_n = sizes
    cycle_size = z_n * y_n * core_n

    def local(queries, keys, values, vertical, slash, out_weight):
        head_dim = HEAD_SIZE
        local_heads = queries.shape[1] // head_dim
        token_count = queries.shape[0]
        block_count = token_count // BLOCK_TOKENS
        score_scale = 1.0 / math.sqrt(head_dim)
        kv_group = lax.axis_index("heads")
        core = lax.axis_index("core")
        cycle_index = lax.axis_index(SEQ)

        vert_group = lax.dynamic_slice_in_dim(vertical, kv_group * local_heads, local_heads, 0)
        slash_group = lax.dynamic_slice_in_dim(slash, kv_group * local_heads, local_heads, 0)
        union_list = vert_group.reshape(-1)
        listed_count = union_list.shape[0]
        owner_dev = union_list // block_count
        within_dev = union_list % block_count
        paired = jnp.stack([keys, values]).reshape(2, block_count, BLOCK_TOKENS, head_dim)
        owned_here = owner_dev == cycle_index
        capacity = min(block_count, max(2, 2 * listed_count // cycle_size))
        positions = jnp.arange(listed_count)
        same_owner = (owner_dev[:, None] == owner_dev[None, :]) & (
            positions[None, :] < positions[:, None]
        )
        slot_index = jnp.sum(same_owner.astype(jnp.int32), axis=1)
        selector = owned_here[None, :] & (slot_index[None, :] == jnp.arange(capacity)[:, None])
        picked = jnp.sum(jnp.where(selector, within_dev[None, :], 0), axis=1)
        outgoing = paired[:, picked].reshape(2, capacity * BLOCK_TOKENS, head_dim)
        arrived = lax.all_gather(outgoing, SEQ, axis=1, tiled=True)

        rows_total, width = out_weight.shape
        col_width = width // heads_n
        half_rows = rows_total // core_n
        fetched = []
        for distance in range(1, heads_n):
            dest_cols = ((kv_group + distance) % heads_n) * col_width
            piece = lax.dynamic_slice(out_weight, (core * half_rows, dest_cols), (half_rows, col_width))
            fetched.append(ring(piece, "heads", heads_n, distance))
        fetched = jnp.stack(fetched)
        sibling_w = ring(fetched, "core", core_n, 1)
        own_w = lax.dynamic_slice(out_weight, (0, kv_group * col_width), (rows_total, col_width))

        earlier = shift(paired, SEQ, cycle_size, 1)
        farther = shift(paired, SEQ, cycle_size, 2)
        context = jnp.concatenate([farther, earlier, paired], axis=1)
        context_blocks = context.shape[1]
        context_k = context[0].reshape(context_blocks * BLOCK_TOKENS, head_dim)
        context_v = context[1].reshape(context_blocks * BLOCK_TOKENS, head_dim)
        first_block = cycle_index * block_count
        query_block = first_block + jnp.arange(block_count, dtype=jnp.int32)
        key_block = first_block - (context_blocks - block_count) + jnp.arange(
            context_blocks, dtype=jnp.int32
        )
        distance_blk = query_block[:, None] - key_block[None, :]
        token_pos = jnp.arange(BLOCK_TOKENS)
        causal_tri = token_pos[None, :] <= token_pos[:, None]
        causal_ctx = jnp.tile(causal_tri, (block_count, context_blocks))

        query_heads = queries.reshape(token_count, local_heads, head_dim).transpose(1, 0, 2)
        score_diag = (
            jnp.einsum("htd,ud->htu", query_heads, context_k, preferred_element_type=jnp.float32)
            * score_scale
        )
        in_slash = jnp.any(distance_blk[None, None] == slash_group[:, :, None, None], axis=1)
        in_vert = jnp.any(key_block[None, None, :] == vert_group[:, :, None], axis=1)
        keep_blk = in_slash & (key_block >= 0)[None, None, :] & jnp.logical_not(in_vert)[:, None, :]
        whole_blk = keep_blk & (distance_blk != 0)[None]
        allow_diag = spread(whole_blk, BLOCK_TOKENS, BLOCK_TOKENS) | (
            spread(keep_blk & (distance_blk == 0)[None], BLOCK_TOKENS, BLOCK_TOKENS)
            & causal_ctx[None]
        )
        top_diag = jnp.max(jnp.where(allow_diag, score_diag, -jnp.inf), axis=2, keepdims=True)
        expo_diag = jnp.where(allow_diag, jnp.exp(score_diag - top_diag), 0.0)
        total_diag = jnp.sum(expo_diag, axis=2, keepdims=True)
        acc_diag = jnp.einsum(
            "htu,ud->htd",
            expo_diag.astype(jnp.bfloat16),
            context_v,
            preferred_element_type=jnp.float32,
        )

        arrived = arrived.reshape(2, cycle_size * capacity, BLOCK_TOKENS, head_dim)
        chosen = arrived[:, owner_dev * capacity + slot_index]
        vert_count = vert_group.shape[1]
        chosen = chosen.reshape(2, local_heads, vert_count * BLOCK_TOKENS, head_dim)
        score_vert = (
            jnp.einsum("htd,hud->htu", query_heads, chosen[0], preferred_element_type=jnp.float32)
            * score_scale
        )
        vert_cols = jnp.repeat(vert_group, BLOCK_TOKENS, axis=1)
        row_block = jnp.repeat(query_block, BLOCK_TOKENS)
        causal_vert = jnp.tile(causal_tri, (block_count, vert_count))
        allow_vert = (vert_cols[:, None, :] < row_block[None, :, None]) | (
            (vert_cols[:, None, :] == row_block[None, :, None]) & causal_vert[None]
        )
        top_vert = jnp.max(jnp.where(allow_vert, score_vert, -jnp.inf), axis=2, keepdims=True)
        row_top = jnp.maximum(top_diag, top_vert)
        expo_vert = jnp.where(allow_vert, jnp.exp(score_vert - row_top), 0.0)
        diag_scale = jnp.exp(top_diag - row_top)
        row_total = total_diag * diag_scale + jnp.sum(expo_vert, axis=2, keepdims=True)
        acc_vert = jnp.einsum(
            "htu,hud->htd",
            expo_vert.astype(jnp.bfloat16),
            chosen[1],
            preferred_element_type=jnp.float32,
        )
        head_out = (acc_diag * diag_scale + acc_vert) / row_total
        attention = head_out.astype(jnp.bfloat16).transpose(1, 0, 2).reshape(token_count, -1)

        total = jnp.dot(attention, own_w, preferred_element_type=jnp.float32)
        for distance in range(1, heads_n):
            other = ring(attention, "heads", heads_n, distance)
            mine = lax.dynamic_slice_in_dim(other, core * half_rows, half_rows, 1)
            theirs = lax.dynamic_slice_in_dim(other, (1 - core) * half_rows, half_rows, 1)
            total = total + jnp.dot(
                mine, fetched[distance - 1], preferred_element_type=jnp.float32
            )
            total = total + jnp.dot(
                theirs, sibling_w[distance - 1], preferred_element_type=jnp.float32
            )
        return total.astype(jnp.bfloat16)

    return local


def split_mesh(mesh):
    devices = mesh.devices
    heads_n, seq_n = devices.shape
    core_n = 2
    y_n = len({d.coords[1] for d in devices.flat})
    z_n = seq_n // (core_n * y_n)
    sizes = (heads_n, z_n, y_n, core_n)
    return Mesh(np.asarray(devices).reshape(sizes), ("heads",) + SEQ), sizes


def solution(mesh):
    sub, sizes = split_mesh(mesh)
    return jax.shard_map(
        make_local(sizes),
        mesh=sub,
        in_specs=(
            P(SEQ, "heads"),
            P(SEQ, "heads"),
            P(SEQ, "heads"),
            P(),
            P(),
            P("heads", None),
        ),
        out_specs=P(SEQ, "heads"),
        check_vma=False,
    )
```

profile of v0, /device:TPU:1, one launch (start us, length us, event | category | flops | bytes accessed | tf_op | source)
XLA Modules:
  0.0 151.8 jit_solution(9992068218329997265)
XLA Ops:
  6.5 0.8 constant_dynamic-slice_fusion
  7.3 0.1 reshape.360
  7.4 0.2 convert_reduce_fusion
  7.6 0.1 fusion.51
  7.7 1.7 %pad_maximum_fusion.1 = bf16[2,8,64,128]{3,2,1,0:T(8,128)(2,1)} fusion(bf16[1,8,64,128]{3,2,1,0:T(8,128)(2,1)} %bitcast.175, bf16[1,8,64,128]{3,2,1,0:T(8,128)(2,1)} %bitcast.177), kind=kLoop, calls=%fused_computation.41 | loop fusion | flops 131072 | bytes 524288 | tf_op jit(solution)/shard_map/stack | solution.py:48
  9.4 1.5 gather_fusion
  11.0 0.6 copy.27
  11.6 0.0 all-gather.2.cloned.1.call-update
  11.6 4.6 %collective-permute-start.1 = (bf16[2,8,64,128]{3,2,1,0:T(8,128)(2,1)}, bf16[2,8,64,128]{3,2,1,0:T(8,128)(2,1)}, u32[]{:S(2)}, u32[]{:S(2)}) collective-permute-start(bf16[2,8,64,128]{3,2,1,0:T(8,128)(2,1)} %pad_maximum_fusion.1), channel_id=1, source_target_pairs={{0,1},{1,2},{2,3},{3,4},{4,5},{5,6},{6,7},{7,8},{8,9},{9,10},{10,1... | collective-permute-start | bytes 786440 | tf_op jit(solution)/shard_map/ppermute | solution.py:17
  16.2 3.9 %collective-permute-start = (bf16[2,8,64,128]{3,2,1,0:T(8,128)(2,1)}, bf16[2,8,64,128]{3,2,1,0:T(8,128)(2,1)}, u32[]{:S(2)}, u32[]{:S(2)}) collective-permute-start(bf16[2,8,64,128]{3,2,1,0:T(8,128)(2,1)} %pad_maximum_fusion.1), channel_id=1, source_target_pairs={{0,2},{1,3},{2,4},{3,5},{4,6},{5,7},{6,8},{7,9},{8,10},{9,11},{10,... | collective-permute-start | bytes 786440 | tf_op jit(solution)/shard_map/ppermute | solution.py:17
  20.1 2.5 %fusion.57 = (bf16[256,1024]{1,0:T(8,128)(2,1)}, bf16[256,1024]{1,0:T(8,128)(2,1)}, bf16[256,1024]{1,0:T(8,128)(2,1)}) fusion(bf16[512,4096]{1,0:T(8,128)(2,1)} %param.11, s32[]{:T(128)S(6)} %select_n.128, s32[]{:T(128)S(6)} %select_n.130, s32[]{:T(128)S(6)} %select_n.135, s32[]{:T(128)S(6)} %select_n.133), kind=kLoop, calls=%fused_computation.100 | loop fusion | bytes 3145744 | tf_op jit(solution)/shard_map/dynamic_slice | solution.py:67
  22.6 2.5 %collective-permute-start.5 = (bf16[256,1024]{1,0:T(8,128)(2,1)}, bf16[256,1024]{1,0:T(8,128)(2,1)}, u32[]{:S(2)}, u32[]{:S(2)}) collective-permute-start(bf16[256,1024]{1,0:T(8,128)(2,1)} %get-tuple-element.12), channel_id=1, source_target_pairs={{0,192},{64,0},{128,64},{192,128},{1,193},{65,1},{129,65},{193,129... | collective-permute-start | bytes 1572872 | tf_op jit(solution)/shard_map/ppermute | solution.py:21
  25.1 0.5 collective-permute-start.4
  25.6 0.6 collective-permute-start.3
  26.2 0.1 reshape.363
  26.3 0.1 constant_dynamic-slice_fusion.1
  26.4 0.1 copy.21
  26.5 0.1 compare_reduce_fusion.1
  26.6 0.1 broadcast_subtract_fusion
  26.7 0.1 compare_reduce_fusion
  26.8 0.1 subtract_compare_fusion.1
  26.9 0.7 tile.4
  27.6 2.1 %and.141 = pred[512,1536]{0,1:T(8,128)(4,1)S(1)} reshape(pred[8,64,24,64]{1,0,3,2:T(8,128)(4,1)S(1)} %tile.4) | data formatting | bytes 1572864 | tf_op jit(solution)/shard_map/and | solution.py:99
  29.7 0.1 copy.23
  29.8 0.2 broadcast_in_dim.39
  30.0 0.2 reshape.357
  30.2 0.1 copy.22
  30.3 0.2 broadcast_in_dim.37
  30.5 0.2 reshape.355
  30.6 0.4 tile.5
  31.1 1.4 and.144
  32.5 0.1 broadcast_in_dim.77
  32.5 0.7 lt.99
  33.2 0.1 broadcast_in_dim.76
  33.3 0.7 lt.97
  34.0 0.6 pad_clamp_fusion
  34.6 1.1 maximum_maximum_fusion
  35.7 0.1 fusion.59
  35.8 3.4 %fusion = (f32[4,512]{1,0:T(4,128)S(1)}, f32[1536,4,512]{2,0,1:T(8,128)S(1)}) fusion(pred[512,1536]{0,1:T(8,128)(4,1)S(1)} %and.141, pred[4,512,24]{1,2,0:T(8,128)(4,1)S(1)} %reshape.357, pred[4,512,24]{1,2,0:T(8,128)(4,1)S(1)} %reshape.355, bf16[1536,128,1]{1,0,2:T(8,128)(2,1)S(1)} %bitcast.167, bf16[512,512]{1,0:T(8,128)(2,1)S(1)} %copy-done), kind=kOutput, calls=%fused_computation.4 | convolution fusion | flops 821032960 | bytes 14393344 | tf_op jit(solution)/shard_map/htd,ud->htu/dot_general | solution.py:91
  39.2 5.7 %fusion.7 = (f32[4,512]{1,0:T(4,128)S(1)}, bf16[4,512,1536]{1,2,0:T(8,128)(2,1)}) fusion(f32[1536,4,512]{2,0,1:T(8,128)S(1)} %get-tuple-element.23, f32[4,512]{1,0:T(4,128)S(1)} %get-tuple-element.22, pred[512,1536]{0,1:T(8,128)(4,1)S(1)} %and.141, pred[4,512,24]{1,2,0:T(8,128)(4,1)S(1)} %reshape.357, pred[4,512,24]{1,2,0:T(8,128)(4,1)S(1)} %reshape.355), kind=kLoop, calls=%fused_computation.15 | loop fusion | flops 22018048 | bytes 19775488 | tf_op jit(solution)/shard_map/reduce_sum | solution.py:104
  44.8 3.2 %collective-permute-done.5 = bf16[256,1024]{1,0:T(8,128)(2,1)} collective-permute-done((bf16[256,1024]{1,0:T(8,128)(2,1)}, bf16[256,1024]{1,0:T(8,128)(2,1)}, u32[]{:S(2)}, u32[]{:S(2)}) %collective-permute-start.5) | collective-permute-done | bytes 524320 | tf_op jit(solution)/shard_map/ppermute | solution.py:21
  48.0 3.9 %collective-permute-done.3 = bf16[256,1024]{1,0:T(8,128)(2,1)} collective-permute-done((bf16[256,1024]{1,0:T(8,128)(2,1)}, bf16[256,1024]{1,0:T(8,128)(2,1)}, u32[]{:S(2)}, u32[]{:S(2)}) %collective-permute-start.3) | collective-permute-done | bytes 524320 | tf_op jit(solution)/shard_map/ppermute | solution.py:21
  51.9 2.7 %pad_maximum_fusion = bf16[3,256,1024]{2,1,0:T(8,128)(2,1)} fusion(bf16[1,256,1024]{2,1,0:T(8,128)(2,1)} %bitcast.30, bf16[1,256,1024]{2,1,0:T(8,128)(2,1)} %bitcast.29, bf16[1,256,1024]{2,1,0:T(8,128)(2,1)} %bitcast.28), kind=kLoop, calls=%fused_computation.21 | loop fusion | flops 1572864 | bytes 3145728 | tf_op jit(solution)/shard_map/stack | solution.py:69
  54.7 0.4 collective-permute-start.6
  55.1 40.0 %all-gather.2.cloned.1.call-done = bf16[2,8192,128]{2,1,0:T(8,128)(2,1)} async-done(((bf16[2,128,128]{2,1,0:T(8,128)(2,1)}), bf16[2,8192,128]{2,1,0:T(8,128)(2,1)}) %all-gather.2.cloned.1.call-update) | async-done | bytes 4194320 | tf_op jit(solution)/shard_map/all_gather | solution.py:59
  95.1 3.3 %gather_fusion.1 = bf16[64,2,64,128]{3,2,1,0:T(8,128)(2,1)S(1)} fusion(bf16[2,128,64,128]{3,2,1,0:T(8,128)(2,1)} %bitcast.172, s32[1024]{0:T(1024)} %pad_clamp_fusion), kind=kCustom, calls=%fused_computation.1 | custom fusion | bytes 4194560 | tf_op jit(solution)/shard_map/gather | solution.py:113
  98.4 0.2 fusion.58
  98.6 0.5 copy-done.4
  99.1 3.0 %fusion.4 = (f32[4,512]{1,0:T(4,128)S(1)}, f32[4,1024,512]{2,1,0:T(8,128)S(1)}) fusion(pred[512,1024]{0,1:T(8,128)(4,1)S(1)} %and.144, s32[512]{0:T(512)S(1)} %copy-done.5, s32[4,1024]{1,0:T(4,128)S(1)} %copy-done.4, bf16[4,1024,128]{2,1,0:T(8,128)(2,1)S(1)} %bitcast.174, bf16[512,512]{1,0:T(8,128)(2,1)S(1)} %copy-done), kind=kOutput, calls=%fused_computation.11 | convolution fusion | flops 551548928 | bytes 10512384 | tf_op jit(solution)/shard_map/htd,hud->htu/dot_general | solution.py:117
  102.1 3.8 %fusion.9 = f32[4,512]{1,0:T(4,128)S(1)} fusion(f32[4,1024,512]{2,1,0:T(8,128)S(1)} %get-tuple-element.25, f32[4,512]{1,0:T(4,128)S(1)} %max.19, pred[512,1024]{0,1:T(8,128)(4,1)S(1)} %and.144, s32[512]{0:T(512)S(1)} %copy-done.5, s32[4,1024]{1,0:T(4,128)S(1)} %copy-done.4), kind=kLoop, calls=%fused_computation.17 | loop fusion | flops 16775168 | bytes 8947712 | tf_op jit(solution)/shard_map/reduce_sum | solution.py:130
  106.0 1.1 fusion.16
  107.1 3.8 %divide_convert_fusion = bf16[512,4,128]{0,2,1:T(8,128)(2,1)S(1)} fusion(f32[512,4,128]{0,2,1:T(8,128)S(1)} %fusion.16, bf16[4,1024,128]{2,1,0:T(8,128)(2,1)S(1)} %bitcast.173, f32[4,1024,512]{2,1,0:T(8,128)S(1)} %get-tuple-element.25, f32[4,512]{1,0:T(4,128)S(1)} %max.19, f32[512,4]{0,1:T(4,128)S(1)} %get-tuple-element.5, s32[512]{0:T(512)S(1)} %copy-done.5, ...), kind=kOutput, calls=%fused_computation.28 | convolution fusion | flops 554434560 | bytes 11569152 | tf_op jit(solution)/shard_map/htu,hud->htd/dot_general | solution.py:131
  110.9 2.8 %collective-permute-start.7 = (bf16[512,512]{0,1:T(8,128)(2,1)S(1)}, bf16[512,512]{0,1:T(8,128)(2,1)S(1)}, u32[]{:S(2)}, u32[]{:S(2)}) collective-permute-start(bf16[512,512]{0,1:T(8,128)(2,1)S(1)} %bitcast.168), channel_id=1, source_target_pairs={{0,128},{64,192},{128,0},{192,64},{1,129},{65,193},{129,1},{193,65... | collective-permute-start | bytes 1572872 | tf_op jit(solution)/shard_map/ppermute | solution.py:21
  113.7 0.9 collective-permute-start.8
  114.6 0.6 collective-permute-start.2
  115.2 1.9 %fusion.20 = f32[512,1024]{1,0:T(8,128)S(1)} fusion(bf16[512,512]{0,1:T(8,128)(2,1)S(1)} %bitcast.171, bf16[512,4096]{1,0:T(8,128)(2,1)} %param.11, s32[]{:T(128)S(6)} %select_n.127), kind=kOutput, calls=%fused_computation.26 | convolution fusion | flops 536870912 | bytes 3670020 | tf_op jit(solution)/shard_map/dot_general | solution.py:140
  117.1 8.6 %collective-permute-done.7 = bf16[512,512]{0,1:T(8,128)(2,1)S(1)} collective-permute-done((bf16[512,512]{0,1:T(8,128)(2,1)S(1)}, bf16[512,512]{0,1:T(8,128)(2,1)S(1)}, u32[]{:S(2)}, u32[]{:S(2)}) %collective-permute-start.7) | collective-permute-done | bytes 524320 | tf_op jit(solution)/shard_map/ppermute | solution.py:21
  125.7 1.5 fusion.35
  127.2 1.5 fusion.27
  128.8 8.8 %collective-permute-done.2 = bf16[512,512]{0,1:T(8,128)(2,1)S(1)} collective-permute-done((bf16[512,512]{0,1:T(8,128)(2,1)S(1)}, bf16[512,512]{0,1:T(8,128)(2,1)S(1)}, u32[]{:S(2)}, u32[]{:S(2)}) %collective-permute-start.2) | collective-permute-done | bytes 524320 | tf_op jit(solution)/shard_map/ppermute | solution.py:21
  137.6 1.5 fusion.28
  139.1 1.5 fusion.38
  140.6 1.5 fusion.32
  142.1 2.8 %add_convert_fusion = bf16[512,1024]{1,0:T(8,128)(2,1)} fusion(f32[512,1024]{1,0:T(8,128)S(1)} %fusion.32, f32[512,1024]{1,0:T(8,128)S(1)} %fusion.27, f32[512,1024]{1,0:T(8,128)S(1)} %fusion.35, f32[512,1024]{1,0:T(8,128)S(1)} %fusion.28, f32[512,1024]{1,0:T(8,128)S(1)} %fusion.20, f32[512,1024]{1,0:T(8,128)S(1)} %fusion.38, ...), kind=kOutput, calls=%fused_computation.20 | convolution fusion | flops 272105472 | bytes 14417924 | tf_op jit(solution)/shard_map/dot_general | solution.py:148
  (37 shorter events, 0.2 us)
Async XLA Ops:
  6.5 29.2 %copy-start = (bf16[512,512]{1,0:T(8,128)(2,1)S(1)}, bf16[512,512]{1,0:T(8,128)(2,1)}, u32[]{:S(2)}) copy-start(bf16[512,512]{1,0:T(8,128)(2,1)} %param.6) | copy-start | bytes 1572868
  6.5 19.8 %copy-start.6 = (s32[16,8]{0,1:T(8,128)S(1)}, s32[16,8]{0,1:T(8,128)}, u32[]{:S(2)}) copy-start(s32[16,8]{0,1:T(8,128)} %param.10) | copy-start | bytes 1540
  6.5 88.5 %all-gather.2.cloned.1.call-start = ((), (), s32[]{:S(2)}) async-start(), calls=%async_computation | async-start | bytes 4259840 | tf_op jit(solution)/shard_map/all_gather | solution.py:59
  11.6 23.0 %collective-permute-start.1 = (bf16[2,8,64,128]{3,2,1,0:T(8,128)(2,1)}, bf16[2,8,64,128]{3,2,1,0:T(8,128)(2,1)}, u32[]{:S(2)}, u32[]{:S(2)}) collective-permute-start(bf16[2,8,64,128]{3,2,1,0:T(8,128)(2,1)} %pad_maximum_fusion.1), channel_id=1, source_target_pairs={{0,1},{1,2},{2,3},{3,4},{4,5},{5,6},{6,7},{7,8},{8,9},{9,10},{10,1... | collective-permute-start | bytes 786440 | tf_op jit(solution)/shard_map/ppermute | solution.py:17
  16.2 18.4 %collective-permute-start = (bf16[2,8,64,128]{3,2,1,0:T(8,128)(2,1)}, bf16[2,8,64,128]{3,2,1,0:T(8,128)(2,1)}, u32[]{:S(2)}, u32[]{:S(2)}) collective-permute-start(bf16[2,8,64,128]{3,2,1,0:T(8,128)(2,1)} %pad_maximum_fusion.1), channel_id=1, source_target_pairs={{0,2},{1,3},{2,4},{3,5},{4,6},{5,7},{6,8},{7,9},{8,10},{9,11},{10,... | collective-permute-start | bytes 786440 | tf_op jit(solution)/shard_map/ppermute | solution.py:17
  22.6 25.4 %collective-permute-start.5 = (bf16[256,1024]{1,0:T(8,128)(2,1)}, bf16[256,1024]{1,0:T(8,128)(2,1)}, u32[]{:S(2)}, u32[]{:S(2)}) collective-permute-start(bf16[256,1024]{1,0:T(8,128)(2,1)} %get-tuple-element.12), channel_id=1, source_target_pairs={{0,192},{64,0},{128,64},{192,128},{1,193},{65,1},{129,65},{193,129... | collective-permute-start | bytes 1572872 | tf_op jit(solution)/shard_map/ppermute | solution.py:21
  25.1 22.9 %collective-permute-start.4 = (bf16[256,1024]{1,0:T(8,128)(2,1)}, bf16[256,1024]{1,0:T(8,128)(2,1)}, u32[]{:S(2)}, u32[]{:S(2)}) collective-permute-start(bf16[256,1024]{1,0:T(8,128)(2,1)} %get-tuple-element.13), channel_id=1, source_target_pairs={{0,128},{64,192},{128,0},{192,64},{1,129},{65,193},{129,1},{193,65... | collective-permute-start | bytes 1572872 | tf_op jit(solution)/shard_map/ppermute | solution.py:21
  25.6 26.3 %collective-permute-start.3 = (bf16[256,1024]{1,0:T(8,128)(2,1)}, bf16[256,1024]{1,0:T(8,128)(2,1)}, u32[]{:S(2)}, u32[]{:S(2)}) collective-permute-start(bf16[256,1024]{1,0:T(8,128)(2,1)} %get-tuple-element.11), channel_id=1, source_target_pairs={{0,64},{64,128},{128,192},{192,0},{1,65},{65,129},{129,193},{193,1... | collective-permute-start | bytes 1572872 | tf_op jit(solution)/shard_map/ppermute | solution.py:21
  27.6 7.0 %copy-start.2 = (bf16[512,128]{1,0:T(8,128)(2,1)S(1)}, bf16[512,128]{1,0:T(8,128)(2,1)}, u32[]{:S(2)}) copy-start(bf16[512,128]{1,0:T(8,128)(2,1)} %param.8) | copy-start | bytes 393220
  29.7 4.9 %copy-start.3 = (bf16[512,128]{1,0:T(8,128)(2,1)S(1)}, bf16[512,128]{1,0:T(8,128)(2,1)}, u32[]{:S(2)}) copy-start(bf16[512,128]{1,0:T(8,128)(2,1)} %param.7) | copy-start | bytes 393220
  54.7 72.6 %collective-permute-start.6 = (bf16[3,256,1024]{2,1,0:T(8,128)(2,1)}, bf16[3,256,1024]{2,1,0:T(8,128)(2,1)}, u32[]{:S(2)}, u32[]{:S(2)}) collective-permute-start(bf16[3,256,1024]{2,1,0:T(8,128)(2,1)} %pad_maximum_fusion), channel_id=1, source_target_pairs={{0,1},{1,0},{2,3},{3,2},{4,5},{5,4},{6,7},{7,6},{8,9},{9,8},{10,11... | collective-permute-start | bytes 4718600 | tf_op jit(solution)/shard_map/ppermute | solution.py:21
  98.3 0.7 copy-start.4
  98.3 0.7 copy-start.5
  98.4 7.6 %slice-start = ((s8[6291456]{0:T(1024)(128)(4,1)}), s8[4194304]{0:T(1024)(128)(4,1)S(1)}, s32[]{:S(2)}) async-start(s8[6291456]{0:T(1024)(128)(4,1)} %bitcast.165), calls=%async_computation.1 | async-start | bytes 8388608
  99.1 6.9 %slice-start.1 = ((s8[6291456]{0:T(1024)(128)(4,1)}), s8[2097152]{0:T(1024)(128)(4,1)S(1)}, s32[]{:S(2)}) async-start(s8[6291456]{0:T(1024)(128)(4,1)} %bitcast.165), calls=%async_computation.2 | async-start | bytes 4194304
  110.9 14.8 %collective-permute-start.7 = (bf16[512,512]{0,1:T(8,128)(2,1)S(1)}, bf16[512,512]{0,1:T(8,128)(2,1)S(1)}, u32[]{:S(2)}, u32[]{:S(2)}) collective-permute-start(bf16[512,512]{0,1:T(8,128)(2,1)S(1)} %bitcast.168), channel_id=1, source_target_pairs={{0,128},{64,192},{128,0},{192,64},{1,129},{65,193},{129,1},{193,65... | collective-permute-start | bytes 1572872 | tf_op jit(solution)/shard_map/ppermute | solution.py:21
  113.7 26.9 %collective-permute-start.8 = (bf16[512,512]{0,1:T(8,128)(2,1)S(1)}, bf16[512,512]{0,1:T(8,128)(2,1)S(1)}, u32[]{:S(2)}, u32[]{:S(2)}) collective-permute-start(bf16[512,512]{0,1:T(8,128)(2,1)S(1)} %bitcast.169), channel_id=1, source_target_pairs={{0,192},{64,0},{128,64},{192,128},{1,193},{65,1},{129,65},{193,129... | collective-permute-start | bytes 1572872 | tf_op jit(solution)/shard_map/ppermute | solution.py:21
  114.6 23.0 %collective-permute-start.2 = (bf16[512,512]{0,1:T(8,128)(2,1)S(1)}, bf16[512,512]{0,1:T(8,128)(2,1)S(1)}, u32[]{:S(2)}, u32[]{:S(2)}) collective-permute-start(bf16[512,512]{0,1:T(8,128)(2,1)S(1)} %bitcast.170), channel_id=1, source_target_pairs={{0,64},{64,128},{128,192},{192,0},{1,65},{65,129},{129,193},{193,1... | collective-permute-start | bytes 1572872 | tf_op jit(solution)/shard_map/ppermute | solution.py:21
  142.1 2.8 %copy-start.1 = (bf16[512,512]{1,0:T(8,128)(2,1)S(1)}, bf16[512,512]{1,0:T(8,128)(2,1)}, u32[]{:S(2)}) copy-start(bf16[512,512]{1,0:T(8,128)(2,1)} %param.6) | copy-start | bytes 1572868
Sparse Core Ops, SparseCore 0:
  11.7 83.3 all-gather.1
where the time goes:
time: 152 us
  waiting for transfers between devices  64.6 us (42%)
  matrix products  23.6 us (16%)
  local copies, waits for them, and re-layouts  16.7 us (11%)
  starting transfers between devices  16.7 us (11%)
  other arithmetic  16.4 us (11%)
  between operations  13.7 us (9%)
    all_gather x1, waiting for transfers between devices, local(): arrived = lax.all_gather(outgoing, SEQ, axis=1, tiled=True)  40 us
    ppermute x7, waiting for transfers between devices, ring(): lax.ppermute(block, axis, [(i, (i + distance) % size) for i in range(size)])  24.6 us
    ppermute x2, starting transfers between devices, shift(): return lax.ppermute(block, axis, route)  8.48 us
    ppermute x7, starting transfers between devices, ring(): lax.ppermute(block, axis, [(i, (i + distance) % size) for i in range(size)])  8.26 us
    dot_general x3, matrix products, local(): jnp.dot(theirs, sibling_w[distance - 1], preferred_element_type=jnp.float32)  5.82 us
    reduce_sum x1, other arithmetic, local(): total_diag = jnp.sum(expo_diag, axis=2, keepdims=True)  5.65 us
    dot_general x3, matrix products, local(): jnp.dot(mine, fetched[distance - 1], preferred_element_type=jnp.float32)  4.51 us
    reduce_sum x1, other arithmetic, local(): jnp.sum(expo_vert, axis=2, keepdims=True)  3.83 us
  transfers between devices with their start and end apart: 10, of which 5 were waited for; matrix products, arithmetic and copies ran while one was open for 31% of the time, Pallas kernels for 0%

commit v1 on v0

--- a/solution.py
+++ b/solution.py
@@ -113,42 +113,49 @@
         chosen = arrived[:, owner_dev * capacity + slot_index]
         vert_count = vert_group.shape[1]
         chosen = chosen.reshape(2, local_heads, vert_count * BLOCK_TOKENS, head_dim)
-        score_vert = (
-            jnp.einsum("htd,hud->htu", query_heads, chosen[0], preferred_element_type=jnp.float32)
-            * score_scale
-        )
         vert_cols = jnp.repeat(vert_group, BLOCK_TOKENS, axis=1)
         row_block = jnp.repeat(query_block, BLOCK_TOKENS)
         causal_vert = jnp.tile(causal_tri, (block_count, vert_count))
-        allow_vert = (vert_cols[:, None, :] < row_block[None, :, None]) | (
-            (vert_cols[:, None, :] == row_block[None, :, None]) & causal_vert[None]
-        )
-        top_vert = jnp.max(jnp.where(allow_vert, score_vert, -jnp.inf), axis=2, keepdims=True)
-        row_top = jnp.maximum(top_diag, top_vert)
-        expo_vert = jnp.where(allow_vert, jnp.exp(score_vert - row_top), 0.0)
-        diag_scale = jnp.exp(top_diag - row_top)
-        row_total = total_diag * diag_scale + jnp.sum(expo_vert, axis=2, keepdims=True)
-        acc_vert = jnp.einsum(
-            "htu,hud->htd",
-            expo_vert.astype(jnp.bfloat16),
-            chosen[1],
-            preferred_element_type=jnp.float32,
-        )
-        head_out = (acc_diag * diag_scale + acc_vert) / row_total
-        attention = head_out.astype(jnp.bfloat16).transpose(1, 0, 2).reshape(token_count, -1)
-
-        total = jnp.dot(attention, own_w, preferred_element_type=jnp.float32)
-        for distance in range(1, heads_n):
-            other = ring(attention, "heads", heads_n, distance)
-            mine = lax.dynamic_slice_in_dim(other, core * half_rows, half_rows, 1)
-            theirs = lax.dynamic_slice_in_dim(other, (1 - core) * half_rows, half_rows, 1)
-            total = total + jnp.dot(
-                mine, fetched[distance - 1], preferred_element_type=jnp.float32
+        chunk_count = 2
+        chunk_rows = token_count // chunk_count
+        results = []
+        for chunk in range(chunk_count):
+            rows = slice(chunk * chunk_rows, (chunk + 1) * chunk_rows)
+            q_part = query_heads[:, rows]
+            score_vert = (
+                jnp.einsum("htd,hud->htu", q_part, chosen[0], preferred_element_type=jnp.float32)
+                * score_scale
             )
-            total = total + jnp.dot(
-                theirs, sibling_w[distance - 1], preferred_element_type=jnp.float32
+            blk_part = row_block[rows]
+            allow_vert = (vert_cols[:, None, :] < blk_part[None, :, None]) | (
+                (vert_cols[:, None, :] == blk_part[None, :, None]) & causal_vert[None, rows]
             )
-        return total.astype(jnp.bfloat16)
+            top_vert = jnp.max(jnp.where(allow_vert, score_vert, -jnp.inf), axis=2, keepdims=True)
+            row_top = jnp.maximum(top_diag[:, rows], top_vert)
+            expo_vert = jnp.where(allow_vert, jnp.exp(score_vert - row_top), 0.0)
+            diag_scale = jnp.exp(top_diag[:, rows] - row_top)
+            row_total = total_diag[:, rows] * diag_scale + jnp.sum(expo_vert, axis=2, keepdims=True)
+            acc_vert = jnp.einsum(
+                "htu,hud->htd",
+                expo_vert.astype(jnp.bfloat16),
+                chosen[1],
+                preferred_element_type=jnp.float32,
+            )
+            head_out = (acc_diag[:, rows] * diag_scale + acc_vert) / row_total
+            attention = head_out.astype(jnp.bfloat16).transpose(1, 0, 2).reshape(chunk_rows, -1)
+            total = jnp.dot(attention, own_w, preferred_element_type=jnp.float32)
+            for distance in range(1, heads_n):
+                other = ring(attention, "heads", heads_n, distance)
+                mine = lax.dynamic_slice_in_dim(other, core * half_rows, half_rows, 1)
+                theirs = lax.dynamic_slice_in_dim(other, (1 - core) * half_rows, half_rows, 1)
+                total = total + jnp.dot(
+                    mine, fetched[distance - 1], preferred_element_type=jnp.float32
+                )
+                total = total + jnp.dot(
+                    theirs, sibling_w[distance - 1], preferred_element_type=jnp.float32
+                )
+            results.append(total.astype(jnp.bfloat16))
+        return jnp.concatenate(results, axis=0)
 
     return local
 

time: 152 us -> 154 us (1.013)
  waiting for transfers between devices: 64.6 us -> 53.4 us
  starting transfers between devices: 16.7 us -> 22.1 us
  matrix products: 23.6 us -> 27.7 us
  local copies, waits for them, and re-layouts: 16.7 us -> 20.1 us
    ppermute x7 -> x10, waiting for transfers between devices: 24.6 us -> 11.6 us  [ring(): lax.ppermute(block, axis, [(i, (i + distance) % size) for i in range(size)])]
    ppermute x7 -> x10, starting transfers between devices: 8.26 us -> 14 us  [ring(): lax.ppermute(block, axis, [(i, (i + distance) % size) for i in range(size)])]
    dot_general x3 -> x6, matrix products: 5.82 us -> 8.46 us  [local(): jnp.dot(theirs, sibling_w[distance - 1], preferred_element_type=jnp.float32)]
    all_gather x1, waiting for transfers between devices: 40 us -> 41.8 us  [local(): arrived = lax.all_gather(outgoing, SEQ, axis=1, tiled=True)]
    unnamed x18 -> x27, local copies, waits for them, and re-layouts: 0.54 us -> 2.2 us
    dot_general x1 -> x2, matrix products: 3.02 us -> 3.58 us  [local(): jnp.einsum('htd,hud->htu', q_part, chosen[0], preferred_element_type=jnp....]
    dot_general x1 -> x2, matrix products: 3.83 us -> 4.29 us  [local(): jnp.einsum('htu,hud->htd', expo_vert.astype(jnp.bfloat16), chosen[1], pre...]
    dot_general x3 -> x6, matrix products: 4.51 us -> 4.06 us  [local(): jnp.dot(mine, fetched[distance - 1], preferred_element_type=jnp.float32)]
  transfers between devices with their start and end apart: 10 -> 13, of which waited for: 5 -> 3; matrix products, arithmetic and copies ran while one was open for 31% -> 34% of each run, Pallas kernels for 0% -> 0%
where the time goes in v1:
time: 154 us; the launch traced here: 153 us
  waiting for transfers between devices  53.4 us (35%)
  matrix products  27.7 us (18%)
  starting transfers between devices  22.1 us (14%)
  local copies, waits for them, and re-layouts  20.1 us (13%)
  other arithmetic  15.8 us (10%)
  between operations  13.9 us (9%)
    all_gather x1, waiting for transfers between devices, local(): arrived = lax.all_gather(outgoing, SEQ, axis=1, tiled=True)  41.8 us
    ppermute x10, starting transfers between devices, ring(): lax.ppermute(block, axis, [(i, (i + distance) % size) for i in range(size)])  14 us
    ppermute x10, waiting for transfers between devices, ring(): lax.ppermute(block, axis, [(i, (i + distance) % size) for i in range(size)])  11.6 us
    dot_general x6, matrix products, local(): jnp.dot(theirs, sibling_w[distance - 1], preferred_element_type=jnp.float32)  8.46 us
    ppermute x2, starting transfers between devices, shift(): return lax.ppermute(block, axis, route)  8.08 us
    dot_general x1, matrix products, local(): jnp.einsum('htd,ud->htu', query_heads, context_k, preferred_element_type=...  4.41 us
    reduce_sum x1, other arithmetic, local(): total_diag = jnp.sum(expo_diag, axis=2, keepdims=True)  4.33 us
    dot_general x2, matrix products, local(): jnp.einsum('htu,hud->htd', expo_vert.astype(jnp.bfloat16), chosen[1], pre...  4.29 us
  transfers between devices with their start and end apart: 13, of which 3 were waited for; matrix products, arithmetic and copies ran while one was open for 34% of the time, Pallas kernels for 0%

profile of v1, /device:TPU:1, one launch (start us, length us, event | category | flops | bytes accessed | tf_op | source)
XLA Modules:
  0.0 153.0 jit_solution(10107170156130318210)
XLA Ops:
  6.6 0.7 copy-done
  7.4 0.2 convert_reduce_fusion
  7.5 0.1 fusion.105
  7.7 0.4 copy-done.12
  8.1 1.7 %pad_maximum_fusion.2 = bf16[2,8,64,128]{3,2,1,0:T(8,128)(2,1)} fusion(bf16[1,8,64,128]{3,2,1,0:T(8,128)(2,1)} %bitcast.206, bf16[1,8,64,128]{3,2,1,0:T(8,128)(2,1)} %bitcast.208), kind=kLoop, calls=%fused_computation.75 | loop fusion | flops 131072 | bytes 524288 | tf_op jit(solution)/shard_map/stack | solution.py:48
  9.8 1.5 gather_fusion
  11.3 0.6 copy.31
  11.9 4.7 %collective-permute-start = (bf16[2,8,64,128]{3,2,1,0:T(8,128)(2,1)}, bf16[2,8,64,128]{3,2,1,0:T(8,128)(2,1)}, u32[]{:S(2)}, u32[]{:S(2)}) collective-permute-start(bf16[2,8,64,128]{3,2,1,0:T(8,128)(2,1)} %pad_maximum_fusion.2), channel_id=1, source_target_pairs={{0,2},{1,3},{2,4},{3,5},{4,6},{5,7},{6,8},{7,9},{8,10},{9,11},{10,... | collective-permute-start | bytes 786440 | tf_op jit(solution)/shard_map/ppermute | solution.py:17
  16.7 3.4 %collective-permute-start.1 = (bf16[2,8,64,128]{3,2,1,0:T(8,128)(2,1)}, bf16[2,8,64,128]{3,2,1,0:T(8,128)(2,1)}, u32[]{:S(2)}, u32[]{:S(2)}) collective-permute-start(bf16[2,8,64,128]{3,2,1,0:T(8,128)(2,1)} %pad_maximum_fusion.2), channel_id=1, source_target_pairs={{0,1},{1,2},{2,3},{3,4},{4,5},{5,6},{6,7},{7,8},{8,9},{9,10},{10,1... | collective-permute-start | bytes 786440 | tf_op jit(solution)/shard_map/ppermute | solution.py:17
  20.1 2.5 %fusion.116 = (bf16[256,1024]{1,0:T(8,128)(2,1)}, bf16[256,1024]{1,0:T(8,128)(2,1)}, bf16[256,1024]{1,0:T(8,128)(2,1)}) fusion(bf16[512,4096]{1,0:T(8,128)(2,1)} %param.11, s32[]{:T(128)S(6)} %select_n.140, s32[]{:T(128)S(6)} %select_n.142, s32[]{:T(128)S(6)} %select_n.147, s32[]{:T(128)S(6)} %select_n.145), kind=kLoop, calls=%fused_computation.162 | loop fusion | bytes 3145744 | tf_op jit(solution)/shard_map/dynamic_slice | solution.py:67
  22.6 1.2 collective-permute-start.3
  23.8 2.5 %collective-permute-start.4 = (bf16[256,1024]{1,0:T(8,128)(2,1)}, bf16[256,1024]{1,0:T(8,128)(2,1)S(1)}, u32[]{:S(2)}, u32[]{:S(2)}) collective-permute-start(bf16[256,1024]{1,0:T(8,128)(2,1)} %get-tuple-element.15), channel_id=1, source_target_pairs={{0,128},{64,192},{128,0},{192,64},{1,129},{65,193},{129,1},{193,65... | collective-permute-start | bytes 1572872 | tf_op jit(solution)/shard_map/ppermute | solution.py:21
  26.3 1.2 collective-permute-start.5
  27.4 0.6 reshape.351
  28.1 0.2 copy.27
  28.3 1.1 copy.28
  29.4 0.7 lt.116
  30.5 0.4 slice.77
  30.9 1.5 and.154
  33.1 0.2 broadcast_in_dim.94
  33.2 0.8 reshape.343
  34.1 0.2 broadcast_in_dim.96
  34.3 0.8 reshape.345
  35.1 0.7 tile.2
  35.8 2.1 %and.151 = pred[512,1536]{0,1:T(8,128)(4,1)S(1)} reshape(pred[8,64,24,64]{1,0,3,2:T(8,128)(4,1)S(1)} %tile.2) | data formatting | bytes 1572864 | tf_op jit(solution)/shard_map/and | solution.py:99
  37.9 0.6 fusion.107
  38.6 1.2 maximum_maximum_fusion
  39.8 4.4 %fusion = (f32[4,512]{1,0:T(4,128)S(1)}, f32[1536,4,512]{2,0,1:T(8,128)S(1)}) fusion(pred[512,1536]{0,1:T(8,128)(4,1)S(1)} %and.151, pred[4,512,24]{1,2,0:T(8,128)(4,1)} %reshape.345, pred[4,512,24]{1,2,0:T(8,128)(4,1)} %reshape.343, bf16[1536,128,1]{1,0,2:T(8,128)(2,1)S(1)} %bitcast.202, bf16[512,4,128]{2,0,1:T(8,128)(2,1)} %copy.28), kind=kOutput, calls=%fused_computation.4 | convolution fusion | flops 821032960 | bytes 14393344 | tf_op jit(solution)/shard_map/htd,ud->htu/dot_general | solution.py:91
  44.3 4.3 %fusion.4 = (f32[4,512]{1,0:T(4,128)S(1)}, bf16[4,512,1536]{1,2,0:T(8,128)(2,1)S(1)}) fusion(f32[1536,4,512]{2,0,1:T(8,128)S(1)} %get-tuple-element.34, f32[4,512]{1,0:T(4,128)S(1)} %get-tuple-element.33, pred[512,1536]{0,1:T(8,128)(4,1)S(1)} %and.151, pred[4,512,24]{1,2,0:T(8,128)(4,1)S(1)} %copy-done.9, pred[4,512,24]{1,2,0:T(8,128)(4,1)S(1)} %copy-done.8), kind=kLoop, calls=%fused_computation.9 | loop fusion | flops 22018048 | bytes 19775488 | tf_op jit(solution)/shard_map/reduce_sum | solution.py:104
  48.6 2.0 %fusion.120 = f32[4,512,128]{1,2,0:T(8,128)} fusion(bf16[4,512,1536]{1,2,0:T(8,128)(2,1)S(1)} %get-tuple-element.12, bf16[1536,128,1]{1,0,2:T(8,128)(2,1)S(1)} %bitcast.201), kind=kOutput, calls=%fused_computation.166 | convolution fusion | flops 805306368 | bytes 7733248 | tf_op jit(solution)/shard_map/htu,ud->htd/dot_general | solution.py:105
  50.6 2.4 %pad_maximum_fusion = bf16[3,256,1024]{2,1,0:T(8,128)(2,1)} fusion(bf16[1,256,1024]{2,1,0:T(8,128)(2,1)S(1)} %bitcast.194, bf16[1,256,1024]{2,1,0:T(8,128)(2,1)S(1)} %bitcast.195, bf16[1,256,1024]{2,1,0:T(8,128)(2,1)} %bitcast.32), kind=kLoop, calls=%fused_computation.35 | loop fusion | flops 1572864 | bytes 3145728 | tf_op jit(solution)/shard_map/stack | solution.py:69
  53.0 0.5 collective-permute-start.6
  53.6 41.8 %all-gather.2.cloned.1.call-done = bf16[2,8192,128]{2,1,0:T(8,128)(2,1)} async-done(((bf16[2,128,128]{2,1,0:T(8,128)(2,1)}), bf16[2,8192,128]{2,1,0:T(8,128)(2,1)}) %all-gather.2.cloned.1.call-update) | async-done | bytes 4194320 | tf_op jit(solution)/shard_map/all_gather | solution.py:59
  95.4 3.1 %gather_fusion.1 = bf16[64,2,64,128]{3,2,1,0:T(8,128)(2,1)S(1)} fusion(bf16[2,128,64,128]{3,2,1,0:T(8,128)(2,1)} %bitcast.203, s32[1024]{0:T(1024)S(1)} %pad_clamp_fusion), kind=kCustom, calls=%fused_computation.1 | custom fusion | bytes 4194560 | tf_op jit(solution)/shard_map/gather | solution.py:113
  98.5 0.2 fusion.117
  98.7 0.8 copy-done.2
  99.5 0.7 fusion.62
  100.3 2.9 %fusion.9 = (f32[4,256]{1,0:T(4,128)S(1)}, f32[4,256]{1,0:T(4,128)S(1)}, f32[4,1024,256]{2,1,0:T(8,128)S(1)}) fusion(pred[256,1024]{0,1:T(8,128)(4,1)S(1)} %copy-done.4, s32[256]{0:T(256)S(1)} %lt.118, s32[4,1024]{1,0:T(4,128)S(1)} %copy-done.10, f32[4,1024,256]{2,1,0:T(8,128)S(1)} %fusion.62, s32[256]{0:T(256)S(1)} %lt.134, ...), kind=kOutput, calls=%fused_computation.18 | convolution fusion | flops 283113472 | bytes 9988096 | tf_op jit(solution)/shard_map/htd,hud->htu/dot_general | solution.py:126
  103.2 3.8 %fusion.12 = (f32[4,256]{1,0:T(4,128)S(1)}, f32[4,256]{1,0:T(4,128)S(1)}) fusion(f32[4,1024,256]{2,1,0:T(8,128)S(1)} %get-tuple-element.32, f32[4,256]{1,0:T(4,128)S(1)} %get-tuple-element.24, pred[256,1024]{0,1:T(8,128)(4,1)S(1)} %copy-done.4, s32[256]{0:T(256)S(1)} %lt.118, s32[4,1024]{1,0:T(4,128)S(1)} %copy-done.10, f32[4,256]{1,0:T(4,128)S(1)} %get-tuple-element.25, ...), kind=kLoop, calls=%fused_computation.23 | loop fusion | flops 16775168 | bytes 8685568 | tf_op jit(solution)/shard_map/reduce_sum | solution.py:137
  107.0 2.1 %fusion.51 = bf16[4,256,128]{1,2,0:T(8,128)(2,1)S(1)} fusion(bf16[4,1024,128]{2,1,0:T(8,128)(2,1)S(1)} %bitcast.204, f32[4,1024,256]{2,1,0:T(8,128)S(1)} %get-tuple-element.32, f32[4,256]{1,0:T(4,128)S(1)} %get-tuple-element.24, f32[4,512,128]{1,2,0:T(8,128)S(1)} %copy-done.5, f32[4,256]{1,0:T(4,128)S(1)} %get-tuple-element.20, ...), kind=kOutput, calls=%fused_computation.56 | convolution fusion | flops 277348352 | bytes 6321152 | tf_op jit(solution)/shard_map/htu,hud->htd/dot_general | solution.py:138
  109.2 1.3 collective-permute-start.2
  110.5 2.4 %collective-permute-start.7 = (bf16[256,512]{0,1:T(8,128)(2,1)S(1)}, bf16[256,512]{0,1:T(8,128)(2,1)S(1)}, u32[]{:S(2)}, u32[]{:S(2)}) collective-permute-start(bf16[256,512]{0,1:T(8,128)(2,1)S(1)} %bitcast.211), channel_id=1, source_target_pairs={{0,128},{64,192},{128,0},{192,64},{1,129},{65,193},{129,1},{193,65... | collective-permute-start | bytes 786440 | tf_op jit(solution)/shard_map/ppermute | solution.py:21
  112.9 1.2 collective-permute-start.8
  114.0 2.1 %fusion.45 = bf16[4,256,128]{1,2,0:T(8,128)(2,1)S(1)} fusion(bf16[4,1024,128]{2,1,0:T(8,128)(2,1)S(1)} %bitcast.205, f32[4,1024,256]{2,1,0:T(8,128)S(1)} %fusion.62, f32[4,256]{1,0:T(4,128)S(1)} %get-tuple-element.25, f32[4,512,128]{1,2,0:T(8,128)S(1)} %copy-done.5, f32[4,256]{1,0:T(4,128)S(1)} %get-tuple-element.21, f32[4,256]{1,0:T(4,128)S(1)} %get-tuple-element.22, ...), kind=kOutput, calls=%fused_computation.54 | convolution fusion | flops 277348352 | bytes 6321152 | tf_op jit(solution)/shard_map/htu,hud->htd/dot_general | solution.py:138
  116.2 0.5 fusion.56
  116.7 0.6 collective-permute-start.9
  117.3 0.5 fusion.54
  117.7 6.9 %collective-permute-done.7 = bf16[256,512]{0,1:T(8,128)(2,1)S(1)} collective-permute-done((bf16[256,512]{0,1:T(8,128)(2,1)S(1)}, bf16[256,512]{0,1:T(8,128)(2,1)S(1)}, u32[]{:S(2)}, u32[]{:S(2)}) %collective-permute-start.7) | collective-permute-done | bytes 262176 | tf_op jit(solution)/shard_map/ppermute | solution.py:21
  124.7 0.6 collective-permute-start.10
  125.2 0.3 fusion.78
  125.5 2.6 %collective-permute-start.11 = (bf16[256,512]{0,1:T(8,128)(2,1)S(1)}, bf16[256,512]{0,1:T(8,128)(2,1)S(1)}, u32[]{:S(2)}, u32[]{:S(2)}) collective-permute-start(bf16[256,512]{0,1:T(8,128)(2,1)S(1)} %bitcast.217), channel_id=1, source_target_pairs={{0,192},{64,0},{128,64},{192,128},{1,193},{65,1},{129,65},{193,129... | collective-permute-start | bytes 786440 | tf_op jit(solution)/shard_map/ppermute | solution.py:21
  128.2 0.3 fusion.75
  128.5 1.4 fusion.59
  129.9 1.4 fusion.61
  131.3 4.6 %collective-permute-done.10 = bf16[256,512]{0,1:T(8,128)(2,1)S(1)} collective-permute-done((bf16[256,512]{0,1:T(8,128)(2,1)S(1)}, bf16[256,512]{0,1:T(8,128)(2,1)S(1)}, u32[]{:S(2)}, u32[]{:S(2)}) %collective-permute-start.10) | collective-permute-done | bytes 262176 | tf_op jit(solution)/shard_map/ppermute | solution.py:21
  135.9 1.4 fusion.58
  137.2 0.3 fusion.70
  137.6 0.3 fusion.67
  137.9 1.4 convolution_add_fusion.3
  139.3 1.4 fusion.60
  140.7 1.4 convolution_add_fusion.1
  142.1 1.5 fusion.34
  143.6 1.5 fusion.35
  145.1 1.0 pad_maximum_fusion.1
  (65 shorter events, 1.5 us)
Async XLA Ops:
  6.5 0.7 copy-start
  6.5 21.5 %copy-start.6 = (bf16[512,512]{1,0:T(8,128)(2,1)S(1)}, bf16[512,512]{1,0:T(8,128)(2,1)}, u32[]{:S(2)}) copy-start(bf16[512,512]{1,0:T(8,128)(2,1)} %param.6) | copy-start | bytes 1572868
  6.5 25.9 %copy-start.11 = (s32[16,8]{0,1:T(8,128)S(1)}, s32[16,8]{0,1:T(8,128)}, u32[]{:S(2)}) copy-start(s32[16,8]{0,1:T(8,128)} %param.10) | copy-start | bytes 1540
  6.5 88.8 %all-gather.2.cloned.1.call-start = ((), (), s32[]{:S(2)}) async-start(), calls=%async_computation | async-start | bytes 4259840 | tf_op jit(solution)/shard_map/all_gather | solution.py:59
  7.5 0.5 copy-start.12
  11.9 26.6 %collective-permute-start = (bf16[2,8,64,128]{3,2,1,0:T(8,128)(2,1)}, bf16[2,8,64,128]{3,2,1,0:T(8,128)(2,1)}, u32[]{:S(2)}, u32[]{:S(2)}) collective-permute-start(bf16[2,8,64,128]{3,2,1,0:T(8,128)(2,1)} %pad_maximum_fusion.2), channel_id=1, source_target_pairs={{0,2},{1,3},{2,4},{3,5},{4,6},{5,7},{6,8},{7,9},{8,10},{9,11},{10,... | collective-permute-start | bytes 786440 | tf_op jit(solution)/shard_map/ppermute | solution.py:17
  16.7 21.9 %collective-permute-start.1 = (bf16[2,8,64,128]{3,2,1,0:T(8,128)(2,1)}, bf16[2,8,64,128]{3,2,1,0:T(8,128)(2,1)}, u32[]{:S(2)}, u32[]{:S(2)}) collective-permute-start(bf16[2,8,64,128]{3,2,1,0:T(8,128)(2,1)} %pad_maximum_fusion.2), channel_id=1, source_target_pairs={{0,1},{1,2},{2,3},{3,4},{4,5},{5,6},{6,7},{7,8},{8,9},{9,10},{10,1... | collective-permute-start | bytes 786440 | tf_op jit(solution)/shard_map/ppermute | solution.py:17
  22.6 16.0 %copy-start.7 = (bf16[512,128]{1,0:T(8,128)(2,1)S(1)}, bf16[512,128]{1,0:T(8,128)(2,1)}, u32[]{:S(2)}) copy-start(bf16[512,128]{1,0:T(8,128)(2,1)} %param.8) | copy-start | bytes 393220
  22.6 28.0 %collective-permute-start.3 = (bf16[256,1024]{1,0:T(8,128)(2,1)}, bf16[256,1024]{1,0:T(8,128)(2,1)}, u32[]{:S(2)}, u32[]{:S(2)}) collective-permute-start(bf16[256,1024]{1,0:T(8,128)(2,1)} %get-tuple-element.13), channel_id=1, source_target_pairs={{0,64},{64,128},{128,192},{192,0},{1,65},{65,129},{129,193},{193,1... | collective-permute-start | bytes 1572872 | tf_op jit(solution)/shard_map/ppermute | solution.py:21
  23.8 26.8 %collective-permute-start.4 = (bf16[256,1024]{1,0:T(8,128)(2,1)}, bf16[256,1024]{1,0:T(8,128)(2,1)S(1)}, u32[]{:S(2)}, u32[]{:S(2)}) collective-permute-start(bf16[256,1024]{1,0:T(8,128)(2,1)} %get-tuple-element.15), channel_id=1, source_target_pairs={{0,128},{64,192},{128,0},{192,64},{1,129},{65,193},{129,1},{193,65... | collective-permute-start | bytes 1572872 | tf_op jit(solution)/shard_map/ppermute | solution.py:21
  26.3 24.4 %collective-permute-start.5 = (bf16[256,1024]{1,0:T(8,128)(2,1)}, bf16[256,1024]{1,0:T(8,128)(2,1)S(1)}, u32[]{:S(2)}, u32[]{:S(2)}) collective-permute-start(bf16[256,1024]{1,0:T(8,128)(2,1)} %get-tuple-element.14), channel_id=1, source_target_pairs={{0,192},{64,0},{128,64},{192,128},{1,193},{65,1},{129,65},{193,129... | collective-permute-start | bytes 1572872 | tf_op jit(solution)/shard_map/ppermute | solution.py:21
  39.8 4.4 %copy-start.8 = (pred[4,512,24]{1,2,0:T(8,128)(4,1)S(1)}, pred[4,512,24]{1,2,0:T(8,128)(4,1)}, u32[]{:S(2)}) copy-start(pred[4,512,24]{1,2,0:T(8,128)(4,1)} %reshape.343) | copy-start | bytes 147460
  39.8 4.4 %copy-start.9 = (pred[4,512,24]{1,2,0:T(8,128)(4,1)S(1)}, pred[4,512,24]{1,2,0:T(8,128)(4,1)}, u32[]{:S(2)}) copy-start(pred[4,512,24]{1,2,0:T(8,128)(4,1)} %reshape.345) | copy-start | bytes 147460
  53.0 75.5 %collective-permute-start.6 = (bf16[3,256,1024]{2,1,0:T(8,128)(2,1)}, bf16[3,256,1024]{2,1,0:T(8,128)(2,1)}, u32[]{:S(2)}, u32[]{:S(2)}) collective-permute-start(bf16[3,256,1024]{2,1,0:T(8,128)(2,1)} %pad_maximum_fusion), channel_id=1, source_target_pairs={{0,1},{1,0},{2,3},{3,2},{4,5},{5,4},{6,7},{7,6},{8,9},{9,8},{10,11... | collective-permute-start | bytes 4718600 | tf_op jit(solution)/shard_map/ppermute | solution.py:21
  98.5 1.0 copy-start.2
  98.5 1.7 %copy-start.4 = (pred[256,1024]{0,1:T(8,128)(4,1)S(1)}, pred[256,1024]{0,1:T(8,128)(4,1)}, u32[]{:S(2)}) copy-start(pred[256,1024]{0,1:T(8,128)(4,1)} %and.154) | copy-start | bytes 786436
  98.5 1.7 %copy-start.10 = (s32[4,1024]{1,0:T(4,128)S(1)}, s32[4,1024]{1,0:T(4,128)}, u32[]{:S(2)}) copy-start(s32[4,1024]{1,0:T(4,128)} %lt.116) | copy-start | bytes 49156
  103.2 3.9 %copy-start.5 = (f32[4,512,128]{1,2,0:T(8,128)S(1)}, f32[4,512,128]{1,2,0:T(8,128)}, u32[]{:S(2)}) copy-start(f32[4,512,128]{1,2,0:T(8,128)} %fusion.120) | copy-start | bytes 3145732
  109.2 28.7 %collective-permute-start.2 = (bf16[256,512]{0,1:T(8,128)(2,1)S(1)}, bf16[256,512]{0,1:T(8,128)(2,1)S(1)}, u32[]{:S(2)}, u32[]{:S(2)}) collective-permute-start(bf16[256,512]{0,1:T(8,128)(2,1)S(1)} %bitcast.210), channel_id=1, source_target_pairs={{0,64},{64,128},{128,192},{192,0},{1,65},{65,129},{129,193},{193,1... | collective-permute-start | bytes 786440 | tf_op jit(solution)/shard_map/ppermute | solution.py:21
  110.5 14.2 %collective-permute-start.7 = (bf16[256,512]{0,1:T(8,128)(2,1)S(1)}, bf16[256,512]{0,1:T(8,128)(2,1)S(1)}, u32[]{:S(2)}, u32[]{:S(2)}) collective-permute-start(bf16[256,512]{0,1:T(8,128)(2,1)S(1)} %bitcast.211), channel_id=1, source_target_pairs={{0,128},{64,192},{128,0},{192,64},{1,129},{65,193},{129,1},{193,65... | collective-permute-start | bytes 786440 | tf_op jit(solution)/shard_map/ppermute | solution.py:21
  112.9 12.7 %collective-permute-start.8 = (bf16[256,512]{0,1:T(8,128)(2,1)S(1)}, bf16[256,512]{0,1:T(8,128)(2,1)S(1)}, u32[]{:S(2)}, u32[]{:S(2)}) collective-permute-start(bf16[256,512]{0,1:T(8,128)(2,1)S(1)} %bitcast.212), channel_id=1, source_target_pairs={{0,192},{64,0},{128,64},{192,128},{1,193},{65,1},{129,65},{193,129... | collective-permute-start | bytes 786440 | tf_op jit(solution)/shard_map/ppermute | solution.py:21
  114.0 2.2 %copy-start.3 = (bf16[512,4096]{1,0:T(8,128)(2,1)S(1)}, bf16[512,4096]{1,0:T(8,128)(2,1)}, u32[]{:S(2)}) copy-start(bf16[512,4096]{1,0:T(8,128)(2,1)} %param.11) | copy-start | bytes 12582916
  116.7 24.0 %collective-permute-start.9 = (bf16[256,512]{0,1:T(8,128)(2,1)S(1)}, bf16[256,512]{0,1:T(8,128)(2,1)S(1)}, u32[]{:S(2)}, u32[]{:S(2)}) collective-permute-start(bf16[256,512]{0,1:T(8,128)(2,1)S(1)} %bitcast.214), channel_id=1, source_target_pairs={{0,64},{64,128},{128,192},{192,0},{1,65},{65,129},{129,193},{193,1... | collective-permute-start | bytes 786440 | tf_op jit(solution)/shard_map/ppermute | solution.py:21
  124.7 11.2 %collective-permute-start.10 = (bf16[256,512]{0,1:T(8,128)(2,1)S(1)}, bf16[256,512]{0,1:T(8,128)(2,1)S(1)}, u32[]{:S(2)}, u32[]{:S(2)}) collective-permute-start(bf16[256,512]{0,1:T(8,128)(2,1)S(1)} %bitcast.216), channel_id=1, source_target_pairs={{0,128},{64,192},{128,0},{192,64},{1,129},{65,193},{129,1},{193,65... | collective-permute-start | bytes 786440 | tf_op jit(solution)/shard_map/ppermute | solution.py:21
  125.5 12.0 %collective-permute-start.11 = (bf16[256,512]{0,1:T(8,128)(2,1)S(1)}, bf16[256,512]{0,1:T(8,128)(2,1)S(1)}, u32[]{:S(2)}, u32[]{:S(2)}) collective-permute-start(bf16[256,512]{0,1:T(8,128)(2,1)S(1)} %bitcast.217), channel_id=1, source_target_pairs={{0,192},{64,0},{128,64},{192,128},{1,193},{65,1},{129,65},{193,129... | collective-permute-start | bytes 786440 | tf_op jit(solution)/shard_map/ppermute | solution.py:21
  142.1 4.1 %copy-start.1 = (s32[16,16]{1,0:T(8,128)S(1)}, s32[16,16]{1,0:T(8,128)}, u32[]{:S(2)}) copy-start(s32[16,16]{1,0:T(8,128)} %param.9) | copy-start | bytes 3076
Sparse Core Ops, SparseCore 0:
  12.1 83.2 all-gather.1

commit v2 on v0

--- a/solution.py
+++ b/solution.py
@@ -2,8 +2,11 @@
 
 import jax
 import jax.numpy as jnp
+import functools
+
 import numpy as np
 from jax import lax
+from jax.experimental import pallas as pl
 from jax.sharding import Mesh
 from jax.sharding import PartitionSpec as P
 
@@ -23,6 +26,49 @@
 
 def spread(table, rows, cols):
     return jnp.repeat(jnp.repeat(table, rows, axis=-2), cols, axis=-1)
+
+
+def vert_kernel(q_ref, k_ref, v_ref, cols_ref, rows_ref, top_ref, tot_ref, acc_ref, o_ref, *, scale):
+    q = q_ref[0]
+    k = k_ref[0]
+    s = lax.dot_general(q, k, (((1,), (1,)), ((), ())), preferred_element_type=jnp.float32) * scale
+    n_rows, n_cols = s.shape
+    tpos = lax.broadcasted_iota(jnp.int32, (n_rows, n_cols), 0) & (BLOCK_TOKENS - 1)
+    upos = lax.broadcasted_iota(jnp.int32, (n_rows, n_cols), 1) & (BLOCK_TOKENS - 1)
+    vc = cols_ref[0]
+    rb = rows_ref[...]
+    allow = (vc < rb) | ((vc == rb) & (upos <= tpos))
+    top_v = jnp.max(jnp.where(allow, s, -jnp.inf), axis=1, keepdims=True)
+    top_d = top_ref[0]
+    top = jnp.maximum(top_d, top_v)
+    p = jnp.where(allow, jnp.exp(s - top), 0.0)
+    sc = jnp.exp(top_d - top)
+    total = tot_ref[0] * sc + jnp.sum(p, axis=1, keepdims=True)
+    acc = jnp.dot(p.astype(jnp.bfloat16), v_ref[0], preferred_element_type=jnp.float32)
+    o_ref[...] = ((acc_ref[0] * sc + acc) / total).astype(o_ref.dtype)
+
+
+def vertical_attention(q, k, v, cols, rows, top_d, tot_d, acc_d, interpret=False):
+    h, t, d = q.shape
+    u = k.shape[1]
+    kern = functools.partial(vert_kernel, scale=1.0 / math.sqrt(d))
+    return pl.pallas_call(
+        kern,
+        grid=(h,),
+        in_specs=[
+            pl.BlockSpec((1, t, d), lambda i: (i, 0, 0)),
+            pl.BlockSpec((1, u, d), lambda i: (i, 0, 0)),
+            pl.BlockSpec((1, u, d), lambda i: (i, 0, 0)),
+            pl.BlockSpec((1, 1, u), lambda i: (i, 0, 0)),
+            pl.BlockSpec((t, 1), lambda i: (0, 0)),
+            pl.BlockSpec((1, t, 1), lambda i: (i, 0, 0)),
+            pl.BlockSpec((1, t, 1), lambda i: (i, 0, 0)),
+            pl.BlockSpec((1, t, d), lambda i: (i, 0, 0)),
+        ],
+        out_specs=pl.BlockSpec((t, d), lambda i: (0, i)),
+        out_shape=jax.ShapeDtypeStruct((t, h * d), jnp.bfloat16),
+        interpret=interpret,
+    )(q, k, v, cols, rows, top_d, tot_d, acc_d)
 
 
 def make_local(sizes):
@@ -113,41 +159,25 @@
         chosen = arrived[:, owner_dev * capacity + slot_index]
         vert_count = vert_group.shape[1]
         chosen = chosen.reshape(2, local_heads, vert_count * BLOCK_TOKENS, head_dim)
-        score_vert = (
-            jnp.einsum("htd,hud->htu", query_heads, chosen[0], preferred_element_type=jnp.float32)
-            * score_scale
-        )
-        vert_cols = jnp.repeat(vert_group, BLOCK_TOKENS, axis=1)
-        row_block = jnp.repeat(query_block, BLOCK_TOKENS)
-        causal_vert = jnp.tile(causal_tri, (block_count, vert_count))
-        allow_vert = (vert_cols[:, None, :] < row_block[None, :, None]) | (
-            (vert_cols[:, None, :] == row_block[None, :, None]) & causal_vert[None]
-        )
-        top_vert = jnp.max(jnp.where(allow_vert, score_vert, -jnp.inf), axis=2, keepdims=True)
-        row_top = jnp.maximum(top_diag, top_vert)
-        expo_vert = jnp.where(allow_vert, jnp.exp(score_vert - row_top), 0.0)
-        diag_scale = jnp.exp(top_diag - row_top)
-        row_total = total_diag * diag_scale + jnp.sum(expo_vert, axis=2, keepdims=True)
-        acc_vert = jnp.einsum(
-            "htu,hud->htd",
-            expo_vert.astype(jnp.bfloat16),
-            chosen[1],
-            preferred_element_type=jnp.float32,
-        )
-        head_out = (acc_diag * diag_scale + acc_vert) / row_total
-        attention = head_out.astype(jnp.bfloat16).transpose(1, 0, 2).reshape(token_count, -1)
-
-        total = jnp.dot(attention, own_w, preferred_element_type=jnp.float32)
+        vert_cols = jnp.repeat(vert_group, BLOCK_TOKENS, axis=1)[:, None, :]
+        row_block = jnp.repeat(query_block, BLOCK_TOKENS)[:, None]
+        attention = vertical_attention(
+            query_heads, chosen[0], chosen[1], vert_cols, row_block, top_diag, total_diag, acc_diag
+        )
+
+        weight_stack = [own_w]
+        for distance in range(1, heads_n):
+            weight_stack += [fetched[distance - 1], sibling_w[distance - 1]]
+        weight_stack = jnp.concatenate(weight_stack, axis=0)
+        attention_stack = [attention]
         for distance in range(1, heads_n):
             other = ring(attention, "heads", heads_n, distance)
-            mine = lax.dynamic_slice_in_dim(other, core * half_rows, half_rows, 1)
-            theirs = lax.dynamic_slice_in_dim(other, (1 - core) * half_rows, half_rows, 1)
-            total = total + jnp.dot(
-                mine, fetched[distance - 1], preferred_element_type=jnp.float32
+            attention_stack.append(lax.dynamic_slice_in_dim(other, core * half_rows, half_rows, 1))
+            attention_stack.append(
+                lax.dynamic_slice_in_dim(other, (1 - core) * half_rows, half_rows, 1)
             )
-            total = total + jnp.dot(
-                theirs, sibling_w[distance - 1], preferred_element_type=jnp.float32
-            )
+        attention_stack = jnp.concatenate(attention_stack, axis=1)
+        total = jnp.dot(attention_stack, weight_stack, preferred_element_type=jnp.float32)
         return total.astype(jnp.bfloat16)
 
     return local

time: 152 us -> 154 us (1.013); the launches traced: 152 us -> 152 us
  waiting for transfers between devices: 64.6 us -> 44.2 us
  local copies, waits for them, and re-layouts: 16.7 us -> 31 us
  Pallas kernels: 0 us -> 11.2 us
  matrix products: 23.6 us -> 17.5 us
    all_gather x1, waiting for transfers between devices: 40 us -> 3.35 us  [local(): arrived = lax.all_gather(outgoing, SEQ, axis=1, tiled=True)]
    ppermute x7, waiting for transfers between devices: 24.6 us -> 40.9 us  [ring(): lax.ppermute(block, axis, [(i, (i + distance) % size) for i in range(size)])]
    dot_general x9 -> x1, matrix products: 19.1 us -> 5.5 us  [local(): jnp.dot(attention_stack, weight_stack, preferred_element_type=jnp.float32)]
    pallas_call x0 -> x1, Pallas kernels: none -> 11.2 us  [vertical_attention(): pl.pallas_call(kern, grid=(h,), in_specs=[pl.BlockSpec((1, t, d), lambda...]
    convert_element_type x0 -> x1, other arithmetic: none -> 10.2 us  [local(): expo_diag.astype(jnp.bfloat16)]
    reduce_sum x2 -> x0, other arithmetic: 9.49 us -> none  [the longest x1 5.65 us: local(): total_diag = jnp.sum(expo_diag, axis=2, keepdims=True)]
    unnamed x18 -> x33, local copies, waits for them, and re-layouts: 0.54 us -> 9.75 us
    dot_general x1, matrix products: 1.07 us -> 5.78 us  [local(): jnp.einsum('htu,ud->htd', expo_diag.astype(jnp.bfloat16), context_v, pref...]
  transfers between devices with their start and end apart: 10 -> 10, of which waited for: 5 -> 7; matrix products, arithmetic and copies ran while one was open for 31% -> 33% of each run, Pallas kernels for 0% -> 0%
where the time goes in v2:
time: 154 us; the launch traced here: 152 us
  waiting for transfers between devices  44.2 us (29%)
  local copies, waits for them, and re-layouts  31 us (20%)
  starting transfers between devices  17.7 us (11%)
  matrix products  17.5 us (11%)
  other arithmetic  16.9 us (11%)
  between operations  13.6 us (9%)
  Pallas kernels  11.2 us (7%)
    ppermute x7, waiting for transfers between devices, ring(): lax.ppermute(block, axis, [(i, (i + distance) % size) for i in range(size)])  40.9 us
    pallas_call x1, Pallas kernels, vertical_attention(): pl.pallas_call(kern, grid=(h,), in_specs=[pl.BlockSpec((1, t, d), lambda...  11.2 us
    convert_element_type x1, other arithmetic, local(): expo_diag.astype(jnp.bfloat16)  10.2 us
    unnamed x33, local copies, waits for them, and re-layouts  9.75 us
    ppermute x7, starting transfers between devices, ring(): lax.ppermute(block, axis, [(i, (i + distance) % size) for i in range(size)])  9.24 us
    ppermute x2, starting transfers between devices, shift(): return lax.ppermute(block, axis, route)  8.51 us
    dot_general x1, matrix products, local(): jnp.einsum('htd,ud->htu', query_heads, context_k, preferred_element_type=...  6.2 us
    dot_general x1, matrix products, local(): jnp.einsum('htu,ud->htd', expo_diag.astype(jnp.bfloat16), context_v, pref...  5.78 us
  transfers between devices with their start and end apart: 10, of which 7 were waited for; matrix products, arithmetic and copies ran while one was open for 33% of the time, Pallas kernels for 0%

profile of v2, /device:TPU:1, one launch (start us, length us, event | category | flops | bytes accessed | tf_op | source)
XLA Modules:
  0.0 152.2 jit_solution(15094589554424285153)
XLA Ops:
  6.5 0.7 copy-done
  7.2 0.1 reshape.324
  7.4 0.2 convert_reduce_fusion
  7.5 0.1 fusion.12
  7.7 1.7 %pad_maximum_fusion.1 = bf16[2,8,64,128]{3,2,1,0:T(8,128)(2,1)} fusion(bf16[1,8,64,128]{3,2,1,0:T(8,128)(2,1)} %bitcast.110, bf16[1,8,64,128]{3,2,1,0:T(8,128)(2,1)} %bitcast.112), kind=kLoop, calls=%fused_computation.21 | loop fusion | flops 131072 | bytes 524288 | tf_op jit(solution)/shard_map/stack | solution.py:94
  9.4 1.5 gather_fusion
  10.9 0.6 copy.29
  11.5 4.6 %collective-permute-start.1 = (bf16[2,8,64,128]{3,2,1,0:T(8,128)(2,1)}, bf16[2,8,64,128]{3,2,1,0:T(8,128)(2,1)}, u32[]{:S(2)}, u32[]{:S(2)}) collective-permute-start(bf16[2,8,64,128]{3,2,1,0:T(8,128)(2,1)} %pad_maximum_fusion.1), channel_id=1, source_target_pairs={{0,1},{1,2},{2,3},{3,4},{4,5},{5,6},{6,7},{7,8},{8,9},{9,10},{10,1... | collective-permute-start | bytes 786440 | tf_op jit(solution)/shard_map/ppermute | solution.py:20
  16.1 3.9 %collective-permute-start = (bf16[2,8,64,128]{3,2,1,0:T(8,128)(2,1)}, bf16[2,8,64,128]{3,2,1,0:T(8,128)(2,1)}, u32[]{:S(2)}, u32[]{:S(2)}) collective-permute-start(bf16[2,8,64,128]{3,2,1,0:T(8,128)(2,1)} %pad_maximum_fusion.1), channel_id=1, source_target_pairs={{0,2},{1,3},{2,4},{3,5},{4,6},{5,7},{6,8},{7,9},{8,10},{9,11},{10,... | collective-permute-start | bytes 786440 | tf_op jit(solution)/shard_map/ppermute | solution.py:20
  20.0 2.4 %fusion.17 = (bf16[256,1024]{1,0:T(8,128)(2,1)S(1)}, bf16[256,1024]{1,0:T(8,128)(2,1)}, bf16[256,1024]{1,0:T(8,128)(2,1)S(1)}) fusion(bf16[512,4096]{1,0:T(8,128)(2,1)} %param.11, s32[]{:T(128)S(6)} %select_n.118, s32[]{:T(128)S(6)} %select_n.124, s32[]{:T(128)S(6)} %select_n.122, s32[]{:T(128)S(6)} %select_n.126), kind=kLoop, calls=%fused_computation.70 | loop fusion | bytes 3145744 | tf_op jit(solution)/shard_map/dynamic_slice | solution.py:113
  22.4 1.2 collective-permute-start.5
  23.6 1.5 collective-permute-start.7
  25.1 1.5 %collective-permute-start.6 = (bf16[256,1024]{1,0:T(8,128)(2,1)S(1)}, bf16[256,1024]{1,0:T(8,128)(2,1)S(1)}, u32[]{:S(2)}, u32[]{:S(2)}) collective-permute-start(bf16[256,1024]{1,0:T(8,128)(2,1)S(1)} %get-tuple-element.9), channel_id=1, source_target_pairs={{0,128},{64,192},{128,0},{192,64},{1,129},{65,193},{129,1},{193,65... | collective-permute-start | bytes 1572872 | tf_op jit(solution)/shard_map/ppermute | solution.py:24
  26.6 0.1 reshape.327
  26.7 0.1 constant_dynamic-slice_fusion
  26.8 0.1 copy.30
  26.9 0.1 broadcast_subtract_fusion
  27.0 0.1 compare_reduce_fusion
  27.1 0.1 compare_reduce_fusion.1
  27.2 0.5 fusion.14
  27.7 0.1 subtract_compare_fusion.1
  27.8 9.3 %collective-permute-done.5 = bf16[256,1024]{1,0:T(8,128)(2,1)S(1)} collective-permute-done((bf16[256,1024]{1,0:T(8,128)(2,1)}, bf16[256,1024]{1,0:T(8,128)(2,1)S(1)}, u32[]{:S(2)}, u32[]{:S(2)}) %collective-permute-start.5) | collective-permute-done | bytes 524320 | tf_op jit(solution)/shard_map/ppermute | solution.py:24
  37.1 10.9 %collective-permute-done.7 = bf16[256,1024]{1,0:T(8,128)(2,1)S(1)} collective-permute-done((bf16[256,1024]{1,0:T(8,128)(2,1)S(1)}, bf16[256,1024]{1,0:T(8,128)(2,1)S(1)}, u32[]{:S(2)}, u32[]{:S(2)}) %collective-permute-start.7) | collective-permute-done | bytes 524320 | tf_op jit(solution)/shard_map/ppermute | solution.py:24
  48.0 1.3 collective-permute-done.6
  49.3 1.4 pad_maximum_fusion
  50.7 0.3 collective-permute-start.8
  51.0 0.6 fusion.11
  51.6 0.2 copy.27
  51.9 0.3 copy.28
  52.2 0.7 broadcast_in_dim_reshape.6.cols_ref
  53.0 0.9 broadcast_in_dim_reshape.8.rows_ref
  53.9 0.7 tile.2
  54.6 2.1 %and.137 = pred[512,1536]{0,1:T(8,128)(4,1)S(1)} reshape(pred[8,64,24,64]{1,0,3,2:T(8,128)(4,1)S(1)} %tile.2) | data formatting | bytes 1572864 | tf_op jit(solution)/shard_map/and | solution.py:145
  56.7 0.8 copy.32
  57.5 0.2 broadcast_in_dim.71
  57.6 0.2 reshape.330
  57.8 0.8 copy.31
  58.6 0.2 broadcast_in_dim.39
  58.8 0.2 reshape.328
  59.0 0.6 pad_clamp_fusion
  59.6 2.3 %dynamic-slice_dynamic-update-slice_fusion = bf16[2048,1024]{1,0:T(8,128)(2,1)} fusion(bf16[512,4096]{1,0:T(8,128)(2,1)} %param.11, s32[]{:T(128)S(6)} %select_n.120), kind=kLoop, calls=%fused_computation.13 | loop fusion | bytes 2097156
  61.9 1.2 maximum_maximum_fusion
  63.1 6.2 %fusion = (f32[4,512]{1,0:T(4,128)S(1)}, f32[1536,4,512]{2,0,1:T(8,128)}) fusion(pred[512,1536]{0,1:T(8,128)(4,1)S(1)} %and.137, pred[4,512,24]{1,2,0:T(8,128)(4,1)S(1)} %reshape.330, pred[4,512,24]{1,2,0:T(8,128)(4,1)S(1)} %reshape.328, bf16[1536,128,1]{1,0,2:T(8,128)(2,1)S(1)} %bitcast.108, bf16[512,4,128]{2,0,1:T(8,128)(2,1)S(1)} %copy.28), kind=kOutput, calls=%fused_computation.4 | convolution fusion | flops 821032960 | bytes 14393344 | tf_op jit(solution)/shard_map/htd,ud->htu/dot_general | solution.py:137
  69.3 1.3 copy.35.top_ref
  70.7 10.2 %fusion.4 = (bf16[4,512,1536]{1,2,0:T(8,128)(2,1)}, f32[4,512]{1,0:T(4,128)S(1)}) fusion(f32[1536,4,512]{2,0,1:T(8,128)} %get-tuple-element.21, f32[4,512]{1,0:T(4,128)S(1)} %get-tuple-element.20, pred[512,1536]{0,1:T(8,128)(4,1)S(1)} %and.137, pred[4,512,24]{1,2,0:T(8,128)(4,1)S(1)} %reshape.330, pred[4,512,24]{1,2,0:T(8,128)(4,1)S(1)} %reshape.328), kind=kLoop, calls=%fused_computation.9 | loop fusion | flops 22018048 | bytes 19775488 | tf_op jit(solution)/shard_map/convert_element_type | solution.py:153
  80.9 1.4 copy.36.tot_ref
  82.2 5.8 %fusion.20.acc_ref = f32[4,512,128]{2,1,0:T(8,128)} fusion(bf16[4,512,1536]{1,2,0:T(8,128)(2,1)} %get-tuple-element.7, bf16[1536,128,1]{1,0,2:T(8,128)(2,1)S(1)} %bitcast.107), kind=kOutput, calls=%fused_computation.73 | convolution fusion | flops 805306368 | bytes 7733248 | tf_op jit(solution)/shard_map/htu,ud->htd/dot_general | solution.py:151
  88.0 0.8 constant_dynamic-update-slice_fusion.3
  88.8 1.9 %fusion.8 = bf16[2048,1024]{1,0:T(8,128)(2,1)} fusion(bf16[2048,1024]{1,0:T(8,128)(2,1)} %constant_dynamic-update-slice_fusion.3, bf16[3,256,1024]{2,1,0:T(8,128)(2,1)} %collective-permute-done.8), kind=kLoop, calls=%fused_computation.20 | loop fusion | bytes 1048576
  90.8 0.9 constant_dynamic-update-slice_fusion.2
  91.6 3.3 %all-gather.2.cloned.1.call-done = bf16[2,8192,128]{2,1,0:T(8,128)(2,1)} async-done(((bf16[2,128,128]{2,1,0:T(8,128)(2,1)}), bf16[2,8192,128]{2,1,0:T(8,128)(2,1)}) %all-gather.2.cloned.1.call-update) | async-done | bytes 4194320 | tf_op jit(solution)/shard_map/all_gather | solution.py:105
  95.0 3.1 %gather_fusion.1 = bf16[64,2,64,128]{3,2,1,0:T(8,128)(2,1)S(1)} fusion(bf16[2,128,64,128]{3,2,1,0:T(8,128)(2,1)} %bitcast.109, s32[1024]{0:T(1024)S(1)} %pad_clamp_fusion), kind=kCustom, calls=%fused_computation.1 | custom fusion | bytes 4194560 | tf_op jit(solution)/shard_map/gather | solution.py:159
  98.1 1.6 %fusion.18 = (bf16[1,64,64,128]{3,2,0,1:T(8,128)(2,1)}, bf16[1,64,64,128]{3,2,0,1:T(8,128)(2,1)}) fusion(bf16[2,64,64,128]{3,2,0,1:T(8,128)(2,1)S(1)} %bitcast.99), kind=kLoop, calls=%fused_computation.71 | loop fusion | bytes 4194304 | tf_op jit(solution)/shard_map/slice | solution.py:165
  99.7 11.2 %shard_map.64 = bf16[512,512]{1,0:T(8,128)(2,1)} custom-call(bf16[4,512,128]{2,1,0:T(8,128)(2,1)} %bitcast.100, bf16[4,1024,128]{2,1,0:T(8,128)(2,1)} %bitcast.102, bf16[4,1024,128]{2,1,0:T(8,128)(2,1)} %bitcast.101, s32[4,1,1024]{2,1,0:T(1,128)} %broadcast_in_dim_reshape.6.cols_ref, s32[512,1]{1,0:T(8,128)} %broadcast_in_dim_reshape.8.rows_ref, ...), custom_call_target="tpu_custom_call" | custom-call | tf_op jit(solution)/shard_map/pallas_call | solution.py:55
  110.9 1.2 collective-permute-start.2
  112.0 1.9 %fusion.7 = bf16[2048,1024]{1,0:T(8,128)(2,1)} fusion(bf16[2048,1024]{1,0:T(8,128)(2,1)} %constant_dynamic-update-slice_fusion.2, bf16[3,256,1024]{2,1,0:T(8,128)(2,1)} %collective-permute-done.8), kind=kLoop, calls=%fused_computation.18 | loop fusion | bytes 1048576
  114.0 0.8 constant_dynamic-update-slice_fusion.1
  114.8 2.4 %collective-permute-start.3 = (bf16[512,512]{1,0:T(8,128)(2,1)}, bf16[512,512]{1,0:T(8,128)(2,1)S(1)}, u32[]{:S(2)}, u32[]{:S(2)}) collective-permute-start(bf16[512,512]{1,0:T(8,128)(2,1)} %shard_map.64), channel_id=1, source_target_pairs={{0,128},{64,192},{128,0},{192,64},{1,129},{65,193},{129,1},{193,65... | collective-permute-start | bytes 1572872 | tf_op jit(solution)/shard_map/ppermute | solution.py:24
  117.2 1.9 %fusion.6 = bf16[2048,1024]{1,0:T(8,128)(2,1)} fusion(bf16[2048,1024]{1,0:T(8,128)(2,1)} %constant_dynamic-update-slice_fusion.1, bf16[3,256,1024]{2,1,0:T(8,128)(2,1)} %collective-permute-done.8), kind=kLoop, calls=%fused_computation.16 | loop fusion | bytes 1048576 | tf_op jit(solution)/shard_map/concatenate | solution.py:171
  119.1 1.2 collective-permute-start.4
  120.3 5.2 %collective-permute-done.2 = bf16[512,512]{1,0:T(8,128)(2,1)S(1)} collective-permute-done((bf16[512,512]{1,0:T(8,128)(2,1)}, bf16[512,512]{1,0:T(8,128)(2,1)S(1)}, u32[]{:S(2)}, u32[]{:S(2)}) %collective-permute-start.2) | collective-permute-done | bytes 524320 | tf_op jit(solution)/shard_map/ppermute | solution.py:24
  125.6 12.1 %collective-permute-done.3 = bf16[512,512]{1,0:T(8,128)(2,1)S(1)} collective-permute-done((bf16[512,512]{1,0:T(8,128)(2,1)}, bf16[512,512]{1,0:T(8,128)(2,1)S(1)}, u32[]{:S(2)}, u32[]{:S(2)}) %collective-permute-start.3) | collective-permute-done | bytes 524320 | tf_op jit(solution)/shard_map/ppermute | solution.py:24
  137.7 2.1 %collective-permute-done.4 = bf16[512,512]{1,0:T(8,128)(2,1)S(1)} collective-permute-done((bf16[512,512]{1,0:T(8,128)(2,1)S(1)}, bf16[512,512]{1,0:T(8,128)(2,1)S(1)}, u32[]{:S(2)}, u32[]{:S(2)}) %collective-permute-start.4) | collective-permute-done | bytes 524320 | tf_op jit(solution)/shard_map/ppermute | solution.py:24
  139.9 5.5 %convolution_convert_fusion = bf16[512,1024]{1,0:T(8,128)(2,1)} fusion(bf16[512,2048]{1,0:T(8,128)(2,1)S(1)} %dynamic-slice_dynamic-update-slice_fusion.1, bf16[2048,1024]{1,0:T(8,128)(2,1)} %fusion.6), kind=kOutput, calls=%fused_computation.12 | convolution fusion | flops 2148007936 | bytes 7340032 | tf_op jit(solution)/shard_map/dot_general | solution.py:180
  (44 shorter events, 0.5 us)
Async XLA Ops:
  6.5 0.7 copy-start
  6.5 20.2 %copy-start.9 = (s32[16,8]{0,1:T(8,128)S(1)}, s32[16,8]{0,1:T(8,128)}, u32[]{:S(2)}) copy-start(s32[16,8]{0,1:T(8,128)} %param.10) | copy-start | bytes 1540
  6.5 88.4 %all-gather.2.cloned.1.call-start = ((), (), s32[]{:S(2)}) async-start(), calls=%async_computation | async-start | bytes 4259840 | tf_op jit(solution)/shard_map/all_gather | solution.py:105
  11.5 50.3 %collective-permute-start.1 = (bf16[2,8,64,128]{3,2,1,0:T(8,128)(2,1)}, bf16[2,8,64,128]{3,2,1,0:T(8,128)(2,1)}, u32[]{:S(2)}, u32[]{:S(2)}) collective-permute-start(bf16[2,8,64,128]{3,2,1,0:T(8,128)(2,1)} %pad_maximum_fusion.1), channel_id=1, source_target_pairs={{0,1},{1,2},{2,3},{3,4},{4,5},{5,6},{6,7},{7,8},{8,9},{9,10},{10,1... | collective-permute-start | bytes 786440 | tf_op jit(solution)/shard_map/ppermute | solution.py:20
  16.1 45.8 %collective-permute-start = (bf16[2,8,64,128]{3,2,1,0:T(8,128)(2,1)}, bf16[2,8,64,128]{3,2,1,0:T(8,128)(2,1)}, u32[]{:S(2)}, u32[]{:S(2)}) collective-permute-start(bf16[2,8,64,128]{3,2,1,0:T(8,128)(2,1)} %pad_maximum_fusion.1), channel_id=1, source_target_pairs={{0,2},{1,3},{2,4},{3,5},{4,6},{5,7},{6,8},{7,9},{8,10},{9,11},{10,... | collective-permute-start | bytes 786440 | tf_op jit(solution)/shard_map/ppermute | solution.py:20
  20.0 31.6 %copy-start.7 = (bf16[512,512]{1,0:T(8,128)(2,1)S(1)}, bf16[512,512]{1,0:T(8,128)(2,1)}, u32[]{:S(2)}) copy-start(bf16[512,512]{1,0:T(8,128)(2,1)} %param.6) | copy-start | bytes 1572868
  22.4 14.6 %collective-permute-start.5 = (bf16[256,1024]{1,0:T(8,128)(2,1)}, bf16[256,1024]{1,0:T(8,128)(2,1)S(1)}, u32[]{:S(2)}, u32[]{:S(2)}) collective-permute-start(bf16[256,1024]{1,0:T(8,128)(2,1)} %get-tuple-element.10), channel_id=1, source_target_pairs={{0,64},{64,128},{128,192},{192,0},{1,65},{65,129},{129,193},{193,1... | collective-permute-start | bytes 1572872 | tf_op jit(solution)/shard_map/ppermute | solution.py:24
  23.6 24.3 %collective-permute-start.7 = (bf16[256,1024]{1,0:T(8,128)(2,1)S(1)}, bf16[256,1024]{1,0:T(8,128)(2,1)S(1)}, u32[]{:S(2)}, u32[]{:S(2)}) collective-permute-start(bf16[256,1024]{1,0:T(8,128)(2,1)S(1)} %get-tuple-element.11), channel_id=1, source_target_pairs={{0,192},{64,0},{128,64},{192,128},{1,193},{65,1},{129,65},{193,129... | collective-permute-start | bytes 1572872 | tf_op jit(solution)/shard_map/ppermute | solution.py:24
  25.1 24.2 %collective-permute-start.6 = (bf16[256,1024]{1,0:T(8,128)(2,1)S(1)}, bf16[256,1024]{1,0:T(8,128)(2,1)S(1)}, u32[]{:S(2)}, u32[]{:S(2)}) collective-permute-start(bf16[256,1024]{1,0:T(8,128)(2,1)S(1)} %get-tuple-element.9), channel_id=1, source_target_pairs={{0,128},{64,192},{128,0},{192,64},{1,129},{65,193},{129,1},{193,65... | collective-permute-start | bytes 1572872 | tf_op jit(solution)/shard_map/ppermute | solution.py:24
  37.1 14.8 %copy-start.3 = (bf16[256,1024]{1,0:T(8,128)(2,1)}, bf16[256,1024]{1,0:T(8,128)(2,1)S(1)}, u32[]{:S(2)}) copy-start(bf16[256,1024]{1,0:T(8,128)(2,1)S(1)} %collective-permute-done.5) | copy-start | bytes 1572868
  49.3 2.3 %copy-start.5 = (bf16[256,1024]{1,0:T(8,128)(2,1)}, bf16[256,1024]{1,0:T(8,128)(2,1)S(1)}, u32[]{:S(2)}) copy-start(bf16[256,1024]{1,0:T(8,128)(2,1)S(1)} %collective-permute-done.6) | copy-start | bytes 1572868
  50.7 38.1 %collective-permute-start.8 = (bf16[3,256,1024]{2,1,0:T(8,128)(2,1)}, bf16[3,256,1024]{2,1,0:T(8,128)(2,1)}, u32[]{:S(2)}, u32[]{:S(2)}) collective-permute-start(bf16[3,256,1024]{2,1,0:T(8,128)(2,1)} %pad_maximum_fusion), channel_id=1, source_target_pairs={{0,1},{1,0},{2,3},{3,2},{4,5},{5,4},{6,7},{7,6},{8,9},{9,8},{10,11... | collective-permute-start | bytes 4718600 | tf_op jit(solution)/shard_map/ppermute | solution.py:24
  52.1 11.0 %copy-start.1 = (bf16[512,4,128]{2,0,1:T(8,128)(2,1)}, bf16[512,4,128]{2,0,1:T(8,128)(2,1)S(1)}, u32[]{:S(2)}) copy-start(bf16[512,4,128]{2,0,1:T(8,128)(2,1)S(1)} %copy.28) | copy-start | bytes 1572868
  53.9 8.0 %copy-start.8 = (bf16[512,128]{1,0:T(8,128)(2,1)S(1)}, bf16[512,128]{1,0:T(8,128)(2,1)}, u32[]{:S(2)}) copy-start(bf16[512,128]{1,0:T(8,128)(2,1)} %param.8) | copy-start | bytes 393220
  82.2 5.8 %copy-start.4 = (bf16[256,1024]{1,0:T(8,128)(2,1)S(1)}, bf16[256,1024]{1,0:T(8,128)(2,1)}, u32[]{:S(2)}) copy-start(bf16[256,1024]{1,0:T(8,128)(2,1)} %copy-done.3) | copy-start | bytes 1572868
  82.2 8.5 %copy-start.6 = (bf16[256,1024]{1,0:T(8,128)(2,1)S(1)}, bf16[256,1024]{1,0:T(8,128)(2,1)}, u32[]{:S(2)}) copy-start(bf16[256,1024]{1,0:T(8,128)(2,1)} %copy-done.5) | copy-start | bytes 1572868
  110.9 8.2 %copy-start.2 = (bf16[512,512]{1,0:T(8,128)(2,1)S(1)}, bf16[512,512]{1,0:T(8,128)(2,1)}, u32[]{:S(2)}) copy-start(bf16[512,512]{1,0:T(8,128)(2,1)} %shard_map.64) | copy-start | bytes 1572868
  110.9 14.6 %collective-permute-start.2 = (bf16[512,512]{1,0:T(8,128)(2,1)}, bf16[512,512]{1,0:T(8,128)(2,1)S(1)}, u32[]{:S(2)}, u32[]{:S(2)}) collective-permute-start(bf16[512,512]{1,0:T(8,128)(2,1)} %shard_map.64), channel_id=1, source_target_pairs={{0,64},{64,128},{128,192},{192,0},{1,65},{65,129},{129,193},{193,1... | collective-permute-start | bytes 1572872 | tf_op jit(solution)/shard_map/ppermute | solution.py:24
  114.8 22.8 %collective-permute-start.3 = (bf16[512,512]{1,0:T(8,128)(2,1)}, bf16[512,512]{1,0:T(8,128)(2,1)S(1)}, u32[]{:S(2)}, u32[]{:S(2)}) collective-permute-start(bf16[512,512]{1,0:T(8,128)(2,1)} %shard_map.64), channel_id=1, source_target_pairs={{0,128},{64,192},{128,0},{192,64},{1,129},{65,193},{129,1},{193,65... | collective-permute-start | bytes 1572872 | tf_op jit(solution)/shard_map/ppermute | solution.py:24
  119.1 20.7 %collective-permute-start.4 = (bf16[512,512]{1,0:T(8,128)(2,1)S(1)}, bf16[512,512]{1,0:T(8,128)(2,1)S(1)}, u32[]{:S(2)}, u32[]{:S(2)}) collective-permute-start(bf16[512,512]{1,0:T(8,128)(2,1)S(1)} %copy-done.2), channel_id=1, source_target_pairs={{0,192},{64,0},{128,64},{192,128},{1,193},{65,1},{129,65},{193,129... | collective-permute-start | bytes 1572872 | tf_op jit(solution)/shard_map/ppermute | solution.py:24
Sparse Core Ops, SparseCore 0:
  11.6 83.2 all-gather.1

commit v3 on v2

--- a/solution.py
+++ b/solution.py
@@ -93,15 +93,20 @@
         within_dev = union_list % block_count
         paired = jnp.stack([keys, values]).reshape(2, block_count, BLOCK_TOKENS, head_dim)
         owned_here = owner_dev == cycle_index
-        capacity = min(block_count, max(2, 2 * listed_count // cycle_size))
-        positions = jnp.arange(listed_count)
+        capacity = 2
+        low = jnp.min(jnp.where(owned_here, within_dev, block_count - 1))
+        high = jnp.max(jnp.where(owned_here, within_dev, 0))
+        outgoing = jnp.concatenate(
+            [
+                lax.dynamic_slice_in_dim(paired, low, 1, 1),
+                lax.dynamic_slice_in_dim(paired, high, 1, 1),
+            ],
+            axis=1,
+        ).reshape(2, capacity * BLOCK_TOKENS, head_dim)
         same_owner = (owner_dev[:, None] == owner_dev[None, :]) & (
-            positions[None, :] < positions[:, None]
+            union_list[None, :] < union_list[:, None]
         )
         slot_index = jnp.sum(same_owner.astype(jnp.int32), axis=1)
-        selector = owned_here[None, :] & (slot_index[None, :] == jnp.arange(capacity)[:, None])
-        picked = jnp.sum(jnp.where(selector, within_dev[None, :], 0), axis=1)
-        outgoing = paired[:, picked].reshape(2, capacity * BLOCK_TOKENS, head_dim)
         arrived = lax.all_gather(outgoing, SEQ, axis=1, tiled=True)
 
         rows_total, width = out_weight.shape
@@ -165,19 +170,24 @@
             query_heads, chosen[0], chosen[1], vert_cols, row_block, top_diag, total_diag, acc_diag
         )
 
-        weight_stack = [own_w]
-        for distance in range(1, heads_n):
-            weight_stack += [fetched[distance - 1], sibling_w[distance - 1]]
-        weight_stack = jnp.concatenate(weight_stack, axis=0)
-        attention_stack = [attention]
-        for distance in range(1, heads_n):
-            other = ring(attention, "heads", heads_n, distance)
-            attention_stack.append(lax.dynamic_slice_in_dim(other, core * half_rows, half_rows, 1))
-            attention_stack.append(
-                lax.dynamic_slice_in_dim(other, (1 - core) * half_rows, half_rows, 1)
+        def rows_of(distance):
+            mine, theirs = fetched[distance - 1], sibling_w[distance - 1]
+            return jnp.where(
+                core == 0,
+                jnp.concatenate([mine, theirs], axis=0),
+                jnp.concatenate([theirs, mine], axis=0),
             )
-        attention_stack = jnp.concatenate(attention_stack, axis=1)
-        total = jnp.dot(attention_stack, weight_stack, preferred_element_type=jnp.float32)
+
+        half_cols = attention.shape[1] // 2
+        behind = ring(attention, "heads", heads_n, 1)
+        ahead = ring(attention, "heads", heads_n, heads_n - 1)
+        total = jnp.dot(attention, own_w, preferred_element_type=jnp.float32)
+        far_low = ring(behind[:, :half_cols], "heads", heads_n, 1)
+        far_high = ring(ahead[:, half_cols:], "heads", heads_n, heads_n - 1)
+        total = total + jnp.dot(behind, rows_of(1), preferred_element_type=jnp.float32)
+        total = total + jnp.dot(ahead, rows_of(heads_n - 1), preferred_element_type=jnp.float32)
+        far = jnp.concatenate([far_low, far_high], axis=1)
+        total = total + jnp.dot(far, rows_of(2), preferred_element_type=jnp.float32)
         return total.astype(jnp.bfloat16)
 
     return local

time: 154 us -> 145 us (0.942)
  local copies, waits for them, and re-layouts: 31 us -> 17.8 us
  between operations: 13.6 us -> 17.5 us
  waiting for transfers between devices: 44.2 us -> 47.1 us
  other arithmetic: 16.9 us -> 14.4 us
    all_gather x1, waiting for transfers between devices: 3.35 us -> 21.7 us  [local(): arrived = lax.all_gather(outgoing, SEQ, axis=1, tiled=True)]
    ppermute x7 -> x8, waiting for transfers between devices: 40.9 us -> 25.4 us  [ring(): lax.ppermute(block, axis, [(i, (i + distance) % size) for i in range(size)])]
    unnamed x33 -> x13, local copies, waits for them, and re-layouts: 9.75 us -> 0.24 us
    convert_element_type x1, other arithmetic: 10.2 us -> 5.59 us  [local(): expo_diag.astype(jnp.bfloat16)]
    dot_general x1, matrix products: 6.2 us -> 3.4 us  [local(): jnp.einsum('htd,ud->htu', query_heads, context_k, preferred_element_type=...]
    dot_general x1 -> x4, matrix products: 5.5 us -> 7.77 us  [the longest x1 2.05 us: local(): jnp.dot(ahead, rows_of(heads_n - 1), preferred_element_type=jnp.float32)]
    gather x2 -> x0, local copies, waits for them, and re-layouts: 2.13 us -> none  [local(): outgoing = paired[:, picked].reshape(2, capacity * BLOCK_TOKENS, head_dim)]
    concatenate x2 -> x0, local copies, waits for them, and re-layouts: 1.91 us -> none  [the longest x1 1.88 us: local(): weight_stack = jnp.concatenate(weight_stack, axis=0)]
  transfers between devices with their start and end apart: 10 -> 11, of which waited for: 7 -> 5; matrix products, arithmetic and copies ran while one was open for 33% -> 31% of each run, Pallas kernels for 0% -> 8%
where the time goes in v3:
time: 145 us; the launch traced here: 144 us
  waiting for transfers between devices  47.1 us (32%)
  starting transfers between devices  19 us (13%)
  local copies, waits for them, and re-layouts  17.8 us (12%)
  between operations  17.5 us (12%)
  matrix products  16.9 us (12%)
  other arithmetic  14.4 us (10%)
  Pallas kernels  11.2 us (8%)
    ppermute x8, waiting for transfers between devices, ring(): lax.ppermute(block, axis, [(i, (i + distance) % size) for i in range(size)])  25.4 us
    all_gather x1, waiting for transfers between devices, local(): arrived = lax.all_gather(outgoing, SEQ, axis=1, tiled=True)  21.7 us
    pallas_call x1, Pallas kernels, vertical_attention(): pl.pallas_call(kern, grid=(h,), in_specs=[pl.BlockSpec((1, t, d), lambda...  11.2 us
    ppermute x8, starting transfers between devices, ring(): lax.ppermute(block, axis, [(i, (i + distance) % size) for i in range(size)])  10.9 us
    ppermute x2, starting transfers between devices, shift(): return lax.ppermute(block, axis, route)  8.04 us
    dot_general x1, matrix products, local(): jnp.einsum('htu,ud->htd', expo_diag.astype(jnp.bfloat16), context_v, pref...  5.72 us
    convert_element_type x1, other arithmetic, local(): expo_diag.astype(jnp.bfloat16)  5.59 us
    dot_general x1, matrix products, local(): jnp.einsum('htd,ud->htu', query_heads, context_k, preferred_element_type=...  3.4 us
  transfers between devices with their start and end apart: 11, of which 5 were waited for; matrix products, arithmetic and copies ran while one was open for 31% of the time, Pallas kernels for 8%

profile of v3, /device:TPU:1, one launch (start us, length us, event | category | flops | bytes accessed | tf_op | source)
XLA Modules:
  0.0 143.9 jit_solution(14939555486881996177)
XLA Ops:
  6.5 0.7 fusion.36
  7.3 0.7 select_reduce_fusion.1
  11.8 0.8 fusion.32
  12.6 0.6 pad_maximum_fusion.2
  13.2 0.0 all-gather.2.cloned.1.call-update
  13.2 1.7 %pad_maximum_fusion.1 = bf16[2,8,64,128]{3,2,1,0:T(8,128)(2,1)} fusion(bf16[1,8,64,128]{3,2,1,0:T(8,128)(2,1)} %bitcast.101, bf16[1,8,64,128]{3,2,1,0:T(8,128)(2,1)} %bitcast.98), kind=kLoop, calls=%fused_computation.47 | loop fusion | flops 131072 | bytes 524288 | tf_op jit(solution)/shard_map/stack | solution.py:94
  14.9 4.7 %collective-permute-start = (bf16[2,8,64,128]{3,2,1,0:T(8,128)(2,1)}, bf16[2,8,64,128]{3,2,1,0:T(8,128)(2,1)}, u32[]{:S(2)}, u32[]{:S(2)}) collective-permute-start(bf16[2,8,64,128]{3,2,1,0:T(8,128)(2,1)} %pad_maximum_fusion.1), channel_id=1, source_target_pairs={{0,2},{1,3},{2,4},{3,5},{4,6},{5,7},{6,8},{7,9},{8,10},{9,11},{10,... | collective-permute-start | bytes 786440 | tf_op jit(solution)/shard_map/ppermute | solution.py:20
  19.6 3.3 %collective-permute-start.1 = (bf16[2,8,64,128]{3,2,1,0:T(8,128)(2,1)}, bf16[2,8,64,128]{3,2,1,0:T(8,128)(2,1)}, u32[]{:S(2)}, u32[]{:S(2)}) collective-permute-start(bf16[2,8,64,128]{3,2,1,0:T(8,128)(2,1)} %pad_maximum_fusion.1), channel_id=1, source_target_pairs={{0,1},{1,2},{2,3},{3,4},{4,5},{5,6},{6,7},{7,8},{8,9},{9,10},{10,1... | collective-permute-start | bytes 786440 | tf_op jit(solution)/shard_map/ppermute | solution.py:20
  23.0 2.5 %fusion.45 = (bf16[256,1024]{1,0:T(8,128)(2,1)}, bf16[256,1024]{1,0:T(8,128)(2,1)}, bf16[256,1024]{1,0:T(8,128)(2,1)}) fusion(bf16[512,4096]{1,0:T(8,128)(2,1)} %param.11, s32[]{:T(128)S(6)} %select_n.131, s32[]{:T(128)S(6)} %select_n.133, s32[]{:T(128)S(6)} %select_n.137, s32[]{:T(128)S(6)} %select_n.135), kind=kLoop, calls=%fused_computation.97 | loop fusion | bytes 3145744 | tf_op jit(solution)/shard_map/dynamic_slice | solution.py:118
  25.6 1.2 collective-permute-start.3
  26.8 2.4 %collective-permute-start.4 = (bf16[256,1024]{1,0:T(8,128)(2,1)}, bf16[256,1024]{1,0:T(8,128)(2,1)S(1)}, u32[]{:S(2)}, u32[]{:S(2)}) collective-permute-start(bf16[256,1024]{1,0:T(8,128)(2,1)} %get-tuple-element.13), channel_id=1, source_target_pairs={{0,128},{64,192},{128,0},{192,64},{1,129},{65,193},{129,1},{193,65... | collective-permute-start | bytes 1572872 | tf_op jit(solution)/shard_map/ppermute | solution.py:24
  29.2 1.2 collective-permute-start.5
  30.4 0.1 reshape.284
  30.5 0.1 reshape.283
  30.6 0.1 compare_reduce_fusion.1
  30.7 0.1 constant_dynamic-slice_fusion
  30.8 0.1 copy.20
  30.9 0.1 broadcast_subtract_fusion
  30.9 0.1 compare_reduce_fusion
  31.0 0.1 subtract_compare_fusion.1
  31.1 0.1 copy.21
  31.2 0.2 broadcast_in_dim.51
  31.4 0.2 reshape.285
  31.6 0.1 copy.22
  31.7 0.0 copy-start.5
  31.7 0.2 broadcast_in_dim.53
  31.9 0.2 reshape.287
  32.1 0.7 tile.2
  32.8 2.1 %and.123 = pred[512,1536]{0,1:T(8,128)(4,1)S(1)} reshape(pred[8,64,24,64]{1,0,3,2:T(8,128)(4,1)S(1)} %tile.2) | data formatting | bytes 1572864 | tf_op jit(solution)/shard_map/and | solution.py:150
  34.9 0.2 copy.18
  35.1 0.0 copy-start.3
  35.1 0.0 copy-start.4
  35.1 0.3 copy.19
  35.4 0.1 broadcast_in_dim.26
  35.5 0.8 broadcast_in_dim_reshape.8.cols_ref
  36.3 0.1 broadcast_in_dim.50
  36.3 0.9 broadcast_in_dim_reshape.10.rows_ref
  37.2 3.6 %collective-permute-done.3 = bf16[256,1024]{1,0:T(8,128)(2,1)} collective-permute-done((bf16[256,1024]{1,0:T(8,128)(2,1)}, bf16[256,1024]{1,0:T(8,128)(2,1)}, u32[]{:S(2)}, u32[]{:S(2)}) %collective-permute-start.3) | collective-permute-done | bytes 524320 | tf_op jit(solution)/shard_map/ppermute | solution.py:24
  40.8 12.1 %collective-permute-done.4 = bf16[256,1024]{1,0:T(8,128)(2,1)S(1)} collective-permute-done((bf16[256,1024]{1,0:T(8,128)(2,1)}, bf16[256,1024]{1,0:T(8,128)(2,1)S(1)}, u32[]{:S(2)}, u32[]{:S(2)}) %collective-permute-start.4) | collective-permute-done | bytes 524320 | tf_op jit(solution)/shard_map/ppermute | solution.py:24
  53.0 2.5 %pad_maximum_fusion = bf16[3,256,1024]{2,1,0:T(8,128)(2,1)} fusion(bf16[1,256,1024]{2,1,0:T(8,128)(2,1)} %bitcast.22, bf16[1,256,1024]{2,1,0:T(8,128)(2,1)S(1)} %bitcast.93, bf16[1,256,1024]{2,1,0:T(8,128)(2,1)} %bitcast.20), kind=kLoop, calls=%fused_computation.11 | loop fusion | flops 1572864 | bytes 3145728 | tf_op jit(solution)/shard_map/stack | solution.py:120
  55.5 0.6 collective-permute-start.6
  56.1 0.2 convert_reduce_fusion
  56.3 1.1 maximum_maximum_fusion
  57.4 0.1 fusion.47
  57.5 3.4 %fusion = (f32[4,512]{1,0:T(4,128)S(1)}, f32[1536,4,512]{2,0,1:T(8,128)S(1)}) fusion(pred[512,1536]{0,1:T(8,128)(4,1)S(1)} %and.123, pred[4,512,24]{1,2,0:T(8,128)(4,1)S(1)} %reshape.287, pred[4,512,24]{1,2,0:T(8,128)(4,1)S(1)} %reshape.285, bf16[1536,128,1]{1,0,2:T(8,128)(2,1)S(1)} %bitcast.96, bf16[512,4,128]{2,0,1:T(8,128)(2,1)S(1)} %copy.19), kind=kOutput, calls=%fused_computation.3 | convolution fusion | flops 821032960 | bytes 14393344 | tf_op jit(solution)/shard_map/htd,ud->htu/dot_general | solution.py:142
  60.9 5.6 %fusion.4 = (bf16[4,512,1536]{1,2,0:T(8,128)(2,1)}, f32[4,512]{1,0:T(4,128)S(1)}) fusion(f32[1536,4,512]{2,0,1:T(8,128)S(1)} %get-tuple-element.28, f32[4,512]{1,0:T(4,128)S(1)} %get-tuple-element.27, pred[512,1536]{0,1:T(8,128)(4,1)S(1)} %and.123, pred[4,512,24]{1,2,0:T(8,128)(4,1)S(1)} %reshape.287, pred[4,512,24]{1,2,0:T(8,128)(4,1)S(1)} %reshape.285), kind=kLoop, calls=%fused_computation.8 | loop fusion | flops 22018048 | bytes 19775488 | tf_op jit(solution)/shard_map/convert_element_type | solution.py:158
  66.5 1.4 copy.26.tot_ref
  67.9 1.4 copy.25.top_ref
  69.2 5.7 %fusion.48.acc_ref = f32[4,512,128]{2,1,0:T(8,128)} fusion(bf16[4,512,1536]{1,2,0:T(8,128)(2,1)} %get-tuple-element.9, bf16[1536,128,1]{1,0,2:T(8,128)(2,1)S(1)} %bitcast.95), kind=kOutput, calls=%fused_computation.100 | convolution fusion | flops 805306368 | bytes 7733248 | tf_op jit(solution)/shard_map/htu,ud->htd/dot_general | solution.py:156
  74.9 21.7 %all-gather.2.cloned.1.call-done = bf16[2,8192,128]{2,1,0:T(8,128)(2,1)} async-done(((bf16[2,128,128]{2,1,0:T(8,128)(2,1)}), bf16[2,8192,128]{2,1,0:T(8,128)(2,1)}) %all-gather.2.cloned.1.call-update) | async-done | bytes 4194320 | tf_op jit(solution)/shard_map/all_gather | solution.py:110
  96.7 3.1 %gather_fusion = bf16[64,2,64,128]{3,2,1,0:T(8,128)(2,1)S(1)} fusion(bf16[2,128,64,128]{3,2,1,0:T(8,128)(2,1)} %bitcast.103, s32[1024]{0:T(1024)S(1)} %pad_clamp_fusion), kind=kCustom, calls=%fused_computation | custom fusion | bytes 4194560 | tf_op jit(solution)/shard_map/gather | solution.py:164
  99.8 1.5 %fusion.46 = (bf16[1,64,64,128]{3,2,0,1:T(8,128)(2,1)}, bf16[1,64,64,128]{3,2,0,1:T(8,128)(2,1)}) fusion(bf16[2,64,64,128]{3,2,0,1:T(8,128)(2,1)S(1)} %bitcast.89), kind=kLoop, calls=%fused_computation.98 | loop fusion | bytes 4194304 | tf_op jit(solution)/shard_map/slice | solution.py:170
  101.3 11.2 %shard_map.64 = bf16[512,512]{1,0:T(8,128)(2,1)} custom-call(bf16[4,512,128]{2,1,0:T(8,128)(2,1)} %bitcast.90, bf16[4,1024,128]{2,1,0:T(8,128)(2,1)} %bitcast.92, bf16[4,1024,128]{2,1,0:T(8,128)(2,1)} %bitcast.91, s32[4,1,1024]{2,1,0:T(1,128)} %broadcast_in_dim_reshape.8.cols_ref, s32[512,1]{1,0:T(8,128)} %broadcast_in_dim_reshape.10.rows_ref, ...), custom_call_target="tpu_custom_call" | custom-call | tf_op jit(solution)/shard_map/pallas_call | solution.py:55
  112.5 1.2 collective-permute-start.2
  113.7 1.5 %collective-permute-start.7 = (bf16[512,512]{1,0:T(8,128)(2,1)}, bf16[512,512]{1,0:T(8,128)(2,1)S(1)}, u32[]{:S(2)}, u32[]{:S(2)}) collective-permute-start(bf16[512,512]{1,0:T(8,128)(2,1)} %shard_map.64), channel_id=1, source_target_pairs={{0,192},{64,0},{128,64},{192,128},{1,193},{65,1},{129,65},{193,129... | collective-permute-start | bytes 1572872 | tf_op jit(solution)/shard_map/ppermute | solution.py:24
  115.2 1.5 %slice_bitcast_fusion = (bf16[256,1024]{1,0:T(8,128)(2,1)S(1)}, bf16[256,1024]{1,0:T(8,128)(2,1)S(1)}, bf16[256,1024]{1,0:T(8,128)(2,1)S(1)}) fusion(bf16[3,256,1024]{2,1,0:T(8,128)(2,1)} %collective-permute-done.6), kind=kLoop, calls=%fused_computation.39 | loop fusion | bytes 3145728 | tf_op jit(solution)/shard_map/squeeze | solution.py:174
  116.7 1.9 %fusion.24 = f32[512,1024]{1,0:T(8,128)S(1)} fusion(bf16[512,512]{1,0:T(8,128)(2,1)S(1)} %copy-done.2, bf16[512,4096]{1,0:T(8,128)(2,1)} %param.11, s32[]{:T(128)S(6)} %select_n.129), kind=kOutput, calls=%fused_computation.33 | convolution fusion | flops 536870912 | bytes 3670020 | tf_op jit(solution)/shard_map/dot_general | solution.py:184
  118.6 8.5 %collective-permute-done.2 = bf16[512,512]{1,0:T(8,128)(2,1)S(1)} collective-permute-done((bf16[512,512]{1,0:T(8,128)(2,1)}, bf16[512,512]{1,0:T(8,128)(2,1)S(1)}, u32[]{:S(2)}, u32[]{:S(2)}) %collective-permute-start.2) | collective-permute-done | bytes 524320 | tf_op jit(solution)/shard_map/ppermute | solution.py:24
  127.2 0.1 collective-permute-start.8
  127.3 2.7 %collective-permute-start.9 = (bf16[512,256]{1,0:T(8,128)(2,1)S(1)}, bf16[512,256]{1,0:T(8,128)(2,1)S(1)}, u32[]{:S(2)}, u32[]{:S(2)}) collective-permute-start(bf16[512,256]{1,0:T(8,128)(2,1)S(1)} %slice.47), channel_id=1, source_target_pairs={{0,192},{64,0},{128,64},{192,128},{1,193},{65,1},{129,65},{193,129... | collective-permute-start | bytes 786440 | tf_op jit(solution)/shard_map/ppermute | solution.py:24
  130.0 1.9 %fusion.6 = f32[512,1024]{1,0:T(8,128)S(1)} fusion(bf16[512,512]{1,0:T(8,128)(2,1)S(1)} %collective-permute-done.2, bf16[256,1024]{1,0:T(8,128)(2,1)S(1)} %get-tuple-element.18, bf16[256,1024]{1,0:T(8,128)(2,1)} %collective-permute-done.3, pred[]{:T(512)S(6)} %eq.77), kind=kOutput, calls=%fused_computation.13 | convolution fusion | flops 541589504 | bytes 3670017 | tf_op jit(solution)/shard_map/dot_general | solution.py:187
  132.0 2.0 %fusion.12 = f32[512,1024]{1,0:T(8,128)S(1)} fusion(bf16[512,512]{1,0:T(8,128)(2,1)S(1)} %collective-permute-done.7, bf16[256,1024]{1,0:T(8,128)(2,1)S(1)} %get-tuple-element.17, bf16[256,1024]{1,0:T(8,128)(2,1)} %collective-permute-done.5, pred[]{:T(512)S(6)} %eq.77), kind=kOutput, calls=%fused_computation.20 | convolution fusion | flops 541589504 | bytes 3670017 | tf_op jit(solution)/shard_map/dot_general | solution.py:188
  134.0 1.2 collective-permute-done.8
  135.2 1.8 %add_convert_fusion = bf16[512,1024]{1,0:T(8,128)(2,1)} fusion(f32[512,1024]{1,0:T(8,128)S(1)} %fusion.12, f32[512,1024]{1,0:T(8,128)S(1)} %fusion.24, f32[512,1024]{1,0:T(8,128)S(1)} %fusion.6, bf16[256,1024]{1,0:T(8,128)(2,1)S(1)} %get-tuple-element.16, bf16[256,1024]{1,0:T(8,128)(2,1)S(1)} %collective-permute-done.4, pred[]{:T(512)S(6)} %eq.77, ...), kind=kOutput, calls=%fused_computation.10 | convolution fusion | flops 544735232 | bytes 8912897 | tf_op jit(solution)/shard_map/dot_general | solution.py:190
  (27 shorter events, 0.1 us)
Async XLA Ops:
  6.5 24.1 %copy-start = (s32[16,8]{0,1:T(8,128)S(1)}, s32[16,8]{0,1:T(8,128)}, u32[]{:S(2)}) copy-start(s32[16,8]{0,1:T(8,128)} %param.10) | copy-start | bytes 1540
  6.5 90.1 %all-gather.2.cloned.1.call-start = ((), (), s32[]{:S(2)}) async-start(), calls=%async_computation | async-start | bytes 4259840 | tf_op jit(solution)/shard_map/all_gather | solution.py:110
  14.9 41.4 %collective-permute-start = (bf16[2,8,64,128]{3,2,1,0:T(8,128)(2,1)}, bf16[2,8,64,128]{3,2,1,0:T(8,128)(2,1)}, u32[]{:S(2)}, u32[]{:S(2)}) collective-permute-start(bf16[2,8,64,128]{3,2,1,0:T(8,128)(2,1)} %pad_maximum_fusion.1), channel_id=1, source_target_pairs={{0,2},{1,3},{2,4},{3,5},{4,6},{5,7},{6,8},{7,9},{8,10},{9,11},{10,... | collective-permute-start | bytes 786440 | tf_op jit(solution)/shard_map/ppermute | solution.py:20
  19.6 36.7 %collective-permute-start.1 = (bf16[2,8,64,128]{3,2,1,0:T(8,128)(2,1)}, bf16[2,8,64,128]{3,2,1,0:T(8,128)(2,1)}, u32[]{:S(2)}, u32[]{:S(2)}) collective-permute-start(bf16[2,8,64,128]{3,2,1,0:T(8,128)(2,1)} %pad_maximum_fusion.1), channel_id=1, source_target_pairs={{0,1},{1,2},{2,3},{3,4},{4,5},{5,6},{6,7},{7,8},{8,9},{9,10},{10,1... | collective-permute-start | bytes 786440 | tf_op jit(solution)/shard_map/ppermute | solution.py:20
  25.6 15.3 %collective-permute-start.3 = (bf16[256,1024]{1,0:T(8,128)(2,1)}, bf16[256,1024]{1,0:T(8,128)(2,1)}, u32[]{:S(2)}, u32[]{:S(2)}) collective-permute-start(bf16[256,1024]{1,0:T(8,128)(2,1)} %get-tuple-element.11), channel_id=1, source_target_pairs={{0,64},{64,128},{128,192},{192,0},{1,65},{65,129},{129,193},{193,1... | collective-permute-start | bytes 1572872 | tf_op jit(solution)/shard_map/ppermute | solution.py:24
  26.8 26.2 %collective-permute-start.4 = (bf16[256,1024]{1,0:T(8,128)(2,1)}, bf16[256,1024]{1,0:T(8,128)(2,1)S(1)}, u32[]{:S(2)}, u32[]{:S(2)}) collective-permute-start(bf16[256,1024]{1,0:T(8,128)(2,1)} %get-tuple-element.13), channel_id=1, source_target_pairs={{0,128},{64,192},{128,0},{192,64},{1,129},{65,193},{129,1},{193,65... | collective-permute-start | bytes 1572872 | tf_op jit(solution)/shard_map/ppermute | solution.py:24
  29.2 23.7 %collective-permute-start.5 = (bf16[256,1024]{1,0:T(8,128)(2,1)}, bf16[256,1024]{1,0:T(8,128)(2,1)}, u32[]{:S(2)}, u32[]{:S(2)}) collective-permute-start(bf16[256,1024]{1,0:T(8,128)(2,1)} %get-tuple-element.12), channel_id=1, source_target_pairs={{0,192},{64,0},{128,64},{192,128},{1,193},{65,1},{129,65},{193,129... | collective-permute-start | bytes 1572872 | tf_op jit(solution)/shard_map/ppermute | solution.py:24
  31.7 3.2 %copy-start.5 = (bf16[512,512]{1,0:T(8,128)(2,1)S(1)}, bf16[512,512]{1,0:T(8,128)(2,1)}, u32[]{:S(2)}) copy-start(bf16[512,512]{1,0:T(8,128)(2,1)} %param.6) | copy-start | bytes 1572868
  35.1 21.2 %copy-start.3 = (bf16[512,128]{1,0:T(8,128)(2,1)S(1)}, bf16[512,128]{1,0:T(8,128)(2,1)}, u32[]{:S(2)}) copy-start(bf16[512,128]{1,0:T(8,128)(2,1)} %param.7) | copy-start | bytes 393220
  35.1 21.2 %copy-start.4 = (bf16[512,128]{1,0:T(8,128)(2,1)S(1)}, bf16[512,128]{1,0:T(8,128)(2,1)}, u32[]{:S(2)}) copy-start(bf16[512,128]{1,0:T(8,128)(2,1)} %param.8) | copy-start | bytes 393220
  35.4 22.1 %copy-start.1 = (bf16[512,4,128]{2,0,1:T(8,128)(2,1)}, bf16[512,4,128]{2,0,1:T(8,128)(2,1)S(1)}, u32[]{:S(2)}) copy-start(bf16[512,4,128]{2,0,1:T(8,128)(2,1)S(1)} %copy.19) | copy-start | bytes 1572868
  55.5 59.7 %collective-permute-start.6 = (bf16[3,256,1024]{2,1,0:T(8,128)(2,1)}, bf16[3,256,1024]{2,1,0:T(8,128)(2,1)}, u32[]{:S(2)}, u32[]{:S(2)}) collective-permute-start(bf16[3,256,1024]{2,1,0:T(8,128)(2,1)} %pad_maximum_fusion), channel_id=1, source_target_pairs={{0,1},{1,0},{2,3},{3,2},{4,5},{5,4},{6,7},{7,6},{8,9},{9,8},{10,11... | collective-permute-start | bytes 4718600 | tf_op jit(solution)/shard_map/ppermute | solution.py:24
  112.5 4.2 %copy-start.2 = (bf16[512,512]{1,0:T(8,128)(2,1)S(1)}, bf16[512,512]{1,0:T(8,128)(2,1)}, u32[]{:S(2)}) copy-start(bf16[512,512]{1,0:T(8,128)(2,1)} %shard_map.64) | copy-start | bytes 1572868
  112.5 14.6 %collective-permute-start.2 = (bf16[512,512]{1,0:T(8,128)(2,1)}, bf16[512,512]{1,0:T(8,128)(2,1)S(1)}, u32[]{:S(2)}, u32[]{:S(2)}) collective-permute-start(bf16[512,512]{1,0:T(8,128)(2,1)} %shard_map.64), channel_id=1, source_target_pairs={{0,64},{64,128},{128,192},{192,0},{1,65},{65,129},{129,193},{193,1... | collective-permute-start | bytes 1572872 | tf_op jit(solution)/shard_map/ppermute | solution.py:24
  113.7 13.6 %collective-permute-start.7 = (bf16[512,512]{1,0:T(8,128)(2,1)}, bf16[512,512]{1,0:T(8,128)(2,1)S(1)}, u32[]{:S(2)}, u32[]{:S(2)}) collective-permute-start(bf16[512,512]{1,0:T(8,128)(2,1)} %shard_map.64), channel_id=1, source_target_pairs={{0,192},{64,0},{128,64},{192,128},{1,193},{65,1},{129,65},{193,129... | collective-permute-start | bytes 1572872 | tf_op jit(solution)/shard_map/ppermute | solution.py:24
  127.2 8.0 %collective-permute-start.8 = (bf16[512,256]{1,0:T(8,128)(2,1)S(1)}, bf16[512,256]{1,0:T(8,128)(2,1)S(1)}, u32[]{:S(2)}, u32[]{:S(2)}) collective-permute-start(bf16[512,256]{1,0:T(8,128)(2,1)S(1)} %slice.46), channel_id=1, source_target_pairs={{0,64},{64,128},{128,192},{192,0},{1,65},{65,129},{129,193},{193,1... | collective-permute-start | bytes 786440 | tf_op jit(solution)/shard_map/ppermute | solution.py:24
  127.3 7.9 %collective-permute-start.9 = (bf16[512,256]{1,0:T(8,128)(2,1)S(1)}, bf16[512,256]{1,0:T(8,128)(2,1)S(1)}, u32[]{:S(2)}, u32[]{:S(2)}) collective-permute-start(bf16[512,256]{1,0:T(8,128)(2,1)S(1)} %slice.47), channel_id=1, source_target_pairs={{0,192},{64,0},{128,64},{192,128},{1,193},{65,1},{129,65},{193,129... | collective-permute-start | bytes 786440 | tf_op jit(solution)/shard_map/ppermute | solution.py:24
Sparse Core Ops, SparseCore 0:
  13.4 83.2 all-gather.1

commit v4 on v3

--- a/solution.py
+++ b/solution.py
@@ -7,6 +7,7 @@
 import numpy as np
 from jax import lax
 from jax.experimental import pallas as pl
+from jax.experimental.pallas import tpu as pltpu
 from jax.sharding import Mesh
 from jax.sharding import PartitionSpec as P
 
@@ -28,47 +29,62 @@
     return jnp.repeat(jnp.repeat(table, rows, axis=-2), cols, axis=-1)
 
 
-def vert_kernel(q_ref, k_ref, v_ref, cols_ref, rows_ref, top_ref, tot_ref, acc_ref, o_ref, *, scale):
-    q = q_ref[0]
-    k = k_ref[0]
-    s = lax.dot_general(q, k, (((1,), (1,)), ((), ())), preferred_element_type=jnp.float32) * scale
-    n_rows, n_cols = s.shape
-    tpos = lax.broadcasted_iota(jnp.int32, (n_rows, n_cols), 0) & (BLOCK_TOKENS - 1)
-    upos = lax.broadcasted_iota(jnp.int32, (n_rows, n_cols), 1) & (BLOCK_TOKENS - 1)
-    vc = cols_ref[0]
-    rb = rows_ref[...]
-    allow = (vc < rb) | ((vc == rb) & (upos <= tpos))
-    top_v = jnp.max(jnp.where(allow, s, -jnp.inf), axis=1, keepdims=True)
+def vertical_kernel(slots_ref, q_ref, kv_hbm, key_tok_ref, query_tok_ref, top_ref, tot_ref, acc_ref,
+                    o_ref, k_buf, v_buf, sems, *, scale):
+    head = pl.program_id(0)
+    vert_count = k_buf.shape[0] // BLOCK_TOKENS
+    copies = []
+    for n in range(vert_count):
+        slot = slots_ref[head, n]
+        rows = pl.ds(n * BLOCK_TOKENS, BLOCK_TOKENS)
+        for part, buf in ((0, k_buf), (1, v_buf)):
+            copy = pltpu.make_async_copy(kv_hbm.at[part, slot], buf.at[rows], sems.at[part, n])
+            copy.start()
+            copies.append(copy)
+    for copy in copies:
+        copy.wait()
+    s = lax.dot_general(
+        q_ref[0], k_buf[...], (((1,), (1,)), ((), ())), preferred_element_type=jnp.float32
+    ) * scale
+    s = jnp.where(key_tok_ref[0] <= query_tok_ref[...], s, -jnp.inf)
     top_d = top_ref[0]
-    top = jnp.maximum(top_d, top_v)
-    p = jnp.where(allow, jnp.exp(s - top), 0.0)
+    top = jnp.maximum(top_d, jnp.max(s, axis=1, keepdims=True))
+    p = jnp.exp(s - top)
     sc = jnp.exp(top_d - top)
     total = tot_ref[0] * sc + jnp.sum(p, axis=1, keepdims=True)
-    acc = jnp.dot(p.astype(jnp.bfloat16), v_ref[0], preferred_element_type=jnp.float32)
+    acc = jnp.dot(p.astype(jnp.bfloat16), v_buf[...], preferred_element_type=jnp.float32)
     o_ref[...] = ((acc_ref[0] * sc + acc) / total).astype(o_ref.dtype)
 
 
-def vertical_attention(q, k, v, cols, rows, top_d, tot_d, acc_d, interpret=False):
-    h, t, d = q.shape
-    u = k.shape[1]
-    kern = functools.partial(vert_kernel, scale=1.0 / math.sqrt(d))
+def vertical_attention(slots, q, kv, key_tok, query_tok, top_d, tot_d, acc_d, interpret=False):
+    heads, rows, dim = q.shape
+    keys_n = key_tok.shape[-1]
+    kernel = functools.partial(vertical_kernel, scale=1.0 / math.sqrt(dim))
+    grid_spec = pltpu.PrefetchScalarGridSpec(
+        num_scalar_prefetch=1,
+        grid=(heads,),
+        in_specs=[
+            pl.BlockSpec((1, rows, dim), lambda i, t: (i, 0, 0)),
+            pl.BlockSpec(memory_space=pl.ANY),
+            pl.BlockSpec((1, 1, keys_n), lambda i, t: (i, 0, 0)),
+            pl.BlockSpec((rows, 1), lambda i, t: (0, 0)),
+            pl.BlockSpec((1, rows, 1), lambda i, t: (i, 0, 0)),
+            pl.BlockSpec((1, rows, 1), lambda i, t: (i, 0, 0)),
+            pl.BlockSpec((1, rows, dim), lambda i, t: (i, 0, 0)),
+        ],
+        out_specs=pl.BlockSpec((rows, dim), lambda i, t: (0, i)),
+        scratch_shapes=[
+            pltpu.VMEM((keys_n, dim), kv.dtype),
+            pltpu.VMEM((keys_n, dim), kv.dtype),
+            pltpu.SemaphoreType.DMA((2, keys_n // BLOCK_TOKENS)),
+        ],
+    )
     return pl.pallas_call(
-        kern,
-        grid=(h,),
-        in_specs=[
-            pl.BlockSpec((1, t, d), lambda i: (i, 0, 0)),
-            pl.BlockSpec((1, u, d), lambda i: (i, 0, 0)),
-            pl.BlockSpec((1, u, d), lambda i: (i, 0, 0)),
-            pl.BlockSpec((1, 1, u), lambda i: (i, 0, 0)),
-            pl.BlockSpec((t, 1), lambda i: (0, 0)),
-            pl.BlockSpec((1, t, 1), lambda i: (i, 0, 0)),
-            pl.BlockSpec((1, t, 1), lambda i: (i, 0, 0)),
-            pl.BlockSpec((1, t, d), lambda i: (i, 0, 0)),
-        ],
-        out_specs=pl.BlockSpec((t, d), lambda i: (0, i)),
-        out_shape=jax.ShapeDtypeStruct((t, h * d), jnp.bfloat16),
+        kernel,
+        grid_spec=grid_spec,
+        out_shape=jax.ShapeDtypeStruct((rows, heads * dim), jnp.bfloat16),
         interpret=interpret,
-    )(q, k, v, cols, rows, top_d, tot_d, acc_d)
+    )(slots, q, kv, key_tok, query_tok, top_d, tot_d, acc_d)
 
 
 def make_local(sizes):
@@ -161,13 +177,19 @@
         )
 
         arrived = arrived.reshape(2, cycle_size * capacity, BLOCK_TOKENS, head_dim)
-        chosen = arrived[:, owner_dev * capacity + slot_index]
         vert_count = vert_group.shape[1]
-        chosen = chosen.reshape(2, local_heads, vert_count * BLOCK_TOKENS, head_dim)
-        vert_cols = jnp.repeat(vert_group, BLOCK_TOKENS, axis=1)[:, None, :]
-        row_block = jnp.repeat(query_block, BLOCK_TOKENS)[:, None]
+        slots = (owner_dev * capacity + slot_index).reshape(local_heads, vert_count)
+        key_tok = (vert_group[:, :, None] * BLOCK_TOKENS + token_pos).reshape(local_heads, 1, -1)
+        query_tok = (first_block * BLOCK_TOKENS + jnp.arange(token_count, dtype=jnp.int32))[:, None]
         attention = vertical_attention(
-            query_heads, chosen[0], chosen[1], vert_cols, row_block, top_diag, total_diag, acc_diag
+            slots.astype(jnp.int32),
+            query_heads,
+            arrived,
+            key_tok.astype(jnp.int32),
+            query_tok,
+            top_diag,
+            total_diag,
+            acc_diag,
         )
 
         def rows_of(distance):

time: 145 us -> 146 us (level)
  local copies, waits for them, and re-layouts: 17.8 us -> 11.9 us
  waiting for transfers between devices: 47.1 us -> 51.8 us
  Pallas kernels: 11.2 us -> 15.2 us
  matrix products: 16.9 us -> 14.4 us
    ppermute x8, waiting for transfers between devices: 25.4 us -> 33.6 us  [ring(): lax.ppermute(block, axis, [(i, (i + distance) % size) for i in range(size)])]
    pallas_call x1, Pallas kernels: 11.2 us -> 15.2 us  [vertical_attention(): pl.pallas_call(kernel, grid_spec=grid_spec, out_shape=jax.ShapeDtypeStruc...]
    all_gather x1, waiting for transfers between devices: 21.7 us -> 18.1 us  [local(): arrived = lax.all_gather(outgoing, SEQ, axis=1, tiled=True)]
    gather x1 -> x0, local copies, waits for them, and re-layouts: 3.14 us -> none  [local(): chosen = arrived[:, owner_dev * capacity + slot_index]]
    another operation x2 -> x0, local copies, waits for them, and re-layouts: 1.66 us -> none  [the longest x1 0.9 us: local(): row_block = jnp.repeat(query_block, BLOCK_TOKENS)[:, None]]
    slice x1 -> x0, local copies, waits for them, and re-layouts: 1.51 us -> none  [local(): chosen[1]]
  transfers between devices with their start and end apart: 11 -> 11, of which waited for: 5 -> 5; matrix products, arithmetic and copies ran while one was open for 31% -> 24% of each run, Pallas kernels for 8% -> 11%
where the time goes in v4:
time: 146 us; the launch traced here: 144 us
  waiting for transfers between devices  51.8 us (35%)
  starting transfers between devices  19.3 us (13%)
  between operations  17.5 us (12%)
  Pallas kernels  15.2 us (10%)
  other arithmetic  14.4 us (10%)
  matrix products  14.4 us (10%)
  local copies, waits for them, and re-layouts  11.9 us (8%)
    ppermute x8, waiting for transfers between devices, ring(): lax.ppermute(block, axis, [(i, (i + distance) % size) for i in range(size)])  33.6 us
    all_gather x1, waiting for transfers between devices, local(): arrived = lax.all_gather(outgoing, SEQ, axis=1, tiled=True)  18.1 us
    pallas_call x1, Pallas kernels, vertical_attention(): pl.pallas_call(kernel, grid_spec=grid_spec, out_shape=jax.ShapeDtypeStruc...  15.2 us
    ppermute x8, starting transfers between devices, ring(): lax.ppermute(block, axis, [(i, (i + distance) % size) for i in range(size)])  11.3 us
    ppermute x2, starting transfers between devices, shift(): return lax.ppermute(block, axis, route)  8.05 us
    dot_general x1, matrix products, local(): jnp.einsum('htu,ud->htd', expo_diag.astype(jnp.bfloat16), context_v, pref...  5.64 us
    convert_element_type x1, other arithmetic, local(): expo_diag.astype(jnp.bfloat16)  5.59 us
    dot_general x1, matrix products, local(): jnp.einsum('htd,ud->htu', query_heads, context_k, preferred_element_type=...  3.4 us
  transfers between devices with their start and end apart: 11, of which 5 were waited for; matrix products, arithmetic and copies ran while one was open for 24% of the time, Pallas kernels for 11%

profile of v4, /device:TPU:1, one launch (start us, length us, event | category | flops | bytes accessed | tf_op | source)
XLA Modules:
  0.0 144.5 jit_solution(17822342363950987042)
XLA Ops:
  6.5 0.7 broadcast_multiply_fusion
  7.2 0.1 reshape.249
  7.3 0.2 convert_reduce_fusion
  7.5 0.1 reduce_sum.21
  7.6 1.3 select_reduce_fusion.1
  12.7 0.8 fusion.32
  13.5 0.6 pad_maximum_fusion.2
  14.2 0.0 all-gather.2.cloned.1.call-update
  14.2 1.0 pad_maximum_fusion.1
  15.2 4.7 %collective-permute-start = (bf16[2,8,64,128]{3,2,1,0:T(8,128)(2,1)S(1)}, bf16[2,8,64,128]{3,2,1,0:T(8,128)(2,1)}, u32[]{:S(2)}, u32[]{:S(2)}) collective-permute-start(bf16[2,8,64,128]{3,2,1,0:T(8,128)(2,1)S(1)} %pad_maximum_fusion.1), channel_id=1, source_target_pairs={{0,2},{1,3},{2,4},{3,5},{4,6},{5,7},{6,8},{7,9},{8,10},{9,11},{10,... | collective-permute-start | bytes 786440 | tf_op jit(solution)/shard_map/ppermute | solution.py:21
  19.9 3.3 %collective-permute-start.1 = (bf16[2,8,64,128]{3,2,1,0:T(8,128)(2,1)S(1)}, bf16[2,8,64,128]{3,2,1,0:T(8,128)(2,1)}, u32[]{:S(2)}, u32[]{:S(2)}) collective-permute-start(bf16[2,8,64,128]{3,2,1,0:T(8,128)(2,1)S(1)} %pad_maximum_fusion.1), channel_id=1, source_target_pairs={{0,1},{1,2},{2,3},{3,4},{4,5},{5,6},{6,7},{7,8},{8,9},{9,10},{10,1... | collective-permute-start | bytes 786440 | tf_op jit(solution)/shard_map/ppermute | solution.py:21
  23.3 1.5 %fusion.43 = (bf16[256,1024]{1,0:T(8,128)(2,1)S(1)}, bf16[256,1024]{1,0:T(8,128)(2,1)S(1)}, bf16[256,1024]{1,0:T(8,128)(2,1)S(1)}) fusion(bf16[512,4096]{1,0:T(8,128)(2,1)} %param.11, s32[]{:T(128)S(6)} %select_n.112, s32[]{:T(128)S(6)} %select_n.114, s32[]{:T(128)S(6)} %select_n.118, s32[]{:T(128)S(6)} %select_n.116), kind=kLoop, calls=%fused_computation.92 | loop fusion | bytes 3145744 | tf_op jit(solution)/shard_map/dynamic_slice | solution.py:134
  24.8 1.3 collective-permute-start.3
  26.1 2.5 %collective-permute-start.4 = (bf16[256,1024]{1,0:T(8,128)(2,1)S(1)}, bf16[256,1024]{1,0:T(8,128)(2,1)S(1)}, u32[]{:S(2)}, u32[]{:S(2)}) collective-permute-start(bf16[256,1024]{1,0:T(8,128)(2,1)S(1)} %get-tuple-element.13), channel_id=1, source_target_pairs={{0,128},{64,192},{128,0},{192,64},{1,129},{65,193},{129,1},{193,65... | collective-permute-start | bytes 1572872 | tf_op jit(solution)/shard_map/ppermute | solution.py:25
  28.5 1.2 collective-permute-start.5
  29.7 0.1 constant_dynamic-slice_fusion
  29.8 0.1 copy.19
  29.9 0.1 compare_reduce_fusion.1
  30.0 0.1 broadcast_subtract_fusion
  30.0 0.1 compare_reduce_fusion
  30.2 0.1 subtract_compare_fusion.1
  30.2 9.6 %collective-permute-done.3 = bf16[256,1024]{1,0:T(8,128)(2,1)S(1)} collective-permute-done((bf16[256,1024]{1,0:T(8,128)(2,1)S(1)}, bf16[256,1024]{1,0:T(8,128)(2,1)S(1)}, u32[]{:S(2)}, u32[]{:S(2)}) %collective-permute-start.3) | collective-permute-done | bytes 524320 | tf_op jit(solution)/shard_map/ppermute | solution.py:25
  39.9 12.2 %collective-permute-done.4 = bf16[256,1024]{1,0:T(8,128)(2,1)S(1)} collective-permute-done((bf16[256,1024]{1,0:T(8,128)(2,1)S(1)}, bf16[256,1024]{1,0:T(8,128)(2,1)S(1)}, u32[]{:S(2)}, u32[]{:S(2)}) %collective-permute-start.4) | collective-permute-done | bytes 524320 | tf_op jit(solution)/shard_map/ppermute | solution.py:25
  52.1 1.3 pad_maximum_fusion
  53.4 0.6 collective-permute-start.6
  54.0 0.7 iota_add_fusion.query_tok_ref
  54.8 0.1 copy.20
  54.9 0.2 broadcast_in_dim.22
  55.0 0.2 reshape.253
  55.2 0.1 copy.21
  55.3 0.2 broadcast_in_dim.24
  55.5 0.2 reshape.255
  55.7 0.7 tile.2
  56.4 0.0 copy-start.3
  56.4 0.0 copy-start.4
  56.4 2.1 %and.110 = pred[512,1536]{0,1:T(8,128)(4,1)S(1)} reshape(pred[8,64,24,64]{1,0,3,2:T(8,128)(4,1)S(1)} %tile.2) | data formatting | bytes 1572864 | tf_op jit(solution)/shard_map/and | solution.py:166
  58.5 1.3 copy.17
  59.8 0.3 copy.18
  60.1 0.1 add.159
  60.2 0.1 add.160
  60.3 0.1 add.162
  60.3 0.6 broadcast_add_fusion.key_tok_ref
  60.9 0.0 collective-permute-done.1
  61.0 1.1 maximum_maximum_fusion
  62.1 0.1 fusion.44
  62.1 3.4 %fusion = (f32[4,512]{1,0:T(4,128)S(1)}, f32[1536,4,512]{2,0,1:T(8,128)S(1)}) fusion(pred[512,1536]{0,1:T(8,128)(4,1)S(1)} %and.110, pred[4,512,24]{1,2,0:T(8,128)(4,1)S(1)} %reshape.255, pred[4,512,24]{1,2,0:T(8,128)(4,1)S(1)} %reshape.253, bf16[1536,128,1]{1,0,2:T(8,128)(2,1)S(1)} %bitcast.85, bf16[512,4,128]{2,0,1:T(8,128)(2,1)S(1)} %copy.18), kind=kOutput, calls=%fused_computation.2 | convolution fusion | flops 821032960 | bytes 14393344 | tf_op jit(solution)/shard_map/htd,ud->htu/dot_general | solution.py:158
  65.6 5.6 %fusion.4 = (bf16[4,512,1536]{1,2,0:T(8,128)(2,1)}, f32[4,512]{1,0:T(4,128)S(1)}) fusion(f32[1536,4,512]{2,0,1:T(8,128)S(1)} %get-tuple-element.27, f32[4,512]{1,0:T(4,128)S(1)} %get-tuple-element.26, pred[512,1536]{0,1:T(8,128)(4,1)S(1)} %and.110, pred[4,512,24]{1,2,0:T(8,128)(4,1)S(1)} %reshape.255, pred[4,512,24]{1,2,0:T(8,128)(4,1)S(1)} %reshape.253), kind=kLoop, calls=%fused_computation.7 | loop fusion | flops 22018048 | bytes 19775488 | tf_op jit(solution)/shard_map/convert_element_type | solution.py:174
  71.1 1.4 copy.24.tot_ref
  72.5 1.3 copy.23.top_ref
  73.8 5.6 %fusion.45.acc_ref = f32[4,512,128]{2,1,0:T(8,128)} fusion(bf16[4,512,1536]{1,2,0:T(8,128)(2,1)} %get-tuple-element.9, bf16[1536,128,1]{1,0,2:T(8,128)(2,1)S(1)} %bitcast.84), kind=kOutput, calls=%fused_computation.94 | convolution fusion | flops 805306368 | bytes 7733248 | tf_op jit(solution)/shard_map/htu,ud->htd/dot_general | solution.py:172
  79.5 18.1 %all-gather.2.cloned.1.call-done = bf16[2,8192,128]{2,1,0:T(8,128)(2,1)} async-done(((bf16[2,128,128]{2,1,0:T(8,128)(2,1)}), bf16[2,8192,128]{2,1,0:T(8,128)(2,1)}) %all-gather.2.cloned.1.call-update) | async-done | bytes 4194320 | tf_op jit(solution)/shard_map/all_gather | solution.py:126
  97.6 15.2 %shard_map.64 = bf16[512,512]{1,0:T(8,128)(2,1)} custom-call(s32[4,16]{1,0:T(4,128)} %get-tuple-element.23.slots_ref, bf16[4,512,128]{2,1,0:T(8,128)(2,1)} %bitcast.80, bf16[2,128,64,128]{3,2,1,0:T(8,128)(2,1)} %bitcast.81, s32[4,1,1024]{2,1,0:T(1,128)} %broadcast_add_fusion.key_tok_ref, s32[512,1]{1,0:T(8,128)} %iota_add_fusion.query_tok_ref, ...), custom_call_target="tpu_custom_call" | custom-call | tf_op jit(solution)/shard_map/pallas_call | solution.py:82
  112.8 1.3 collective-permute-start.2
  114.1 1.5 %collective-permute-start.7 = (bf16[512,512]{1,0:T(8,128)(2,1)}, bf16[512,512]{1,0:T(8,128)(2,1)S(1)}, u32[]{:S(2)}, u32[]{:S(2)}) collective-permute-start(bf16[512,512]{1,0:T(8,128)(2,1)} %shard_map.64), channel_id=1, source_target_pairs={{0,192},{64,0},{128,64},{192,128},{1,193},{65,1},{129,65},{193,129... | collective-permute-start | bytes 1572872 | tf_op jit(solution)/shard_map/ppermute | solution.py:25
  115.6 1.5 %slice_bitcast_fusion = (bf16[256,1024]{1,0:T(8,128)(2,1)S(1)}, bf16[256,1024]{1,0:T(8,128)(2,1)S(1)}, bf16[256,1024]{1,0:T(8,128)(2,1)S(1)}) fusion(bf16[3,256,1024]{2,1,0:T(8,128)(2,1)} %collective-permute-done.6), kind=kLoop, calls=%fused_computation.38 | loop fusion | bytes 3145728 | tf_op jit(solution)/shard_map/squeeze | solution.py:196
  117.1 2.0 %fusion.24 = f32[512,1024]{1,0:T(8,128)S(1)} fusion(bf16[512,512]{1,0:T(8,128)(2,1)S(1)} %copy-done.2, bf16[512,4096]{1,0:T(8,128)(2,1)} %param.11, s32[]{:T(128)S(6)} %select_n.110), kind=kOutput, calls=%fused_computation.32 | convolution fusion | flops 536870912 | bytes 3670020 | tf_op jit(solution)/shard_map/dot_general | solution.py:206
  119.1 8.4 %collective-permute-done.2 = bf16[512,512]{1,0:T(8,128)(2,1)S(1)} collective-permute-done((bf16[512,512]{1,0:T(8,128)(2,1)}, bf16[512,512]{1,0:T(8,128)(2,1)S(1)}, u32[]{:S(2)}, u32[]{:S(2)}) %collective-permute-start.2) | collective-permute-done | bytes 524320 | tf_op jit(solution)/shard_map/ppermute | solution.py:25
  127.6 0.3 collective-permute-start.8
  127.9 2.7 %collective-permute-start.9 = (bf16[512,256]{1,0:T(8,128)(2,1)S(1)}, bf16[512,256]{1,0:T(8,128)(2,1)S(1)}, u32[]{:S(2)}, u32[]{:S(2)}) collective-permute-start(bf16[512,256]{1,0:T(8,128)(2,1)S(1)} %slice.33), channel_id=1, source_target_pairs={{0,192},{64,0},{128,64},{192,128},{1,193},{65,1},{129,65},{193,129... | collective-permute-start | bytes 786440 | tf_op jit(solution)/shard_map/ppermute | solution.py:25
  130.6 0.7 fusion.6
  131.4 0.3 copy-done.8
  131.7 0.7 fusion.12
  132.4 3.4 %collective-permute-done.8 = bf16[512,256]{1,0:T(8,128)(2,1)S(1)} collective-permute-done((bf16[512,256]{1,0:T(8,128)(2,1)S(1)}, bf16[512,256]{1,0:T(8,128)(2,1)S(1)}, u32[]{:S(2)}, u32[]{:S(2)}) %collective-permute-start.8) | collective-permute-done | bytes 262176 | tf_op jit(solution)/shard_map/ppermute | solution.py:25
  135.8 1.8 %add_convert_fusion = bf16[512,1024]{1,0:T(8,128)(2,1)} fusion(f32[512,1024]{1,0:T(8,128)S(1)} %fusion.12, f32[512,1024]{1,0:T(8,128)S(1)} %fusion.24, f32[512,1024]{1,0:T(8,128)S(1)} %fusion.6, bf16[256,1024]{1,0:T(8,128)(2,1)S(1)} %get-tuple-element.14, bf16[256,1024]{1,0:T(8,128)(2,1)S(1)} %collective-permute-done.4, pred[]{:T(512)S(6)} %eq.77, ...), kind=kOutput, calls=%fused_computation.9 | convolution fusion | flops 544735232 | bytes 8912897 | tf_op jit(solution)/shard_map/dot_general | solution.py:212
  (31 shorter events, 0.1 us)
Async XLA Ops:
  6.5 23.2 %copy-start = (s32[16,8]{0,1:T(8,128)S(1)}, s32[16,8]{0,1:T(8,128)}, u32[]{:S(2)}) copy-start(s32[16,8]{0,1:T(8,128)} %param.10) | copy-start | bytes 1540
  6.5 91.1 %all-gather.2.cloned.1.call-start = ((), (), s32[]{:S(2)}) async-start(), calls=%async_computation | async-start | bytes 4259840 | tf_op jit(solution)/shard_map/all_gather | solution.py:126
  15.2 45.8 %collective-permute-start = (bf16[2,8,64,128]{3,2,1,0:T(8,128)(2,1)S(1)}, bf16[2,8,64,128]{3,2,1,0:T(8,128)(2,1)}, u32[]{:S(2)}, u32[]{:S(2)}) collective-permute-start(bf16[2,8,64,128]{3,2,1,0:T(8,128)(2,1)S(1)} %pad_maximum_fusion.1), channel_id=1, source_target_pairs={{0,2},{1,3},{2,4},{3,5},{4,6},{5,7},{6,8},{7,9},{8,10},{9,11},{10,... | collective-permute-start | bytes 786440 | tf_op jit(solution)/shard_map/ppermute | solution.py:21
  19.9 41.0 %collective-permute-start.1 = (bf16[2,8,64,128]{3,2,1,0:T(8,128)(2,1)S(1)}, bf16[2,8,64,128]{3,2,1,0:T(8,128)(2,1)}, u32[]{:S(2)}, u32[]{:S(2)}) collective-permute-start(bf16[2,8,64,128]{3,2,1,0:T(8,128)(2,1)S(1)} %pad_maximum_fusion.1), channel_id=1, source_target_pairs={{0,1},{1,2},{2,3},{3,4},{4,5},{5,6},{6,7},{7,8},{8,9},{9,10},{10,1... | collective-permute-start | bytes 786440 | tf_op jit(solution)/shard_map/ppermute | solution.py:21
  24.8 15.1 %collective-permute-start.3 = (bf16[256,1024]{1,0:T(8,128)(2,1)S(1)}, bf16[256,1024]{1,0:T(8,128)(2,1)S(1)}, u32[]{:S(2)}, u32[]{:S(2)}) collective-permute-start(bf16[256,1024]{1,0:T(8,128)(2,1)S(1)} %get-tuple-element.11), channel_id=1, source_target_pairs={{0,64},{64,128},{128,192},{192,0},{1,65},{65,129},{129,193},{193,1... | collective-permute-start | bytes 1572872 | tf_op jit(solution)/shard_map/ppermute | solution.py:25
  26.1 26.0 %collective-permute-start.4 = (bf16[256,1024]{1,0:T(8,128)(2,1)S(1)}, bf16[256,1024]{1,0:T(8,128)(2,1)S(1)}, u32[]{:S(2)}, u32[]{:S(2)}) collective-permute-start(bf16[256,1024]{1,0:T(8,128)(2,1)S(1)} %get-tuple-element.13), channel_id=1, source_target_pairs={{0,128},{64,192},{128,0},{192,64},{1,129},{65,193},{129,1},{193,65... | collective-permute-start | bytes 1572872 | tf_op jit(solution)/shard_map/ppermute | solution.py:25
  28.5 23.5 %collective-permute-start.5 = (bf16[256,1024]{1,0:T(8,128)(2,1)S(1)}, bf16[256,1024]{1,0:T(8,128)(2,1)S(1)}, u32[]{:S(2)}, u32[]{:S(2)}) collective-permute-start(bf16[256,1024]{1,0:T(8,128)(2,1)S(1)} %get-tuple-element.12), channel_id=1, source_target_pairs={{0,192},{64,0},{128,64},{192,128},{1,193},{65,1},{129,65},{193,129... | collective-permute-start | bytes 1572872 | tf_op jit(solution)/shard_map/ppermute | solution.py:25
  39.9 15.8 %copy-start.5 = (bf16[256,1024]{1,0:T(8,128)(2,1)}, bf16[256,1024]{1,0:T(8,128)(2,1)S(1)}, u32[]{:S(2)}) copy-start(bf16[256,1024]{1,0:T(8,128)(2,1)S(1)} %collective-permute-done.3) | copy-start | bytes 1572868
  52.1 3.4 %copy-start.7 = (bf16[256,1024]{1,0:T(8,128)(2,1)}, bf16[256,1024]{1,0:T(8,128)(2,1)S(1)}, u32[]{:S(2)}) copy-start(bf16[256,1024]{1,0:T(8,128)(2,1)S(1)} %collective-permute-done.5) | copy-start | bytes 1572868
  53.4 62.2 %collective-permute-start.6 = (bf16[3,256,1024]{2,1,0:T(8,128)(2,1)}, bf16[3,256,1024]{2,1,0:T(8,128)(2,1)}, u32[]{:S(2)}, u32[]{:S(2)}) collective-permute-start(bf16[3,256,1024]{2,1,0:T(8,128)(2,1)} %pad_maximum_fusion), channel_id=1, source_target_pairs={{0,1},{1,0},{2,3},{3,2},{4,5},{5,4},{6,7},{7,6},{8,9},{9,8},{10,11... | collective-permute-start | bytes 4718600 | tf_op jit(solution)/shard_map/ppermute | solution.py:25
  56.4 4.6 %copy-start.3 = (bf16[512,128]{1,0:T(8,128)(2,1)S(1)}, bf16[512,128]{1,0:T(8,128)(2,1)}, u32[]{:S(2)}) copy-start(bf16[512,128]{1,0:T(8,128)(2,1)} %param.7) | copy-start | bytes 393220
  56.4 4.6 %copy-start.4 = (bf16[512,128]{1,0:T(8,128)(2,1)S(1)}, bf16[512,128]{1,0:T(8,128)(2,1)}, u32[]{:S(2)}) copy-start(bf16[512,128]{1,0:T(8,128)(2,1)} %param.8) | copy-start | bytes 393220
  60.1 5.5 %copy-start.1 = (bf16[512,4,128]{2,0,1:T(8,128)(2,1)}, bf16[512,4,128]{2,0,1:T(8,128)(2,1)S(1)}, u32[]{:S(2)}) copy-start(bf16[512,4,128]{2,0,1:T(8,128)(2,1)S(1)} %copy.18) | copy-start | bytes 1572868
  112.8 4.2 %copy-start.2 = (bf16[512,512]{1,0:T(8,128)(2,1)S(1)}, bf16[512,512]{1,0:T(8,128)(2,1)}, u32[]{:S(2)}) copy-start(bf16[512,512]{1,0:T(8,128)(2,1)} %shard_map.64) | copy-start | bytes 1572868
  112.8 14.7 %collective-permute-start.2 = (bf16[512,512]{1,0:T(8,128)(2,1)}, bf16[512,512]{1,0:T(8,128)(2,1)S(1)}, u32[]{:S(2)}, u32[]{:S(2)}) collective-permute-start(bf16[512,512]{1,0:T(8,128)(2,1)} %shard_map.64), channel_id=1, source_target_pairs={{0,64},{64,128},{128,192},{192,0},{1,65},{65,129},{129,193},{193,1... | collective-permute-start | bytes 1572872 | tf_op jit(solution)/shard_map/ppermute | solution.py:25
  114.1 13.8 %collective-permute-start.7 = (bf16[512,512]{1,0:T(8,128)(2,1)}, bf16[512,512]{1,0:T(8,128)(2,1)S(1)}, u32[]{:S(2)}, u32[]{:S(2)}) collective-permute-start(bf16[512,512]{1,0:T(8,128)(2,1)} %shard_map.64), channel_id=1, source_target_pairs={{0,192},{64,0},{128,64},{192,128},{1,193},{65,1},{129,65},{193,129... | collective-permute-start | bytes 1572872 | tf_op jit(solution)/shard_map/ppermute | solution.py:25
  117.1 13.5 %copy-start.6 = (bf16[256,1024]{1,0:T(8,128)(2,1)S(1)}, bf16[256,1024]{1,0:T(8,128)(2,1)}, u32[]{:S(2)}) copy-start(bf16[256,1024]{1,0:T(8,128)(2,1)} %copy-done.5) | copy-start | bytes 1572868
  127.6 8.2 %collective-permute-start.8 = (bf16[512,256]{1,0:T(8,128)(2,1)S(1)}, bf16[512,256]{1,0:T(8,128)(2,1)S(1)}, u32[]{:S(2)}, u32[]{:S(2)}) collective-permute-start(bf16[512,256]{1,0:T(8,128)(2,1)S(1)} %slice.32), channel_id=1, source_target_pairs={{0,64},{64,128},{128,192},{192,0},{1,65},{65,129},{129,193},{193,1... | collective-permute-start | bytes 786440 | tf_op jit(solution)/shard_map/ppermute | solution.py:25
  127.9 7.9 %collective-permute-start.9 = (bf16[512,256]{1,0:T(8,128)(2,1)S(1)}, bf16[512,256]{1,0:T(8,128)(2,1)S(1)}, u32[]{:S(2)}, u32[]{:S(2)}) collective-permute-start(bf16[512,256]{1,0:T(8,128)(2,1)S(1)} %slice.33), channel_id=1, source_target_pairs={{0,192},{64,0},{128,64},{192,128},{1,193},{65,1},{129,65},{193,129... | collective-permute-start | bytes 786440 | tf_op jit(solution)/shard_map/ppermute | solution.py:25
  130.6 1.0 copy-start.8
Sparse Core Ops, SparseCore 0:
  14.3 83.2 all-gather.1

commit v5 on v4

--- a/solution.py
+++ b/solution.py
@@ -32,19 +32,38 @@
 def vertical_kernel(slots_ref, q_ref, kv_hbm, key_tok_ref, query_tok_ref, top_ref, tot_ref, acc_ref,
                     o_ref, k_buf, v_buf, sems, *, scale):
     head = pl.program_id(0)
-    vert_count = k_buf.shape[0] // BLOCK_TOKENS
-    copies = []
-    for n in range(vert_count):
-        slot = slots_ref[head, n]
-        rows = pl.ds(n * BLOCK_TOKENS, BLOCK_TOKENS)
-        for part, buf in ((0, k_buf), (1, v_buf)):
-            copy = pltpu.make_async_copy(kv_hbm.at[part, slot], buf.at[rows], sems.at[part, n])
+    heads = pl.num_programs(0)
+    vert_count = k_buf.shape[1] // BLOCK_TOKENS
+
+    def block_copies(h, buf_index):
+        copies = []
+        for n in range(vert_count):
+            slot = slots_ref[h, n]
+            rows = pl.ds(n * BLOCK_TOKENS, BLOCK_TOKENS)
+            for part, buf in ((0, k_buf), (1, v_buf)):
+                copies.append(
+                    pltpu.make_async_copy(
+                        kv_hbm.at[part, slot], buf.at[buf_index, rows], sems.at[buf_index, part, n]
+                    )
+                )
+        return copies
+
+    current = head % 2
+
+    @pl.when(head == 0)
+    def _():
+        for copy in block_copies(0, 0):
             copy.start()
-            copies.append(copy)
-    for copy in copies:
+
+    @pl.when(head + 1 < heads)
+    def _():
+        for copy in block_copies(head + 1, 1 - current):
+            copy.start()
+
+    for copy in block_copies(head, current):
         copy.wait()
     s = lax.dot_general(
-        q_ref[0], k_buf[...], (((1,), (1,)), ((), ())), preferred_element_type=jnp.float32
+        q_ref[0], k_buf[current], (((1,), (1,)), ((), ())), preferred_element_type=jnp.float32
     ) * scale
     s = jnp.where(key_tok_ref[0] <= query_tok_ref[...], s, -jnp.inf)
     top_d = top_ref[0]
@@ -52,7 +71,7 @@
     p = jnp.exp(s - top)
     sc = jnp.exp(top_d - top)
     total = tot_ref[0] * sc + jnp.sum(p, axis=1, keepdims=True)
-    acc = jnp.dot(p.astype(jnp.bfloat16), v_buf[...], preferred_element_type=jnp.float32)
+    acc = jnp.dot(p.astype(jnp.bfloat16), v_buf[current], preferred_element_type=jnp.float32)
     o_ref[...] = ((acc_ref[0] * sc + acc) / total).astype(o_ref.dtype)
 
 
@@ -74,9 +93,9 @@
         ],
         out_specs=pl.BlockSpec((rows, dim), lambda i, t: (0, i)),
         scratch_shapes=[
-            pltpu.VMEM((keys_n, dim), kv.dtype),
-            pltpu.VMEM((keys_n, dim), kv.dtype),
-            pltpu.SemaphoreType.DMA((2, keys_n // BLOCK_TOKENS)),
+            pltpu.VMEM((2, keys_n, dim), kv.dtype),
+            pltpu.VMEM((2, keys_n, dim), kv.dtype),
+            pltpu.SemaphoreType.DMA((2, 2, keys_n // BLOCK_TOKENS)),
         ],
     )
     return pl.pallas_call(
@@ -110,15 +129,21 @@
         paired = jnp.stack([keys, values]).reshape(2, block_count, BLOCK_TOKENS, head_dim)
         owned_here = owner_dev == cycle_index
         capacity = 2
-        low = jnp.min(jnp.where(owned_here, within_dev, block_count - 1))
-        high = jnp.max(jnp.where(owned_here, within_dev, 0))
-        outgoing = jnp.concatenate(
-            [
-                lax.dynamic_slice_in_dim(paired, low, 1, 1),
-                lax.dynamic_slice_in_dim(paired, high, 1, 1),
-            ],
+        local_ids = jnp.arange(block_count, dtype=jnp.int32)
+        owned_blocks = jnp.any(
+            owned_here[None, :] & (within_dev[None, :] == local_ids[:, None]), axis=1
+        )
+        below = jnp.sum(
+            (owned_blocks[None, :] & (local_ids[None, :] < local_ids[:, None])).astype(jnp.int32),
             axis=1,
-        ).reshape(2, capacity * BLOCK_TOKENS, head_dim)
+        )
+        owned_total = jnp.sum(owned_blocks.astype(jnp.int32))
+        pick = jnp.stack(
+            [owned_blocks & (below == 0), owned_blocks & (below == owned_total - 1)]
+        ).astype(jnp.bfloat16)
+        outgoing = jnp.einsum(
+            "cb,kbtd->kctd", pick, paired, preferred_element_type=jnp.float32
+        ).astype(jnp.bfloat16).reshape(2, capacity * BLOCK_TOKENS, head_dim)
         same_owner = (owner_dev[:, None] == owner_dev[None, :]) & (
             union_list[None, :] < union_list[:, None]
         )

time: 146 us -> 141 us (0.966)
  between operations: 17.5 us -> 14.4 us
  Pallas kernels: 15.2 us -> 12.3 us
  local copies, waits for them, and re-layouts: 11.9 us -> 14.7 us
  other arithmetic: 14.4 us -> 12.3 us
    pallas_call x1, Pallas kernels: 15.2 us -> 12.3 us  [vertical_attention(): pl.pallas_call(kernel, grid_spec=grid_spec, out_shape=jax.ShapeDtypeStruc...]
    another operation x2 -> x0, other arithmetic: 1.81 us -> none  [local(): jnp.stack([keys, values]).reshape(2, block_count, BLOCK_TOKENS, head_dim)]
  transfers between devices with their start and end apart: 11 -> 11, of which waited for: 5 -> 5; matrix products, arithmetic and copies ran while one was open for 24% -> 25% of each run, Pallas kernels for 11% -> 9%
where the time goes in v5:
time: 141 us; the launch traced here: 139 us
  waiting for transfers between devices  51.6 us (37%)
  starting transfers between devices  19.3 us (14%)
  local copies, waits for them, and re-layouts  14.7 us (10%)
  matrix products  14.6 us (10%)
  between operations  14.4 us (10%)
  other arithmetic  12.3 us (9%)
  Pallas kernels  12.3 us (9%)
    ppermute x8, waiting for transfers between devices, ring(): lax.ppermute(block, axis, [(i, (i + distance) % size) for i in range(size)])  32.8 us
    all_gather x1, waiting for transfers between devices, local(): arrived = lax.all_gather(outgoing, SEQ, axis=1, tiled=True)  18.8 us
    pallas_call x1, Pallas kernels, vertical_attention(): pl.pallas_call(kernel, grid_spec=grid_spec, out_shape=jax.ShapeDtypeStruc...  12.3 us
    ppermute x8, starting transfers between devices, ring(): lax.ppermute(block, axis, [(i, (i + distance) % size) for i in range(size)])  11.2 us
    ppermute x2, starting transfers between devices, shift(): return lax.ppermute(block, axis, route)  8.08 us
    dot_general x1, matrix products, local(): jnp.einsum('htu,ud->htd', expo_diag.astype(jnp.bfloat16), context_v, pref...  5.69 us
    convert_element_type x1, other arithmetic, local(): expo_diag.astype(jnp.bfloat16)  5.61 us
    dot_general x1, matrix products, local(): jnp.einsum('htd,ud->htu', query_heads, context_k, preferred_element_type=...  3.4 us
  transfers between devices with their start and end apart: 11, of which 5 were waited for; matrix products, arithmetic and copies ran while one was open for 25% of the time, Pallas kernels for 9%

profile of v5, /device:TPU:1, one launch (start us, length us, event | category | flops | bytes accessed | tf_op | source)
XLA Modules:
  0.0 139.2 jit_solution(1448293686694901568)
XLA Ops:
  6.5 0.7 broadcast_multiply_fusion
  7.2 0.1 reshape.315
  7.4 0.1 fusion.36
  7.5 0.6 convert_reduce_fusion.2
  8.1 0.1 convert_reduce_fusion.1
  8.2 1.0 copy_dynamic-update-slice_fusion.1
  9.2 1.0 copy_dynamic-update-slice_fusion
  10.9 0.2 fusion.6
  11.1 0.6 copy.26
  11.8 4.7 %collective-permute-start = (bf16[2,8,64,128]{3,1,2,0:T(8,128)(2,1)S(1)}, bf16[2,8,64,128]{3,1,2,0:T(8,128)(2,1)}, u32[]{:S(2)}, u32[]{:S(2)}) collective-permute-start(bf16[2,8,64,128]{3,1,2,0:T(8,128)(2,1)S(1)} %copy_dynamic-update-slice_fusion), channel_id=1, source_target_pairs={{0,2},{1,3},{2,4},{3,5},{4,6},{5,7},{6,8},{7,9},{8,10},{9,11},{10,... | collective-permute-start | bytes 786440 | tf_op jit(solution)/shard_map/ppermute | solution.py:21
  16.5 3.3 %collective-permute-start.1 = (bf16[2,8,64,128]{3,1,2,0:T(8,128)(2,1)S(1)}, bf16[2,8,64,128]{3,1,2,0:T(8,128)(2,1)}, u32[]{:S(2)}, u32[]{:S(2)}) collective-permute-start(bf16[2,8,64,128]{3,1,2,0:T(8,128)(2,1)S(1)} %copy_dynamic-update-slice_fusion), channel_id=1, source_target_pairs={{0,1},{1,2},{2,3},{3,4},{4,5},{5,6},{6,7},{7,8},{8,9},{9,10},{10,1... | collective-permute-start | bytes 786440 | tf_op jit(solution)/shard_map/ppermute | solution.py:21
  19.9 1.5 %fusion.51 = (bf16[256,1024]{1,0:T(8,128)(2,1)S(1)}, bf16[256,1024]{1,0:T(8,128)(2,1)S(1)}, bf16[256,1024]{1,0:T(8,128)(2,1)S(1)}) fusion(bf16[512,4096]{1,0:T(8,128)(2,1)} %param.11, s32[]{:T(128)S(6)} %select_n.96, s32[]{:T(128)S(6)} %select_n.98, s32[]{:T(128)S(6)} %select_n.102, s32[]{:T(128)S(6)} %select_n.100), kind=kLoop, calls=%fused_computation.100 | loop fusion | bytes 3145744 | tf_op jit(solution)/shard_map/dynamic_slice | solution.py:159
  21.4 1.3 collective-permute-start.3
  22.7 2.4 %collective-permute-start.4 = (bf16[256,1024]{1,0:T(8,128)(2,1)S(1)}, bf16[256,1024]{1,0:T(8,128)(2,1)S(1)}, u32[]{:S(2)}, u32[]{:S(2)}) collective-permute-start(bf16[256,1024]{1,0:T(8,128)(2,1)S(1)} %get-tuple-element.13), channel_id=1, source_target_pairs={{0,128},{64,192},{128,0},{192,64},{1,129},{65,193},{129,1},{193,65... | collective-permute-start | bytes 1572872 | tf_op jit(solution)/shard_map/ppermute | solution.py:25
  25.2 1.2 collective-permute-start.5
  26.3 0.1 constant_dynamic-slice_fusion
  26.4 0.1 copy.27
  26.5 0.2 convert_reduce_fusion
  26.7 0.1 reduce_sum.39
  26.7 0.1 broadcast_subtract_fusion
  26.8 0.1 compare_reduce_fusion
  26.9 0.1 compare_reduce_fusion.1
  27.0 0.1 subtract_compare_fusion.1
  27.1 0.6 fusion.40.slots_ref
  27.7 8.8 %collective-permute-done.3 = bf16[256,1024]{1,0:T(8,128)(2,1)S(1)} collective-permute-done((bf16[256,1024]{1,0:T(8,128)(2,1)S(1)}, bf16[256,1024]{1,0:T(8,128)(2,1)S(1)}, u32[]{:S(2)}, u32[]{:S(2)}) %collective-permute-start.3) | collective-permute-done | bytes 524320 | tf_op jit(solution)/shard_map/ppermute | solution.py:25
  36.5 12.2 %collective-permute-done.4 = bf16[256,1024]{1,0:T(8,128)(2,1)S(1)} collective-permute-done((bf16[256,1024]{1,0:T(8,128)(2,1)S(1)}, bf16[256,1024]{1,0:T(8,128)(2,1)S(1)}, u32[]{:S(2)}, u32[]{:S(2)}) %collective-permute-start.4) | collective-permute-done | bytes 524320 | tf_op jit(solution)/shard_map/ppermute | solution.py:25
  48.7 1.3 pad_maximum_fusion
  50.0 0.6 collective-permute-start.6
  50.6 0.7 iota_add_fusion.query_tok_ref
  51.4 0.1 copy.28
  51.5 0.2 broadcast_in_dim.18
  51.6 0.2 reshape.319
  51.8 0.1 copy.29
  51.9 0.2 broadcast_in_dim.20
  52.1 0.2 reshape.321
  52.3 0.7 tile.2
  53.0 2.1 %and.167 = pred[512,1536]{0,1:T(8,128)(4,1)S(1)} reshape(pred[8,64,24,64]{1,0,3,2:T(8,128)(4,1)S(1)} %tile.2) | data formatting | bytes 1572864 | tf_op jit(solution)/shard_map/and | solution.py:191
  55.1 1.3 copy.22
  56.4 0.3 copy.23
  56.7 0.1 add.156
  56.9 0.6 broadcast_add_fusion.key_tok_ref
  57.5 1.2 pad_maximum_fusion.1
  58.8 0.1 fusion.52
  58.8 0.1 copy.30
  58.9 0.1 copy.31
  59.0 3.4 %fusion = (f32[4,512]{1,0:T(4,128)S(1)}, f32[1536,4,512]{2,0,1:T(8,128)S(1)}) fusion(pred[512,1536]{0,1:T(8,128)(4,1)S(1)} %and.167, pred[4,512,24]{1,2,0:T(8,128)(4,1)S(1)} %reshape.321, pred[4,512,24]{1,2,0:T(8,128)(4,1)S(1)} %reshape.319, bf16[1536,128,1]{1,0,2:T(8,128)(2,1)S(1)} %bitcast.97, bf16[512,4,128]{2,0,1:T(8,128)(2,1)S(1)} %copy.23), kind=kOutput, calls=%fused_computation.2 | convolution fusion | flops 821032960 | bytes 14393344 | tf_op jit(solution)/shard_map/htd,ud->htu/dot_general | solution.py:183
  62.4 5.6 %fusion.4 = (bf16[4,512,1536]{1,2,0:T(8,128)(2,1)}, f32[4,512]{1,0:T(4,128)S(1)}) fusion(f32[1536,4,512]{2,0,1:T(8,128)S(1)} %get-tuple-element.26, f32[4,512]{1,0:T(4,128)S(1)} %get-tuple-element.25, pred[512,1536]{0,1:T(8,128)(4,1)S(1)} %and.167, pred[4,512,24]{1,2,0:T(8,128)(4,1)S(1)} %reshape.321, pred[4,512,24]{1,2,0:T(8,128)(4,1)S(1)} %reshape.319), kind=kLoop, calls=%fused_computation.7 | loop fusion | flops 22018048 | bytes 19775488 | tf_op jit(solution)/shard_map/convert_element_type | solution.py:199
  68.0 1.4 copy.34.tot_ref
  69.4 1.3 copy.33.top_ref
  70.7 5.7 %fusion.53.acc_ref = f32[4,512,128]{2,1,0:T(8,128)} fusion(bf16[4,512,1536]{1,2,0:T(8,128)(2,1)} %get-tuple-element.9, bf16[1536,128,1]{1,0,2:T(8,128)(2,1)S(1)} %bitcast.96), kind=kOutput, calls=%fused_computation.102 | convolution fusion | flops 805306368 | bytes 7733248 | tf_op jit(solution)/shard_map/htu,ud->htd/dot_general | solution.py:197
  76.4 18.8 %all-gather.2.cloned.1.call-done = bf16[2,8192,128]{2,1,0:T(8,128)(2,1)} async-done(((bf16[2,128,128]{2,1,0:T(8,128)(2,1)}), bf16[2,8192,128]{2,1,0:T(8,128)(2,1)}) %all-gather.2.cloned.1.call-update) | async-done | bytes 4194320 | tf_op jit(solution)/shard_map/all_gather | solution.py:151
  95.2 12.3 %shard_map.64 = bf16[512,512]{1,0:T(8,128)(2,1)} custom-call(s32[4,16]{1,0:T(4,128)} %fusion.40.slots_ref, bf16[4,512,128]{2,1,0:T(8,128)(2,1)} %bitcast.92, bf16[2,128,64,128]{3,2,1,0:T(8,128)(2,1)} %bitcast.93, s32[4,1,1024]{2,1,0:T(1,128)} %broadcast_add_fusion.key_tok_ref, s32[512,1]{1,0:T(8,128)} %iota_add_fusion.query_tok_ref, ...), custom_call_target="tpu_custom_call" | custom-call | tf_op jit(solution)/shard_map/pallas_call | solution.py:101
  107.5 1.3 collective-permute-start.2
  108.8 1.5 %collective-permute-start.7 = (bf16[512,512]{1,0:T(8,128)(2,1)}, bf16[512,512]{1,0:T(8,128)(2,1)S(1)}, u32[]{:S(2)}, u32[]{:S(2)}) collective-permute-start(bf16[512,512]{1,0:T(8,128)(2,1)} %shard_map.64), channel_id=1, source_target_pairs={{0,192},{64,0},{128,64},{192,128},{1,193},{65,1},{129,65},{193,129... | collective-permute-start | bytes 1572872 | tf_op jit(solution)/shard_map/ppermute | solution.py:25
  110.3 1.5 %slice_bitcast_fusion = (bf16[256,1024]{1,0:T(8,128)(2,1)S(1)}, bf16[256,1024]{1,0:T(8,128)(2,1)S(1)}, bf16[256,1024]{1,0:T(8,128)(2,1)S(1)}) fusion(bf16[3,256,1024]{2,1,0:T(8,128)(2,1)} %collective-permute-done.6), kind=kLoop, calls=%fused_computation.40 | loop fusion | bytes 3145728 | tf_op jit(solution)/shard_map/squeeze | solution.py:221
  111.8 2.0 %fusion.25 = f32[512,1024]{1,0:T(8,128)S(1)} fusion(bf16[512,512]{1,0:T(8,128)(2,1)S(1)} %copy-done.2, bf16[512,4096]{1,0:T(8,128)(2,1)} %param.11, s32[]{:T(128)S(6)} %select_n.94), kind=kOutput, calls=%fused_computation.34 | convolution fusion | flops 536870912 | bytes 3670020 | tf_op jit(solution)/shard_map/dot_general | solution.py:231
  113.8 8.4 %collective-permute-done.2 = bf16[512,512]{1,0:T(8,128)(2,1)S(1)} collective-permute-done((bf16[512,512]{1,0:T(8,128)(2,1)}, bf16[512,512]{1,0:T(8,128)(2,1)S(1)}, u32[]{:S(2)}, u32[]{:S(2)}) %collective-permute-start.2) | collective-permute-done | bytes 524320 | tf_op jit(solution)/shard_map/ppermute | solution.py:25
  122.2 0.3 collective-permute-start.8
  122.6 2.7 %collective-permute-start.9 = (bf16[512,256]{1,0:T(8,128)(2,1)S(1)}, bf16[512,256]{1,0:T(8,128)(2,1)S(1)}, u32[]{:S(2)}, u32[]{:S(2)}) collective-permute-start(bf16[512,256]{1,0:T(8,128)(2,1)S(1)} %slice.33), channel_id=1, source_target_pairs={{0,192},{64,0},{128,64},{192,128},{1,193},{65,1},{129,65},{193,129... | collective-permute-start | bytes 786440 | tf_op jit(solution)/shard_map/ppermute | solution.py:25
  125.3 0.7 fusion.7
  126.1 0.3 copy-done.6
  126.4 0.7 fusion.13
  127.1 3.4 %collective-permute-done.8 = bf16[512,256]{1,0:T(8,128)(2,1)S(1)} collective-permute-done((bf16[512,256]{1,0:T(8,128)(2,1)S(1)}, bf16[512,256]{1,0:T(8,128)(2,1)S(1)}, u32[]{:S(2)}, u32[]{:S(2)}) %collective-permute-start.8) | collective-permute-done | bytes 262176 | tf_op jit(solution)/shard_map/ppermute | solution.py:25
  130.5 1.8 %add_convert_fusion = bf16[512,1024]{1,0:T(8,128)(2,1)} fusion(f32[512,1024]{1,0:T(8,128)S(1)} %fusion.13, f32[512,1024]{1,0:T(8,128)S(1)} %fusion.25, f32[512,1024]{1,0:T(8,128)S(1)} %fusion.7, bf16[256,1024]{1,0:T(8,128)(2,1)S(1)} %get-tuple-element.14, bf16[256,1024]{1,0:T(8,128)(2,1)S(1)} %collective-permute-done.4, pred[]{:T(512)S(6)} %eq.123, ...), kind=kOutput, calls=%fused_computation.9 | convolution fusion | flops 544735232 | bytes 8912897 | tf_op jit(solution)/shard_map/dot_general | solution.py:237
  (35 shorter events, 0.3 us)
Async XLA Ops:
  6.5 19.8 %copy-start = (s32[16,8]{0,1:T(8,128)S(1)}, s32[16,8]{0,1:T(8,128)}, u32[]{:S(2)}) copy-start(s32[16,8]{0,1:T(8,128)} %param.10) | copy-start | bytes 1540
  6.5 88.7 %all-gather.2.cloned.1.call-start = ((), (), s32[]{:S(2)}) async-start(), calls=%async_computation | async-start | bytes 4259840 | tf_op jit(solution)/shard_map/all_gather | solution.py:151
  11.8 45.7 %collective-permute-start = (bf16[2,8,64,128]{3,1,2,0:T(8,128)(2,1)S(1)}, bf16[2,8,64,128]{3,1,2,0:T(8,128)(2,1)}, u32[]{:S(2)}, u32[]{:S(2)}) collective-permute-start(bf16[2,8,64,128]{3,1,2,0:T(8,128)(2,1)S(1)} %copy_dynamic-update-slice_fusion), channel_id=1, source_target_pairs={{0,2},{1,3},{2,4},{3,5},{4,6},{5,7},{6,8},{7,9},{8,10},{9,11},{10,... | collective-permute-start | bytes 786440 | tf_op jit(solution)/shard_map/ppermute | solution.py:21
  16.5 41.0 %collective-permute-start.1 = (bf16[2,8,64,128]{3,1,2,0:T(8,128)(2,1)S(1)}, bf16[2,8,64,128]{3,1,2,0:T(8,128)(2,1)}, u32[]{:S(2)}, u32[]{:S(2)}) collective-permute-start(bf16[2,8,64,128]{3,1,2,0:T(8,128)(2,1)S(1)} %copy_dynamic-update-slice_fusion), channel_id=1, source_target_pairs={{0,1},{1,2},{2,3},{3,4},{4,5},{5,6},{6,7},{7,8},{8,9},{9,10},{10,1... | collective-permute-start | bytes 786440 | tf_op jit(solution)/shard_map/ppermute | solution.py:21
  21.4 15.1 %collective-permute-start.3 = (bf16[256,1024]{1,0:T(8,128)(2,1)S(1)}, bf16[256,1024]{1,0:T(8,128)(2,1)S(1)}, u32[]{:S(2)}, u32[]{:S(2)}) collective-permute-start(bf16[256,1024]{1,0:T(8,128)(2,1)S(1)} %get-tuple-element.11), channel_id=1, source_target_pairs={{0,64},{64,128},{128,192},{192,0},{1,65},{65,129},{129,193},{193,1... | collective-permute-start | bytes 1572872 | tf_op jit(solution)/shard_map/ppermute | solution.py:25
  22.7 26.0 %collective-permute-start.4 = (bf16[256,1024]{1,0:T(8,128)(2,1)S(1)}, bf16[256,1024]{1,0:T(8,128)(2,1)S(1)}, u32[]{:S(2)}, u32[]{:S(2)}) collective-permute-start(bf16[256,1024]{1,0:T(8,128)(2,1)S(1)} %get-tuple-element.13), channel_id=1, source_target_pairs={{0,128},{64,192},{128,0},{192,64},{1,129},{65,193},{129,1},{193,65... | collective-permute-start | bytes 1572872 | tf_op jit(solution)/shard_map/ppermute | solution.py:25
  25.2 23.6 %collective-permute-start.5 = (bf16[256,1024]{1,0:T(8,128)(2,1)S(1)}, bf16[256,1024]{1,0:T(8,128)(2,1)S(1)}, u32[]{:S(2)}, u32[]{:S(2)}) collective-permute-start(bf16[256,1024]{1,0:T(8,128)(2,1)S(1)} %get-tuple-element.12), channel_id=1, source_target_pairs={{0,192},{64,0},{128,64},{192,128},{1,193},{65,1},{129,65},{193,129... | collective-permute-start | bytes 1572872 | tf_op jit(solution)/shard_map/ppermute | solution.py:25
  36.5 15.8 %copy-start.3 = (bf16[256,1024]{1,0:T(8,128)(2,1)}, bf16[256,1024]{1,0:T(8,128)(2,1)S(1)}, u32[]{:S(2)}) copy-start(bf16[256,1024]{1,0:T(8,128)(2,1)S(1)} %collective-permute-done.3) | copy-start | bytes 1572868
  48.7 3.4 %copy-start.5 = (bf16[256,1024]{1,0:T(8,128)(2,1)}, bf16[256,1024]{1,0:T(8,128)(2,1)S(1)}, u32[]{:S(2)}) copy-start(bf16[256,1024]{1,0:T(8,128)(2,1)S(1)} %collective-permute-done.5) | copy-start | bytes 1572868
  50.0 60.3 %collective-permute-start.6 = (bf16[3,256,1024]{2,1,0:T(8,128)(2,1)}, bf16[3,256,1024]{2,1,0:T(8,128)(2,1)}, u32[]{:S(2)}, u32[]{:S(2)}) collective-permute-start(bf16[3,256,1024]{2,1,0:T(8,128)(2,1)} %pad_maximum_fusion), channel_id=1, source_target_pairs={{0,1},{1,0},{2,3},{3,2},{4,5},{5,4},{6,7},{7,6},{8,9},{9,8},{10,11... | collective-permute-start | bytes 4718600 | tf_op jit(solution)/shard_map/ppermute | solution.py:25
  56.6 2.4 %copy-start.1 = (bf16[512,4,128]{2,0,1:T(8,128)(2,1)}, bf16[512,4,128]{2,0,1:T(8,128)(2,1)S(1)}, u32[]{:S(2)}) copy-start(bf16[512,4,128]{2,0,1:T(8,128)(2,1)S(1)} %copy.23) | copy-start | bytes 1572868
  107.5 4.2 %copy-start.2 = (bf16[512,512]{1,0:T(8,128)(2,1)S(1)}, bf16[512,512]{1,0:T(8,128)(2,1)}, u32[]{:S(2)}) copy-start(bf16[512,512]{1,0:T(8,128)(2,1)} %shard_map.64) | copy-start | bytes 1572868
  107.5 14.7 %collective-permute-start.2 = (bf16[512,512]{1,0:T(8,128)(2,1)}, bf16[512,512]{1,0:T(8,128)(2,1)S(1)}, u32[]{:S(2)}, u32[]{:S(2)}) collective-permute-start(bf16[512,512]{1,0:T(8,128)(2,1)} %shard_map.64), channel_id=1, source_target_pairs={{0,64},{64,128},{128,192},{192,0},{1,65},{65,129},{129,193},{193,1... | collective-permute-start | bytes 1572872 | tf_op jit(solution)/shard_map/ppermute | solution.py:25
  108.8 13.8 %collective-permute-start.7 = (bf16[512,512]{1,0:T(8,128)(2,1)}, bf16[512,512]{1,0:T(8,128)(2,1)S(1)}, u32[]{:S(2)}, u32[]{:S(2)}) collective-permute-start(bf16[512,512]{1,0:T(8,128)(2,1)} %shard_map.64), channel_id=1, source_target_pairs={{0,192},{64,0},{128,64},{192,128},{1,193},{65,1},{129,65},{193,129... | collective-permute-start | bytes 1572872 | tf_op jit(solution)/shard_map/ppermute | solution.py:25
  111.8 13.5 %copy-start.4 = (bf16[256,1024]{1,0:T(8,128)(2,1)S(1)}, bf16[256,1024]{1,0:T(8,128)(2,1)}, u32[]{:S(2)}) copy-start(bf16[256,1024]{1,0:T(8,128)(2,1)} %copy-done.3) | copy-start | bytes 1572868
  122.2 8.2 %collective-permute-start.8 = (bf16[512,256]{1,0:T(8,128)(2,1)S(1)}, bf16[512,256]{1,0:T(8,128)(2,1)S(1)}, u32[]{:S(2)}, u32[]{:S(2)}) collective-permute-start(bf16[512,256]{1,0:T(8,128)(2,1)S(1)} %slice.32), channel_id=1, source_target_pairs={{0,64},{64,128},{128,192},{192,0},{1,65},{65,129},{129,193},{193,1... | collective-permute-start | bytes 786440 | tf_op jit(solution)/shard_map/ppermute | solution.py:25
  122.6 7.9 %collective-permute-start.9 = (bf16[512,256]{1,0:T(8,128)(2,1)S(1)}, bf16[512,256]{1,0:T(8,128)(2,1)S(1)}, u32[]{:S(2)}, u32[]{:S(2)}) collective-permute-start(bf16[512,256]{1,0:T(8,128)(2,1)S(1)} %slice.33), channel_id=1, source_target_pairs={{0,192},{64,0},{128,64},{192,128},{1,193},{65,1},{129,65},{193,129... | collective-permute-start | bytes 786440 | tf_op jit(solution)/shard_map/ppermute | solution.py:25
  125.3 1.0 copy-start.6
Sparse Core Ops, SparseCore 0:
  11.9 83.2 all-gather.1

commit v6 on v5

--- a/solution.py
+++ b/solution.py
@@ -206,17 +206,6 @@
         slots = (owner_dev * capacity + slot_index).reshape(local_heads, vert_count)
         key_tok = (vert_group[:, :, None] * BLOCK_TOKENS + token_pos).reshape(local_heads, 1, -1)
         query_tok = (first_block * BLOCK_TOKENS + jnp.arange(token_count, dtype=jnp.int32))[:, None]
-        attention = vertical_attention(
-            slots.astype(jnp.int32),
-            query_heads,
-            arrived,
-            key_tok.astype(jnp.int32),
-            query_tok,
-            top_diag,
-            total_diag,
-            acc_diag,
-        )
-
         def rows_of(distance):
             mine, theirs = fetched[distance - 1], sibling_w[distance - 1]
             return jnp.where(
@@ -225,16 +214,37 @@
                 jnp.concatenate([theirs, mine], axis=0),
             )
 
-        half_cols = attention.shape[1] // 2
-        behind = ring(attention, "heads", heads_n, 1)
-        ahead = ring(attention, "heads", heads_n, heads_n - 1)
-        total = jnp.dot(attention, own_w, preferred_element_type=jnp.float32)
-        far_low = ring(behind[:, :half_cols], "heads", heads_n, 1)
-        far_high = ring(ahead[:, half_cols:], "heads", heads_n, heads_n - 1)
-        total = total + jnp.dot(behind, rows_of(1), preferred_element_type=jnp.float32)
-        total = total + jnp.dot(ahead, rows_of(heads_n - 1), preferred_element_type=jnp.float32)
-        far = jnp.concatenate([far_low, far_high], axis=1)
-        total = total + jnp.dot(far, rows_of(2), preferred_element_type=jnp.float32)
+        pair_count = 2
+        pair_heads = local_heads // pair_count
+        pair_cols = pair_heads * head_dim
+        weights = [own_w] + [rows_of(distance) for distance in range(1, heads_n)]
+        total = None
+        for pair in range(pair_count):
+            heads_here = slice(pair * pair_heads, (pair + 1) * pair_heads)
+            rows_here = slice(pair * pair_cols, (pair + 1) * pair_cols)
+            attention = vertical_attention(
+                slots[heads_here].astype(jnp.int32),
+                query_heads[heads_here],
+                arrived,
+                key_tok[heads_here].astype(jnp.int32),
+                query_tok,
+                top_diag[heads_here],
+                total_diag[heads_here],
+                acc_diag[heads_here],
+            )
+            half_cols = pair_cols // 2
+            behind = ring(attention, "heads", heads_n, 1)
+            ahead = ring(attention, "heads", heads_n, heads_n - 1)
+            far_low = ring(behind[:, :half_cols], "heads", heads_n, 1)
+            far_high = ring(ahead[:, half_cols:], "heads", heads_n, heads_n - 1)
+            part = jnp.dot(attention, weights[0][rows_here], preferred_element_type=jnp.float32)
+            total = part if total is None else total + part
+            total = total + jnp.dot(behind, weights[1][rows_here], preferred_element_type=jnp.float32)
+            total = total + jnp.dot(
+                ahead, weights[heads_n - 1][rows_here], preferred_element_type=jnp.float32
+            )
+            far = jnp.concatenate([far_low, far_high], axis=1)
+            total = total + jnp.dot(far, weights[2][rows_here], preferred_element_type=jnp.float32)
         return total.astype(jnp.bfloat16)
 
     return local

time: 141 us -> 144 us (1.021)
  waiting for transfers between devices: 51.6 us -> 33.8 us
  local copies, waits for them, and re-layouts: 14.7 us -> 22.7 us
  starting transfers between devices: 19.3 us -> 24.6 us
  Pallas kernels: 12.3 us -> 16.6 us
  matrix products: 14.6 us -> 18.1 us
    ppermute x8 -> x12, waiting for transfers between devices: 32.8 us -> 19.1 us  [ring(): lax.ppermute(block, axis, [(i, (i + distance) % size) for i in range(size)])]
    slice x0 -> x12, local copies, waits for them, and re-layouts: none -> 7.96 us  [the longest x3 2.1 us: local(): total_diag[heads_here]]
    ppermute x8 -> x12, starting transfers between devices: 11.2 us -> 16.5 us  [ring(): lax.ppermute(block, axis, [(i, (i + distance) % size) for i in range(size)])]
    pallas_call x1 -> x2, Pallas kernels: 12.3 us -> 16.6 us  [vertical_attention(): pl.pallas_call(kernel, grid_spec=grid_spec, out_shape=jax.ShapeDtypeStruc...]
    all_gather x1, waiting for transfers between devices: 18.8 us -> 14.7 us  [local(): arrived = lax.all_gather(outgoing, SEQ, axis=1, tiled=True)]
    dot_general x4 -> x8, matrix products: 5.32 us -> 8.85 us  [the longest x2 2.96 us: local(): jnp.dot(attention, weights[0][rows_here], preferred_element_type=jnp.floa...]
    broadcast_in_dim x2 -> x0, local copies, waits for them, and re-layouts: 2.7 us -> none  [the longest x1 1.36 us: local(): total_diag = jnp.sum(expo_diag, axis=2, keepdims=True)]
    select_n x0 -> x2, other arithmetic: none -> 1.48 us  [rows_of(): jnp.where(core == 0, jnp.concatenate([mine, theirs], axis=0), jnp.concate...]
  transfers between devices with their start and end apart: 11 -> 15, of which waited for: 5 -> 3; matrix products, arithmetic and copies ran while one was open for 25% -> 31% of each run, Pallas kernels for 9% -> 6%
where the time goes in v6:
time: 144 us; the launch traced here: 143 us
  waiting for transfers between devices  33.8 us (23%)
  starting transfers between devices  24.6 us (17%)
  local copies, waits for them, and re-layouts  22.7 us (16%)
  matrix products  18.1 us (13%)
  Pallas kernels  16.6 us (12%)
  between operations  14.5 us (10%)
  other arithmetic  12.7 us (9%)
    ppermute x12, waiting for transfers between devices, ring(): lax.ppermute(block, axis, [(i, (i + distance) % size) for i in range(size)])  19.1 us
    pallas_call x2, Pallas kernels, vertical_attention(): pl.pallas_call(kernel, grid_spec=grid_spec, out_shape=jax.ShapeDtypeStruc...  16.6 us
    ppermute x12, starting transfers between devices, ring(): lax.ppermute(block, axis, [(i, (i + distance) % size) for i in range(size)])  16.5 us
    all_gather x1, waiting for transfers between devices, local(): arrived = lax.all_gather(outgoing, SEQ, axis=1, tiled=True)  14.7 us
    ppermute x2, starting transfers between devices, shift(): return lax.ppermute(block, axis, route)  8.08 us
    convert_element_type x1, other arithmetic, local(): expo_diag.astype(jnp.bfloat16)  5.63 us
    dot_general x1, matrix products, local(): jnp.einsum('htu,ud->htd', expo_diag.astype(jnp.bfloat16), context_v, pref...  4.66 us
    dot_general x1, matrix products, local(): jnp.einsum('htd,ud->htu', query_heads, context_k, preferred_element_type=...  3.45 us
  transfers between devices with their start and end apart: 15, of which 3 were waited for; matrix products, arithmetic and copies ran while one was open for 31% of the time, Pallas kernels for 6%

profile of v6, /device:TPU:1, one launch (start us, length us, event | category | flops | bytes accessed | tf_op | source)
XLA Modules:
  0.0 143.0 jit_solution(8295684754092551041)
XLA Ops:
  6.5 0.7 broadcast_multiply_fusion
  7.4 0.1 fusion.34
  7.5 0.6 convert_reduce_fusion.2
  8.1 0.1 convert_reduce_fusion.1
  8.2 1.6 %copy_dynamic-update-slice_fusion.1 = bf16[2,8,64,128]{3,1,2,0:T(8,128)(2,1)} fusion(bf16[1,8,64,128]{3,2,1,0:T(8,128)(2,1)} %bitcast.111), kind=kLoop, calls=%fused_computation.44 | loop fusion | bytes 262144
  9.9 1.6 %copy_dynamic-update-slice_fusion = bf16[2,8,64,128]{3,1,2,0:T(8,128)(2,1)} fusion(bf16[2,8,64,128]{3,1,2,0:T(8,128)(2,1)} %copy_dynamic-update-slice_fusion.1, bf16[1,8,64,128]{3,2,1,0:T(8,128)(2,1)} %bitcast.112), kind=kLoop, calls=%fused_computation.43 | loop fusion | bytes 262144 | tf_op jit(solution)/shard_map/stack | solution.py:129
  12.3 1.2 fusion.6
  13.4 0.6 copy.42
  14.1 4.7 %collective-permute-start = (bf16[2,8,64,128]{3,1,2,0:T(8,128)(2,1)}, bf16[2,8,64,128]{3,1,2,0:T(8,128)(2,1)}, u32[]{:S(2)}, u32[]{:S(2)}) collective-permute-start(bf16[2,8,64,128]{3,1,2,0:T(8,128)(2,1)} %copy_dynamic-update-slice_fusion), channel_id=1, source_target_pairs={{0,2},{1,3},{2,4},{3,5},{4,6},{5,7},{6,8},{7,9},{8,10},{9,11},{10,... | collective-permute-start | bytes 786440 | tf_op jit(solution)/shard_map/ppermute | solution.py:21
  18.8 3.4 %collective-permute-start.1 = (bf16[2,8,64,128]{3,1,2,0:T(8,128)(2,1)}, bf16[2,8,64,128]{3,1,2,0:T(8,128)(2,1)}, u32[]{:S(2)}, u32[]{:S(2)}) collective-permute-start(bf16[2,8,64,128]{3,1,2,0:T(8,128)(2,1)} %copy_dynamic-update-slice_fusion), channel_id=1, source_target_pairs={{0,1},{1,2},{2,3},{3,4},{4,5},{5,6},{6,7},{7,8},{8,9},{9,10},{10,1... | collective-permute-start | bytes 786440 | tf_op jit(solution)/shard_map/ppermute | solution.py:21
  22.2 2.5 %fusion.48 = (bf16[256,1024]{1,0:T(8,128)(2,1)}, bf16[256,1024]{1,0:T(8,128)(2,1)}, bf16[256,1024]{1,0:T(8,128)(2,1)}) fusion(bf16[512,4096]{1,0:T(8,128)(2,1)} %param.11, s32[]{:T(128)S(6)} %select_n.97, s32[]{:T(128)S(6)} %select_n.99, s32[]{:T(128)S(6)} %select_n.103, s32[]{:T(128)S(6)} %select_n.101), kind=kLoop, calls=%fused_computation.99 | loop fusion | bytes 3145744 | tf_op jit(solution)/shard_map/dynamic_slice | solution.py:159
  24.7 1.2 collective-permute-start.3
  26.0 2.5 %collective-permute-start.4 = (bf16[256,1024]{1,0:T(8,128)(2,1)}, bf16[256,1024]{1,0:T(8,128)(2,1)S(1)}, u32[]{:S(2)}, u32[]{:S(2)}) collective-permute-start(bf16[256,1024]{1,0:T(8,128)(2,1)} %get-tuple-element.13), channel_id=1, source_target_pairs={{0,128},{64,192},{128,0},{192,64},{1,129},{65,193},{129,1},{193,65... | collective-permute-start | bytes 1572872 | tf_op jit(solution)/shard_map/ppermute | solution.py:25
  28.4 1.2 collective-permute-start.5
  29.7 0.1 compare_reduce_fusion.1
  29.8 0.2 convert_reduce_fusion
  30.2 0.1 compare_reduce_fusion
  30.4 0.6 fusion.53
  31.0 0.8 iota_add_fusion.query_tok_ref
  31.8 0.2 copy.38
  32.0 0.3 copy.39
  32.3 0.8 fusion.51
  33.1 6.9 %collective-permute-done.3 = bf16[256,1024]{1,0:T(8,128)(2,1)S(1)} collective-permute-done((bf16[256,1024]{1,0:T(8,128)(2,1)}, bf16[256,1024]{1,0:T(8,128)(2,1)S(1)}, u32[]{:S(2)}, u32[]{:S(2)}) %collective-permute-start.3) | collective-permute-done | bytes 524320 | tf_op jit(solution)/shard_map/ppermute | solution.py:25
  40.0 12.2 %collective-permute-done.4 = bf16[256,1024]{1,0:T(8,128)(2,1)S(1)} collective-permute-done((bf16[256,1024]{1,0:T(8,128)(2,1)}, bf16[256,1024]{1,0:T(8,128)(2,1)S(1)}, u32[]{:S(2)}, u32[]{:S(2)}) %collective-permute-start.4) | collective-permute-done | bytes 524320 | tf_op jit(solution)/shard_map/ppermute | solution.py:25
  52.2 1.3 pad_maximum_fusion
  53.5 0.5 collective-permute-start.6
  54.1 0.2 broadcast_in_dim.14
  54.3 0.2 reshape.296
  54.6 0.2 broadcast_in_dim.16
  54.8 0.2 reshape.298
  55.0 0.7 tile.2
  55.7 2.1 %and.169 = pred[512,1536]{0,1:T(8,128)(4,1)S(1)} reshape(pred[8,64,24,64]{1,0,3,2:T(8,128)(4,1)S(1)} %tile.2) | data formatting | bytes 1572864 | tf_op jit(solution)/shard_map/and | solution.py:191
  57.8 0.7 slice.112.key_tok_ref
  58.5 0.7 slice.132.key_tok_ref
  59.2 1.2 pad_maximum_fusion.1
  60.7 3.4 %fusion = (f32[4,512]{1,0:T(4,128)S(1)}, f32[1536,4,512]{2,0,1:T(8,128)S(1)}) fusion(pred[512,1536]{0,1:T(8,128)(4,1)S(1)} %and.169, pred[4,512,24]{1,2,0:T(8,128)(4,1)S(1)} %reshape.298, pred[4,512,24]{1,2,0:T(8,128)(4,1)S(1)} %reshape.296, bf16[1536,128,1]{1,0,2:T(8,128)(2,1)S(1)} %bitcast.109, bf16[512,4,128]{2,0,1:T(8,128)(2,1)S(1)} %copy.39), kind=kOutput, calls=%fused_computation.2 | convolution fusion | flops 821032960 | bytes 14393344 | tf_op jit(solution)/shard_map/htd,ud->htu/dot_general | solution.py:183
  64.1 5.6 %fusion.4 = (bf16[4,512,1536]{1,2,0:T(8,128)(2,1)}, f32[4,512]{1,0:T(4,128)S(1)}) fusion(f32[1536,4,512]{2,0,1:T(8,128)S(1)} %get-tuple-element.38, f32[4,512]{1,0:T(4,128)S(1)} %get-tuple-element.37, pred[512,1536]{0,1:T(8,128)(4,1)S(1)} %and.169, pred[4,512,24]{1,2,0:T(8,128)(4,1)S(1)} %reshape.298, pred[4,512,24]{1,2,0:T(8,128)(4,1)S(1)} %reshape.296), kind=kLoop, calls=%fused_computation.7 | loop fusion | flops 22018048 | bytes 19775488 | tf_op jit(solution)/shard_map/convert_element_type | solution.py:199
  69.8 1.0 copy.50.tot_ref
  70.8 1.0 copy.49.top_ref
  71.8 1.0 copy.52.tot_ref
  72.9 1.0 copy.51.top_ref
  73.9 4.7 %fusion.54 = f32[4,512,128]{2,1,0:T(8,128)S(1)} fusion(bf16[4,512,1536]{1,2,0:T(8,128)(2,1)} %get-tuple-element.9, bf16[1536,128,1]{1,0,2:T(8,128)(2,1)S(1)} %bitcast.108), kind=kOutput, calls=%fused_computation.105 | convolution fusion | flops 805306368 | bytes 7733248 | tf_op jit(solution)/shard_map/htu,ud->htd/dot_general | solution.py:197
  78.6 1.1 fusion.49
  79.6 1.6 %slice_bitcast_fusion = (bf16[256,1024]{1,0:T(8,128)(2,1)S(1)}, bf16[256,1024]{1,0:T(8,128)(2,1)S(1)}, bf16[256,1024]{1,0:T(8,128)(2,1)S(1)}) fusion(bf16[3,256,1024]{2,1,0:T(8,128)(2,1)} %collective-permute-done.6), kind=kLoop, calls=%fused_computation.27 | loop fusion | bytes 3145728 | tf_op jit(solution)/shard_map/squeeze | solution.py:210
  81.3 0.5 maximum_select_fusion.2
  81.8 1.0 maximum_select_fusion
  82.8 14.7 %all-gather.2.cloned.1.call-done = bf16[2,8192,128]{2,1,0:T(8,128)(2,1)} async-done(((bf16[2,128,128]{2,1,0:T(8,128)(2,1)}), bf16[2,8192,128]{2,1,0:T(8,128)(2,1)}) %all-gather.2.cloned.1.call-update) | async-done | bytes 4194320 | tf_op jit(solution)/shard_map/all_gather | solution.py:151
  97.5 8.2 %shard_map.64 = bf16[512,256]{1,0:T(8,128)(2,1)} custom-call(s32[2,16]{1,0:T(2,128)} %get-tuple-element.31.slots_ref, bf16[2,512,128]{2,1,0:T(8,128)(2,1)} %get-tuple-element.21.q_ref, bf16[2,128,64,128]{3,2,1,0:T(8,128)(2,1)} %bitcast.101, s32[2,1,1024]{2,1,0:T(1,128)} %slice.112.key_tok_ref, s32[512,1]{1,0:T(8,128)} %iota_add_fusion.query_tok_ref, ...), custom_call_target="tpu_custom_call" | custom-call | tf_op jit(solution)/shard_map/pallas_call | solution.py:101
  105.7 1.1 collective-permute-start.2
  106.8 1.7 %collective-permute-start.7 = (bf16[512,256]{1,0:T(8,128)(2,1)}, bf16[512,256]{1,0:T(8,128)(2,1)}, u32[]{:S(2)}, u32[]{:S(2)}) collective-permute-start(bf16[512,256]{1,0:T(8,128)(2,1)} %shard_map.64), channel_id=1, source_target_pairs={{0,192},{64,0},{128,64},{192,128},{1,193},{65,1},{129,65},{193,129... | collective-permute-start | bytes 786440 | tf_op jit(solution)/shard_map/ppermute | solution.py:25
  108.5 8.4 %shard_map.65 = bf16[512,256]{1,0:T(8,128)(2,1)} custom-call(s32[2,16]{1,0:T(2,128)} %get-tuple-element.32.slots_ref, bf16[2,512,128]{2,1,0:T(8,128)(2,1)} %get-tuple-element.22.q_ref, bf16[2,128,64,128]{3,2,1,0:T(8,128)(2,1)} %bitcast.102, s32[2,1,1024]{2,1,0:T(1,128)} %slice.132.key_tok_ref, s32[512,1]{1,0:T(8,128)} %iota_add_fusion.query_tok_ref, ...), custom_call_target="tpu_custom_call" | custom-call | tf_op jit(solution)/shard_map/pallas_call | solution.py:101
  117.0 2.7 %collective-permute-start.11 = (bf16[512,256]{1,0:T(8,128)(2,1)}, bf16[512,256]{1,0:T(8,128)(2,1)S(1)}, u32[]{:S(2)}, u32[]{:S(2)}) collective-permute-start(bf16[512,256]{1,0:T(8,128)(2,1)} %shard_map.65), channel_id=1, source_target_pairs={{0,192},{64,0},{128,64},{192,128},{1,193},{65,1},{129,65},{193,129... | collective-permute-start | bytes 786440 | tf_op jit(solution)/shard_map/ppermute | solution.py:25
  119.6 1.5 %fusion.23 = f32[512,1024]{1,0:T(8,128)S(1)} fusion(bf16[512,256]{1,0:T(8,128)(2,1)S(1)} %copy-done.6, bf16[512,4096]{1,0:T(8,128)(2,1)} %param.11, s32[]{:T(128)S(6)} %select_n.95), kind=kOutput, calls=%fused_computation.34 | convolution fusion | flops 268435456 | bytes 2883588 | tf_op jit(solution)/shard_map/dot_general | solution.py:240
  121.1 1.5 %fusion.15 = f32[512,1024]{1,0:T(8,128)S(1)} fusion(bf16[512,256]{1,0:T(8,128)(2,1)S(1)} %copy-done.7, bf16[512,4096]{1,0:T(8,128)(2,1)} %param.11, s32[]{:T(128)S(6)} %add.184, s32[]{:T(128)S(6)} %select_n.95), kind=kOutput, calls=%fused_computation.23 | convolution fusion | flops 268435456 | bytes 2883592 | tf_op jit(solution)/shard_map/dot_general | solution.py:240
  122.6 0.9 slice.155
  123.7 0.9 slice.156
  124.6 2.7 %collective-permute-start.9 = (bf16[512,128]{1,0:T(8,128)(2,1)S(1)}, bf16[512,128]{1,0:T(8,128)(2,1)S(1)}, u32[]{:S(2)}, u32[]{:S(2)}) collective-permute-start(bf16[512,128]{1,0:T(8,128)(2,1)S(1)} %slice.156), channel_id=1, source_target_pairs={{0,192},{64,0},{128,64},{192,128},{1,193},{65,1},{129,65},{193,129... | collective-permute-start | bytes 393224 | tf_op jit(solution)/shard_map/ppermute | solution.py:25
  127.4 2.7 %collective-permute-start.13 = (bf16[512,128]{1,0:T(8,128)(2,1)S(1)}, bf16[512,128]{1,0:T(8,128)(2,1)S(1)}, u32[]{:S(2)}, u32[]{:S(2)}) collective-permute-start(bf16[512,128]{1,0:T(8,128)(2,1)S(1)} %slice.167), channel_id=1, source_target_pairs={{0,192},{64,0},{128,64},{192,128},{1,193},{65,1},{129,65},{193,129... | collective-permute-start | bytes 393224 | tf_op jit(solution)/shard_map/ppermute | solution.py:25
  130.2 1.4 fusion.21
  131.6 0.4 fusion.13
  132.0 1.4 fusion.19
  133.4 0.4 fusion.11
  133.9 0.4 fusion.17
  134.3 1.8 %add_convert_fusion = bf16[512,1024]{1,0:T(8,128)(2,1)} fusion(f32[512,1024]{1,0:T(8,128)S(1)} %fusion.11, f32[512,1024]{1,0:T(8,128)S(1)} %fusion.13, f32[512,1024]{1,0:T(8,128)S(1)} %fusion.15, f32[512,1024]{1,0:T(8,128)S(1)} %fusion.17, f32[512,1024]{1,0:T(8,128)S(1)} %fusion.19, f32[512,1024]{1,0:T(8,128)S(1)} %fusion.23, f32[512,1024]{1,0:T(8,128)S(1)} %fusion.21, ...), kind=kOutput, calls=%fused_computation.9 | convolution fusion | flops 273154048 | bytes 16515072 | tf_op jit(solution)/shard_map/dot_general | solution.py:247
  (62 shorter events, 1.4 us)
Async XLA Ops:
  6.5 23.0 %copy-start = (s32[16,8]{0,1:T(8,128)S(1)}, s32[16,8]{0,1:T(8,128)}, u32[]{:S(2)}) copy-start(s32[16,8]{0,1:T(8,128)} %param.10) | copy-start | bytes 1540
  6.5 91.0 %all-gather.2.cloned.1.call-start = ((), (), s32[]{:S(2)}) async-start(), calls=%async_computation | async-start | bytes 4259840 | tf_op jit(solution)/shard_map/all_gather | solution.py:151
  11.5 20.2 %copy-start.8 = (bf16[512,512]{1,0:T(8,128)(2,1)S(1)}, bf16[512,512]{1,0:T(8,128)(2,1)}, u32[]{:S(2)}) copy-start(bf16[512,512]{1,0:T(8,128)(2,1)} %param.6) | copy-start | bytes 1572868
  14.1 45.1 %collective-permute-start = (bf16[2,8,64,128]{3,1,2,0:T(8,128)(2,1)}, bf16[2,8,64,128]{3,1,2,0:T(8,128)(2,1)}, u32[]{:S(2)}, u32[]{:S(2)}) collective-permute-start(bf16[2,8,64,128]{3,1,2,0:T(8,128)(2,1)} %copy_dynamic-update-slice_fusion), channel_id=1, source_target_pairs={{0,2},{1,3},{2,4},{3,5},{4,6},{5,7},{6,8},{7,9},{8,10},{9,11},{10,... | collective-permute-start | bytes 786440 | tf_op jit(solution)/shard_map/ppermute | solution.py:21
  18.8 40.4 %collective-permute-start.1 = (bf16[2,8,64,128]{3,1,2,0:T(8,128)(2,1)}, bf16[2,8,64,128]{3,1,2,0:T(8,128)(2,1)}, u32[]{:S(2)}, u32[]{:S(2)}) collective-permute-start(bf16[2,8,64,128]{3,1,2,0:T(8,128)(2,1)} %copy_dynamic-update-slice_fusion), channel_id=1, source_target_pairs={{0,1},{1,2},{2,3},{3,4},{4,5},{5,6},{6,7},{7,8},{8,9},{9,10},{10,1... | collective-permute-start | bytes 786440 | tf_op jit(solution)/shard_map/ppermute | solution.py:21
  24.7 15.2 %collective-permute-start.3 = (bf16[256,1024]{1,0:T(8,128)(2,1)}, bf16[256,1024]{1,0:T(8,128)(2,1)S(1)}, u32[]{:S(2)}, u32[]{:S(2)}) collective-permute-start(bf16[256,1024]{1,0:T(8,128)(2,1)} %get-tuple-element.11), channel_id=1, source_target_pairs={{0,64},{64,128},{128,192},{192,0},{1,65},{65,129},{129,193},{193,1... | collective-permute-start | bytes 1572872 | tf_op jit(solution)/shard_map/ppermute | solution.py:25
  26.0 26.2 %collective-permute-start.4 = (bf16[256,1024]{1,0:T(8,128)(2,1)}, bf16[256,1024]{1,0:T(8,128)(2,1)S(1)}, u32[]{:S(2)}, u32[]{:S(2)}) collective-permute-start(bf16[256,1024]{1,0:T(8,128)(2,1)} %get-tuple-element.13), channel_id=1, source_target_pairs={{0,128},{64,192},{128,0},{192,64},{1,129},{65,193},{129,1},{193,65... | collective-permute-start | bytes 1572872 | tf_op jit(solution)/shard_map/ppermute | solution.py:25
  28.4 23.8 %collective-permute-start.5 = (bf16[256,1024]{1,0:T(8,128)(2,1)}, bf16[256,1024]{1,0:T(8,128)(2,1)S(1)}, u32[]{:S(2)}, u32[]{:S(2)}) collective-permute-start(bf16[256,1024]{1,0:T(8,128)(2,1)} %get-tuple-element.12), channel_id=1, source_target_pairs={{0,192},{64,0},{128,64},{192,128},{1,193},{65,1},{129,65},{193,129... | collective-permute-start | bytes 1572872 | tf_op jit(solution)/shard_map/ppermute | solution.py:25
  40.0 15.0 %copy-start.2 = (bf16[256,1024]{1,0:T(8,128)(2,1)}, bf16[256,1024]{1,0:T(8,128)(2,1)S(1)}, u32[]{:S(2)}) copy-start(bf16[256,1024]{1,0:T(8,128)(2,1)S(1)} %collective-permute-done.3) | copy-start | bytes 1572868
  52.2 2.6 %copy-start.4 = (bf16[256,1024]{1,0:T(8,128)(2,1)}, bf16[256,1024]{1,0:T(8,128)(2,1)S(1)}, u32[]{:S(2)}) copy-start(bf16[256,1024]{1,0:T(8,128)(2,1)S(1)} %collective-permute-done.5) | copy-start | bytes 1572868
  53.5 26.2 %collective-permute-start.6 = (bf16[3,256,1024]{2,1,0:T(8,128)(2,1)}, bf16[3,256,1024]{2,1,0:T(8,128)(2,1)}, u32[]{:S(2)}, u32[]{:S(2)}) collective-permute-start(bf16[3,256,1024]{2,1,0:T(8,128)(2,1)} %pad_maximum_fusion), channel_id=1, source_target_pairs={{0,1},{1,0},{2,3},{3,2},{4,5},{5,4},{6,7},{7,6},{8,9},{9,8},{10,11... | collective-permute-start | bytes 4718600 | tf_op jit(solution)/shard_map/ppermute | solution.py:25
  79.6 2.1 %copy-start.3 = (bf16[256,1024]{1,0:T(8,128)(2,1)S(1)}, bf16[256,1024]{1,0:T(8,128)(2,1)}, u32[]{:S(2)}) copy-start(bf16[256,1024]{1,0:T(8,128)(2,1)} %copy-done.2) | copy-start | bytes 1572868
  79.6 2.1 %copy-start.5 = (bf16[256,1024]{1,0:T(8,128)(2,1)S(1)}, bf16[256,1024]{1,0:T(8,128)(2,1)}, u32[]{:S(2)}) copy-start(bf16[256,1024]{1,0:T(8,128)(2,1)} %copy-done.4) | copy-start | bytes 1572868
  105.7 16.9 %collective-permute-start.2 = (bf16[512,256]{1,0:T(8,128)(2,1)}, bf16[512,256]{1,0:T(8,128)(2,1)}, u32[]{:S(2)}, u32[]{:S(2)}) collective-permute-start(bf16[512,256]{1,0:T(8,128)(2,1)} %shard_map.64), channel_id=1, source_target_pairs={{0,64},{64,128},{128,192},{192,0},{1,65},{65,129},{129,193},{193,1... | collective-permute-start | bytes 786440 | tf_op jit(solution)/shard_map/ppermute | solution.py:25
  106.8 16.9 %collective-permute-start.7 = (bf16[512,256]{1,0:T(8,128)(2,1)}, bf16[512,256]{1,0:T(8,128)(2,1)}, u32[]{:S(2)}, u32[]{:S(2)}) collective-permute-start(bf16[512,256]{1,0:T(8,128)(2,1)} %shard_map.64), channel_id=1, source_target_pairs={{0,192},{64,0},{128,64},{192,128},{1,193},{65,1},{129,65},{193,129... | collective-permute-start | bytes 786440 | tf_op jit(solution)/shard_map/ppermute | solution.py:25
  108.5 11.1 %copy-start.6 = (bf16[512,256]{1,0:T(8,128)(2,1)S(1)}, bf16[512,256]{1,0:T(8,128)(2,1)}, u32[]{:S(2)}) copy-start(bf16[512,256]{1,0:T(8,128)(2,1)} %shard_map.64) | copy-start | bytes 786436
  116.9 4.2 %copy-start.7 = (bf16[512,256]{1,0:T(8,128)(2,1)S(1)}, bf16[512,256]{1,0:T(8,128)(2,1)}, u32[]{:S(2)}) copy-start(bf16[512,256]{1,0:T(8,128)(2,1)} %shard_map.65) | copy-start | bytes 786436
  116.9 10.4 %collective-permute-start.10 = (bf16[512,256]{1,0:T(8,128)(2,1)}, bf16[512,256]{1,0:T(8,128)(2,1)S(1)}, u32[]{:S(2)}, u32[]{:S(2)}) collective-permute-start(bf16[512,256]{1,0:T(8,128)(2,1)} %shard_map.65), channel_id=1, source_target_pairs={{0,64},{64,128},{128,192},{192,0},{1,65},{65,129},{129,193},{193,1... | collective-permute-start | bytes 786440 | tf_op jit(solution)/shard_map/ppermute | solution.py:25
  117.0 10.4 %collective-permute-start.11 = (bf16[512,256]{1,0:T(8,128)(2,1)}, bf16[512,256]{1,0:T(8,128)(2,1)S(1)}, u32[]{:S(2)}, u32[]{:S(2)}) collective-permute-start(bf16[512,256]{1,0:T(8,128)(2,1)} %shard_map.65), channel_id=1, source_target_pairs={{0,192},{64,0},{128,64},{192,128},{1,193},{65,1},{129,65},{193,129... | collective-permute-start | bytes 786440 | tf_op jit(solution)/shard_map/ppermute | solution.py:25
  123.6 10.3 %collective-permute-start.8 = (bf16[512,128]{1,0:T(8,128)(2,1)S(1)}, bf16[512,128]{1,0:T(8,128)(2,1)S(1)}, u32[]{:S(2)}, u32[]{:S(2)}) collective-permute-start(bf16[512,128]{1,0:T(8,128)(2,1)S(1)} %slice.155), channel_id=1, source_target_pairs={{0,64},{64,128},{128,192},{192,0},{1,65},{65,129},{129,193},{193,1... | collective-permute-start | bytes 393224 | tf_op jit(solution)/shard_map/ppermute | solution.py:25
  124.6 9.3 %collective-permute-start.9 = (bf16[512,128]{1,0:T(8,128)(2,1)S(1)}, bf16[512,128]{1,0:T(8,128)(2,1)S(1)}, u32[]{:S(2)}, u32[]{:S(2)}) collective-permute-start(bf16[512,128]{1,0:T(8,128)(2,1)S(1)} %slice.156), channel_id=1, source_target_pairs={{0,192},{64,0},{128,64},{192,128},{1,193},{65,1},{129,65},{193,129... | collective-permute-start | bytes 393224 | tf_op jit(solution)/shard_map/ppermute | solution.py:25
  127.3 7.0 %collective-permute-start.12 = (bf16[512,128]{1,0:T(8,128)(2,1)S(1)}, bf16[512,128]{1,0:T(8,128)(2,1)S(1)}, u32[]{:S(2)}, u32[]{:S(2)}) collective-permute-start(bf16[512,128]{1,0:T(8,128)(2,1)S(1)} %slice.166), channel_id=1, source_target_pairs={{0,64},{64,128},{128,192},{192,0},{1,65},{65,129},{129,193},{193,1... | collective-permute-start | bytes 393224 | tf_op jit(solution)/shard_map/ppermute | solution.py:25
  127.4 6.9 %collective-permute-start.13 = (bf16[512,128]{1,0:T(8,128)(2,1)S(1)}, bf16[512,128]{1,0:T(8,128)(2,1)S(1)}, u32[]{:S(2)}, u32[]{:S(2)}) collective-permute-start(bf16[512,128]{1,0:T(8,128)(2,1)S(1)} %slice.167), channel_id=1, source_target_pairs={{0,192},{64,0},{128,64},{192,128},{1,193},{65,1},{129,65},{193,129... | collective-permute-start | bytes 393224 | tf_op jit(solution)/shard_map/ppermute | solution.py:25
  134.3 1.8 %copy-start.1 = (s32[16,8]{0,1:T(8,128)S(1)}, s32[16,8]{0,1:T(8,128)}, u32[]{:S(2)}) copy-start(s32[16,8]{0,1:T(8,128)} %param.10) | copy-start | bytes 1540
Sparse Core Ops, SparseCore 0:
  14.2 83.2 all-gather.1

commit v7 on v5

--- a/solution.py
+++ b/solution.py
@@ -55,13 +55,14 @@
         for copy in block_copies(0, 0):
             copy.start()
 
+    for copy in block_copies(head, current):
+        copy.wait()
+
     @pl.when(head + 1 < heads)
     def _():
         for copy in block_copies(head + 1, 1 - current):
             copy.start()
 
-    for copy in block_copies(head, current):
-        copy.wait()
     s = lax.dot_general(
         q_ref[0], k_buf[current], (((1,), (1,)), ((), ())), preferred_element_type=jnp.float32
     ) * scale
@@ -141,9 +142,17 @@
         pick = jnp.stack(
             [owned_blocks & (below == 0), owned_blocks & (below == owned_total - 1)]
         ).astype(jnp.bfloat16)
-        outgoing = jnp.einsum(
-            "cb,kbtd->kctd", pick, paired, preferred_element_type=jnp.float32
-        ).astype(jnp.bfloat16).reshape(2, capacity * BLOCK_TOKENS, head_dim)
+        outgoing = jnp.stack(
+            [
+                jnp.einsum(
+                    "cb,btd->ctd",
+                    pick,
+                    part.reshape(block_count, BLOCK_TOKENS, head_dim),
+                    preferred_element_type=jnp.float32,
+                ).astype(jnp.bfloat16)
+                for part in (keys, values)
+            ]
+        ).reshape(2, capacity * BLOCK_TOKENS, head_dim)
         same_owner = (owner_dev[:, None] == owner_dev[None, :]) & (
             union_list[None, :] < union_list[:, None]
         )

time: 141 us -> 141 us (level)
  local copies, waits for them, and re-layouts: 14.7 us -> 11.9 us
  matrix products: 14.6 us -> 16.6 us
  other arithmetic: 12.3 us -> 13.8 us
    dot_general x1 -> x2, matrix products: 0.22 us -> 2.2 us  [local(): jnp.einsum('cb,btd->ctd', pick, part.reshape(block_count, BLOCK_TOKENS, h...]
    another operation x0 -> x2, other arithmetic: none -> 1.64 us  [the longest x1 1 us: local(): jnp.stack([keys, values]).reshape(2, block_count, BLOCK_TOKENS, head_dim)]
  transfers between devices with their start and end apart: 11 -> 11, of which waited for: 5 -> 5; matrix products, arithmetic and copies ran while one was open for 25% -> 26% of each run, Pallas kernels for 9% -> 9%
where the time goes in v7:
time: 141 us; the launch traced here: 139 us
  waiting for transfers between devices  50.9 us (36%)
  starting transfers between devices  19.3 us (14%)
  matrix products  16.6 us (12%)
  between operations  14.4 us (10%)
  other arithmetic  13.8 us (10%)
  Pallas kernels  12.3 us (9%)
  local copies, waits for them, and re-layouts  11.9 us (8%)
    ppermute x8, waiting for transfers between devices, ring(): lax.ppermute(block, axis, [(i, (i + distance) % size) for i in range(size)])  32.8 us
    all_gather x1, waiting for transfers between devices, local(): arrived = lax.all_gather(outgoing, SEQ, axis=1, tiled=True)  18.1 us
    pallas_call x1, Pallas kernels, vertical_attention(): pl.pallas_call(kernel, grid_spec=grid_spec, out_shape=jax.ShapeDtypeStruc...  12.3 us
    ppermute x8, starting transfers between devices, ring(): lax.ppermute(block, axis, [(i, (i + distance) % size) for i in range(size)])  11.3 us
    ppermute x2, starting transfers between devices, shift(): return lax.ppermute(block, axis, route)  8.08 us
    dot_general x1, matrix products, local(): jnp.einsum('htu,ud->htd', expo_diag.astype(jnp.bfloat16), context_v, pref...  5.66 us
    convert_element_type x1, other arithmetic, local(): expo_diag.astype(jnp.bfloat16)  5.59 us
    dot_general x1, matrix products, local(): jnp.einsum('htd,ud->htu', query_heads, context_k, preferred_element_type=...  3.4 us
  transfers between devices with their start and end apart: 11, of which 5 were waited for; matrix products, arithmetic and copies ran while one was open for 26% of the time, Pallas kernels for 9%

profile of v7, /device:TPU:1, one launch (start us, length us, event | category | flops | bytes accessed | tf_op | source)
XLA Modules:
  0.0 139.2 jit_solution(2213013451628649852)
XLA Ops:
  6.5 0.7 broadcast_multiply_fusion
  7.2 0.1 reshape.323
  7.4 0.1 fusion.37
  7.5 0.6 convert_reduce_fusion.2
  8.1 0.1 convert_reduce_fusion.1
  8.9 1.1 convolution_convert_fusion.1
  10.0 1.1 convolution_convert_fusion
  11.1 0.6 pad_maximum_fusion.2
  11.8 1.0 pad_maximum_fusion.1
  12.8 4.7 %collective-permute-start = (bf16[2,8,64,128]{3,2,1,0:T(8,128)(2,1)S(1)}, bf16[2,8,64,128]{3,2,1,0:T(8,128)(2,1)}, u32[]{:S(2)}, u32[]{:S(2)}) collective-permute-start(bf16[2,8,64,128]{3,2,1,0:T(8,128)(2,1)S(1)} %pad_maximum_fusion.1), channel_id=1, source_target_pairs={{0,2},{1,3},{2,4},{3,5},{4,6},{5,7},{6,8},{7,9},{8,10},{9,11},{10,... | collective-permute-start | bytes 786440 | tf_op jit(solution)/shard_map/ppermute | solution.py:21
  17.6 3.3 %collective-permute-start.1 = (bf16[2,8,64,128]{3,2,1,0:T(8,128)(2,1)S(1)}, bf16[2,8,64,128]{3,2,1,0:T(8,128)(2,1)}, u32[]{:S(2)}, u32[]{:S(2)}) collective-permute-start(bf16[2,8,64,128]{3,2,1,0:T(8,128)(2,1)S(1)} %pad_maximum_fusion.1), channel_id=1, source_target_pairs={{0,1},{1,2},{2,3},{3,4},{4,5},{5,6},{6,7},{7,8},{8,9},{9,10},{10,1... | collective-permute-start | bytes 786440 | tf_op jit(solution)/shard_map/ppermute | solution.py:21
  20.9 1.5 %fusion.49 = (bf16[256,1024]{1,0:T(8,128)(2,1)S(1)}, bf16[256,1024]{1,0:T(8,128)(2,1)S(1)}, bf16[256,1024]{1,0:T(8,128)(2,1)S(1)}) fusion(bf16[512,4096]{1,0:T(8,128)(2,1)} %param.11, s32[]{:T(128)S(6)} %select_n.96, s32[]{:T(128)S(6)} %select_n.98, s32[]{:T(128)S(6)} %select_n.102, s32[]{:T(128)S(6)} %select_n.100), kind=kLoop, calls=%fused_computation.99 | loop fusion | bytes 3145744 | tf_op jit(solution)/shard_map/dynamic_slice | solution.py:168
  22.4 1.3 collective-permute-start.3
  23.7 2.5 %collective-permute-start.4 = (bf16[256,1024]{1,0:T(8,128)(2,1)S(1)}, bf16[256,1024]{1,0:T(8,128)(2,1)S(1)}, u32[]{:S(2)}, u32[]{:S(2)}) collective-permute-start(bf16[256,1024]{1,0:T(8,128)(2,1)S(1)} %get-tuple-element.13), channel_id=1, source_target_pairs={{0,128},{64,192},{128,0},{192,64},{1,129},{65,193},{129,1},{193,65... | collective-permute-start | bytes 1572872 | tf_op jit(solution)/shard_map/ppermute | solution.py:25
  26.2 1.2 collective-permute-start.5
  27.3 0.1 constant_dynamic-slice_fusion
  27.4 0.1 copy.29
  27.5 0.2 convert_reduce_fusion
  27.7 0.1 reduce_sum.39
  27.8 0.1 broadcast_subtract_fusion
  27.8 0.1 compare_reduce_fusion
  28.0 0.1 compare_reduce_fusion.1
  28.1 0.1 subtract_compare_fusion.1
  28.1 0.6 fusion.41.slots_ref
  28.7 8.8 %collective-permute-done.3 = bf16[256,1024]{1,0:T(8,128)(2,1)S(1)} collective-permute-done((bf16[256,1024]{1,0:T(8,128)(2,1)S(1)}, bf16[256,1024]{1,0:T(8,128)(2,1)S(1)}, u32[]{:S(2)}, u32[]{:S(2)}) %collective-permute-start.3) | collective-permute-done | bytes 524320 | tf_op jit(solution)/shard_map/ppermute | solution.py:25
  37.5 12.2 %collective-permute-done.4 = bf16[256,1024]{1,0:T(8,128)(2,1)S(1)} collective-permute-done((bf16[256,1024]{1,0:T(8,128)(2,1)S(1)}, bf16[256,1024]{1,0:T(8,128)(2,1)S(1)}, u32[]{:S(2)}, u32[]{:S(2)}) %collective-permute-start.4) | collective-permute-done | bytes 524320 | tf_op jit(solution)/shard_map/ppermute | solution.py:25
  49.7 1.3 pad_maximum_fusion
  51.1 0.6 collective-permute-start.6
  51.6 0.7 iota_add_fusion.query_tok_ref
  52.4 0.1 copy.30
  52.5 0.2 broadcast_in_dim.18
  52.7 0.2 reshape.328
  52.9 0.1 copy.31
  53.0 0.2 broadcast_in_dim.20
  53.2 0.2 reshape.330
  53.4 0.7 tile.2
  54.1 2.1 %and.167 = pred[512,1536]{0,1:T(8,128)(4,1)S(1)} reshape(pred[8,64,24,64]{1,0,3,2:T(8,128)(4,1)S(1)} %tile.2) | data formatting | bytes 1572864 | tf_op jit(solution)/shard_map/and | solution.py:200
  56.2 1.3 copy.23
  57.4 0.3 copy.24
  57.7 0.1 add.155
  57.8 0.1 add.156
  57.9 0.1 add.158
  58.0 0.6 broadcast_add_fusion.key_tok_ref
  58.6 1.1 maximum_maximum_fusion
  59.7 0.1 fusion.50
  59.8 3.4 %fusion = (f32[4,512]{1,0:T(4,128)S(1)}, f32[1536,4,512]{2,0,1:T(8,128)S(1)}) fusion(pred[512,1536]{0,1:T(8,128)(4,1)S(1)} %and.167, pred[4,512,24]{1,2,0:T(8,128)(4,1)S(1)} %reshape.330, pred[4,512,24]{1,2,0:T(8,128)(4,1)S(1)} %reshape.328, bf16[1536,128,1]{1,0,2:T(8,128)(2,1)S(1)} %bitcast.96, bf16[512,4,128]{2,0,1:T(8,128)(2,1)S(1)} %copy.24), kind=kOutput, calls=%fused_computation.2 | convolution fusion | flops 821032960 | bytes 14393344 | tf_op jit(solution)/shard_map/htd,ud->htu/dot_general | solution.py:192
  63.2 5.6 %fusion.4 = (bf16[4,512,1536]{1,2,0:T(8,128)(2,1)}, f32[4,512]{1,0:T(4,128)S(1)}) fusion(f32[1536,4,512]{2,0,1:T(8,128)S(1)} %get-tuple-element.26, f32[4,512]{1,0:T(4,128)S(1)} %get-tuple-element.25, pred[512,1536]{0,1:T(8,128)(4,1)S(1)} %and.167, pred[4,512,24]{1,2,0:T(8,128)(4,1)S(1)} %reshape.330, pred[4,512,24]{1,2,0:T(8,128)(4,1)S(1)} %reshape.328), kind=kLoop, calls=%fused_computation.7 | loop fusion | flops 22018048 | bytes 19775488 | tf_op jit(solution)/shard_map/convert_element_type | solution.py:208
  68.8 1.4 copy.34.tot_ref
  70.2 1.3 copy.33.top_ref
  71.5 5.7 %fusion.51.acc_ref = f32[4,512,128]{2,1,0:T(8,128)} fusion(bf16[4,512,1536]{1,2,0:T(8,128)(2,1)} %get-tuple-element.9, bf16[1536,128,1]{1,0,2:T(8,128)(2,1)S(1)} %bitcast.95), kind=kOutput, calls=%fused_computation.101 | convolution fusion | flops 805306368 | bytes 7733248 | tf_op jit(solution)/shard_map/htu,ud->htd/dot_general | solution.py:206
  77.2 18.1 %all-gather.2.cloned.1.call-done = bf16[2,8192,128]{2,1,0:T(8,128)(2,1)} async-done(((bf16[2,128,128]{2,1,0:T(8,128)(2,1)}), bf16[2,8192,128]{2,1,0:T(8,128)(2,1)}) %all-gather.2.cloned.1.call-update) | async-done | bytes 4194320 | tf_op jit(solution)/shard_map/all_gather | solution.py:160
  95.2 12.3 %shard_map.64 = bf16[512,512]{1,0:T(8,128)(2,1)} custom-call(s32[4,16]{1,0:T(4,128)} %fusion.41.slots_ref, bf16[4,512,128]{2,1,0:T(8,128)(2,1)} %bitcast.91, bf16[2,128,64,128]{3,2,1,0:T(8,128)(2,1)} %bitcast.92, s32[4,1,1024]{2,1,0:T(1,128)} %broadcast_add_fusion.key_tok_ref, s32[512,1]{1,0:T(8,128)} %iota_add_fusion.query_tok_ref, ...), custom_call_target="tpu_custom_call" | custom-call | tf_op jit(solution)/shard_map/pallas_call | solution.py:102
  107.5 1.3 collective-permute-start.2
  108.8 1.5 %collective-permute-start.7 = (bf16[512,512]{1,0:T(8,128)(2,1)}, bf16[512,512]{1,0:T(8,128)(2,1)S(1)}, u32[]{:S(2)}, u32[]{:S(2)}) collective-permute-start(bf16[512,512]{1,0:T(8,128)(2,1)} %shard_map.64), channel_id=1, source_target_pairs={{0,192},{64,0},{128,64},{192,128},{1,193},{65,1},{129,65},{193,129... | collective-permute-start | bytes 1572872 | tf_op jit(solution)/shard_map/ppermute | solution.py:25
  110.3 1.5 %slice_bitcast_fusion = (bf16[256,1024]{1,0:T(8,128)(2,1)S(1)}, bf16[256,1024]{1,0:T(8,128)(2,1)S(1)}, bf16[256,1024]{1,0:T(8,128)(2,1)S(1)}) fusion(bf16[3,256,1024]{2,1,0:T(8,128)(2,1)} %collective-permute-done.6), kind=kLoop, calls=%fused_computation.40 | loop fusion | bytes 3145728 | tf_op jit(solution)/shard_map/squeeze | solution.py:230
  111.8 2.0 %fusion.24 = f32[512,1024]{1,0:T(8,128)S(1)} fusion(bf16[512,512]{1,0:T(8,128)(2,1)S(1)} %copy-done.2, bf16[512,4096]{1,0:T(8,128)(2,1)} %param.11, s32[]{:T(128)S(6)} %select_n.94), kind=kOutput, calls=%fused_computation.34 | convolution fusion | flops 536870912 | bytes 3670020 | tf_op jit(solution)/shard_map/dot_general | solution.py:240
  113.8 8.4 %collective-permute-done.2 = bf16[512,512]{1,0:T(8,128)(2,1)S(1)} collective-permute-done((bf16[512,512]{1,0:T(8,128)(2,1)}, bf16[512,512]{1,0:T(8,128)(2,1)S(1)}, u32[]{:S(2)}, u32[]{:S(2)}) %collective-permute-start.2) | collective-permute-done | bytes 524320 | tf_op jit(solution)/shard_map/ppermute | solution.py:25
  122.3 0.3 collective-permute-start.8
  122.6 2.7 %collective-permute-start.9 = (bf16[512,256]{1,0:T(8,128)(2,1)S(1)}, bf16[512,256]{1,0:T(8,128)(2,1)S(1)}, u32[]{:S(2)}, u32[]{:S(2)}) collective-permute-start(bf16[512,256]{1,0:T(8,128)(2,1)S(1)} %slice.33), channel_id=1, source_target_pairs={{0,192},{64,0},{128,64},{192,128},{1,193},{65,1},{129,65},{193,129... | collective-permute-start | bytes 786440 | tf_op jit(solution)/shard_map/ppermute | solution.py:25
  125.4 0.7 fusion.6
  126.1 0.3 copy-done.8
  126.4 0.7 fusion.12
  127.1 3.4 %collective-permute-done.8 = bf16[512,256]{1,0:T(8,128)(2,1)S(1)} collective-permute-done((bf16[512,256]{1,0:T(8,128)(2,1)S(1)}, bf16[512,256]{1,0:T(8,128)(2,1)S(1)}, u32[]{:S(2)}, u32[]{:S(2)}) %collective-permute-start.8) | collective-permute-done | bytes 262176 | tf_op jit(solution)/shard_map/ppermute | solution.py:25
  130.5 1.8 %add_convert_fusion = bf16[512,1024]{1,0:T(8,128)(2,1)} fusion(f32[512,1024]{1,0:T(8,128)S(1)} %fusion.12, f32[512,1024]{1,0:T(8,128)S(1)} %fusion.24, f32[512,1024]{1,0:T(8,128)S(1)} %fusion.6, bf16[256,1024]{1,0:T(8,128)(2,1)S(1)} %get-tuple-element.14, bf16[256,1024]{1,0:T(8,128)(2,1)S(1)} %collective-permute-done.4, pred[]{:T(512)S(6)} %eq.123, ...), kind=kOutput, calls=%fused_computation.9 | convolution fusion | flops 544735232 | bytes 8912897 | tf_op jit(solution)/shard_map/dot_general | solution.py:246
  (39 shorter events, 0.2 us)
Async XLA Ops:
  6.5 20.8 %copy-start = (s32[16,8]{0,1:T(8,128)S(1)}, s32[16,8]{0,1:T(8,128)}, u32[]{:S(2)}) copy-start(s32[16,8]{0,1:T(8,128)} %param.10) | copy-start | bytes 1540
  6.5 88.7 %all-gather.2.cloned.1.call-start = ((), (), s32[]{:S(2)}) async-start(), calls=%async_computation | async-start | bytes 4259840 | tf_op jit(solution)/shard_map/all_gather | solution.py:160
  12.8 45.8 %collective-permute-start = (bf16[2,8,64,128]{3,2,1,0:T(8,128)(2,1)S(1)}, bf16[2,8,64,128]{3,2,1,0:T(8,128)(2,1)}, u32[]{:S(2)}, u32[]{:S(2)}) collective-permute-start(bf16[2,8,64,128]{3,2,1,0:T(8,128)(2,1)S(1)} %pad_maximum_fusion.1), channel_id=1, source_target_pairs={{0,2},{1,3},{2,4},{3,5},{4,6},{5,7},{6,8},{7,9},{8,10},{9,11},{10,... | collective-permute-start | bytes 786440 | tf_op jit(solution)/shard_map/ppermute | solution.py:21
  17.6 41.1 %collective-permute-start.1 = (bf16[2,8,64,128]{3,2,1,0:T(8,128)(2,1)S(1)}, bf16[2,8,64,128]{3,2,1,0:T(8,128)(2,1)}, u32[]{:S(2)}, u32[]{:S(2)}) collective-permute-start(bf16[2,8,64,128]{3,2,1,0:T(8,128)(2,1)S(1)} %pad_maximum_fusion.1), channel_id=1, source_target_pairs={{0,1},{1,2},{2,3},{3,4},{4,5},{5,6},{6,7},{7,8},{8,9},{9,10},{10,1... | collective-permute-start | bytes 786440 | tf_op jit(solution)/shard_map/ppermute | solution.py:21
  22.4 15.1 %collective-permute-start.3 = (bf16[256,1024]{1,0:T(8,128)(2,1)S(1)}, bf16[256,1024]{1,0:T(8,128)(2,1)S(1)}, u32[]{:S(2)}, u32[]{:S(2)}) collective-permute-start(bf16[256,1024]{1,0:T(8,128)(2,1)S(1)} %get-tuple-element.11), channel_id=1, source_target_pairs={{0,64},{64,128},{128,192},{192,0},{1,65},{65,129},{129,193},{193,1... | collective-permute-start | bytes 1572872 | tf_op jit(solution)/shard_map/ppermute | solution.py:25
  23.7 26.0 %collective-permute-start.4 = (bf16[256,1024]{1,0:T(8,128)(2,1)S(1)}, bf16[256,1024]{1,0:T(8,128)(2,1)S(1)}, u32[]{:S(2)}, u32[]{:S(2)}) collective-permute-start(bf16[256,1024]{1,0:T(8,128)(2,1)S(1)} %get-tuple-element.13), channel_id=1, source_target_pairs={{0,128},{64,192},{128,0},{192,64},{1,129},{65,193},{129,1},{193,65... | collective-permute-start | bytes 1572872 | tf_op jit(solution)/shard_map/ppermute | solution.py:25
  26.2 23.5 %collective-permute-start.5 = (bf16[256,1024]{1,0:T(8,128)(2,1)S(1)}, bf16[256,1024]{1,0:T(8,128)(2,1)S(1)}, u32[]{:S(2)}, u32[]{:S(2)}) collective-permute-start(bf16[256,1024]{1,0:T(8,128)(2,1)S(1)} %get-tuple-element.12), channel_id=1, source_target_pairs={{0,192},{64,0},{128,64},{192,128},{1,193},{65,1},{129,65},{193,129... | collective-permute-start | bytes 1572872 | tf_op jit(solution)/shard_map/ppermute | solution.py:25
  37.5 15.9 %copy-start.5 = (bf16[256,1024]{1,0:T(8,128)(2,1)}, bf16[256,1024]{1,0:T(8,128)(2,1)S(1)}, u32[]{:S(2)}) copy-start(bf16[256,1024]{1,0:T(8,128)(2,1)S(1)} %collective-permute-done.3) | copy-start | bytes 1572868
  49.7 3.4 %copy-start.7 = (bf16[256,1024]{1,0:T(8,128)(2,1)}, bf16[256,1024]{1,0:T(8,128)(2,1)S(1)}, u32[]{:S(2)}) copy-start(bf16[256,1024]{1,0:T(8,128)(2,1)S(1)} %collective-permute-done.5) | copy-start | bytes 1572868
  51.1 59.2 %collective-permute-start.6 = (bf16[3,256,1024]{2,1,0:T(8,128)(2,1)}, bf16[3,256,1024]{2,1,0:T(8,128)(2,1)}, u32[]{:S(2)}, u32[]{:S(2)}) collective-permute-start(bf16[3,256,1024]{2,1,0:T(8,128)(2,1)} %pad_maximum_fusion), channel_id=1, source_target_pairs={{0,1},{1,0},{2,3},{3,2},{4,5},{5,4},{6,7},{7,6},{8,9},{9,8},{10,11... | collective-permute-start | bytes 4718600 | tf_op jit(solution)/shard_map/ppermute | solution.py:25
  54.0 4.6 %copy-start.3 = (bf16[512,128]{1,0:T(8,128)(2,1)S(1)}, bf16[512,128]{1,0:T(8,128)(2,1)}, u32[]{:S(2)}) copy-start(bf16[512,128]{1,0:T(8,128)(2,1)} %param.8) | copy-start | bytes 393220
  54.1 4.6 %copy-start.4 = (bf16[512,128]{1,0:T(8,128)(2,1)S(1)}, bf16[512,128]{1,0:T(8,128)(2,1)}, u32[]{:S(2)}) copy-start(bf16[512,128]{1,0:T(8,128)(2,1)} %param.7) | copy-start | bytes 393220
  57.7 5.5 %copy-start.1 = (bf16[512,4,128]{2,0,1:T(8,128)(2,1)}, bf16[512,4,128]{2,0,1:T(8,128)(2,1)S(1)}, u32[]{:S(2)}) copy-start(bf16[512,4,128]{2,0,1:T(8,128)(2,1)S(1)} %copy.24) | copy-start | bytes 1572868
  107.5 4.2 %copy-start.2 = (bf16[512,512]{1,0:T(8,128)(2,1)S(1)}, bf16[512,512]{1,0:T(8,128)(2,1)}, u32[]{:S(2)}) copy-start(bf16[512,512]{1,0:T(8,128)(2,1)} %shard_map.64) | copy-start | bytes 1572868
  107.5 14.7 %collective-permute-start.2 = (bf16[512,512]{1,0:T(8,128)(2,1)}, bf16[512,512]{1,0:T(8,128)(2,1)S(1)}, u32[]{:S(2)}, u32[]{:S(2)}) collective-permute-start(bf16[512,512]{1,0:T(8,128)(2,1)} %shard_map.64), channel_id=1, source_target_pairs={{0,64},{64,128},{128,192},{192,0},{1,65},{65,129},{129,193},{193,1... | collective-permute-start | bytes 1572872 | tf_op jit(solution)/shard_map/ppermute | solution.py:25
  108.8 13.8 %collective-permute-start.7 = (bf16[512,512]{1,0:T(8,128)(2,1)}, bf16[512,512]{1,0:T(8,128)(2,1)S(1)}, u32[]{:S(2)}, u32[]{:S(2)}) collective-permute-start(bf16[512,512]{1,0:T(8,128)(2,1)} %shard_map.64), channel_id=1, source_target_pairs={{0,192},{64,0},{128,64},{192,128},{1,193},{65,1},{129,65},{193,129... | collective-permute-start | bytes 1572872 | tf_op jit(solution)/shard_map/ppermute | solution.py:25
  111.8 13.6 %copy-start.6 = (bf16[256,1024]{1,0:T(8,128)(2,1)S(1)}, bf16[256,1024]{1,0:T(8,128)(2,1)}, u32[]{:S(2)}) copy-start(bf16[256,1024]{1,0:T(8,128)(2,1)} %copy-done.5) | copy-start | bytes 1572868
  122.3 8.2 %collective-permute-start.8 = (bf16[512,256]{1,0:T(8,128)(2,1)S(1)}, bf16[512,256]{1,0:T(8,128)(2,1)S(1)}, u32[]{:S(2)}, u32[]{:S(2)}) collective-permute-start(bf16[512,256]{1,0:T(8,128)(2,1)S(1)} %slice.32), channel_id=1, source_target_pairs={{0,64},{64,128},{128,192},{192,0},{1,65},{65,129},{129,193},{193,1... | collective-permute-start | bytes 786440 | tf_op jit(solution)/shard_map/ppermute | solution.py:25
  122.6 7.9 %collective-permute-start.9 = (bf16[512,256]{1,0:T(8,128)(2,1)S(1)}, bf16[512,256]{1,0:T(8,128)(2,1)S(1)}, u32[]{:S(2)}, u32[]{:S(2)}) collective-permute-start(bf16[512,256]{1,0:T(8,128)(2,1)S(1)} %slice.33), channel_id=1, source_target_pairs={{0,192},{64,0},{128,64},{192,128},{1,193},{65,1},{129,65},{193,129... | collective-permute-start | bytes 786440 | tf_op jit(solution)/shard_map/ppermute | solution.py:25
  125.4 1.0 copy-start.8
Sparse Core Ops, SparseCore 0:
  11.9 83.2 all-gather.1

commit v8 on v5

--- a/solution.py
+++ b/solution.py
@@ -55,13 +55,14 @@
         for copy in block_copies(0, 0):
             copy.start()
 
+    for copy in block_copies(head, current):
+        copy.wait()
+
     @pl.when(head + 1 < heads)
     def _():
         for copy in block_copies(head + 1, 1 - current):
             copy.start()
 
-    for copy in block_copies(head, current):
-        copy.wait()
     s = lax.dot_general(
         q_ref[0], k_buf[current], (((1,), (1,)), ((), ())), preferred_element_type=jnp.float32
     ) * scale
@@ -138,12 +139,16 @@
             axis=1,
         )
         owned_total = jnp.sum(owned_blocks.astype(jnp.int32))
-        pick = jnp.stack(
-            [owned_blocks & (below == 0), owned_blocks & (below == owned_total - 1)]
-        ).astype(jnp.bfloat16)
-        outgoing = jnp.einsum(
-            "cb,kbtd->kctd", pick, paired, preferred_element_type=jnp.float32
-        ).astype(jnp.bfloat16).reshape(2, capacity * BLOCK_TOKENS, head_dim)
+        pick = jnp.stack([owned_blocks & (below == 0), owned_blocks & (below == owned_total - 1)])
+
+        def picked(part):
+            blocks = part.reshape(block_count, BLOCK_TOKENS, head_dim).astype(jnp.float32)
+            chosen_blocks = jnp.where(pick[:, :, None, None], blocks[None], 0.0)
+            return jnp.sum(chosen_blocks, axis=1).astype(part.dtype)
+
+        outgoing = jnp.stack([picked(keys), picked(values)]).reshape(
+            2, capacity * BLOCK_TOKENS, head_dim
+        )
         same_owner = (owner_dev[:, None] == owner_dev[None, :]) & (
             union_list[None, :] < union_list[:, None]
         )

time: 141 us -> 139 us (0.986)
  local copies, waits for them, and re-layouts: 14.7 us -> 11.9 us
  other arithmetic: 12.3 us -> 14.9 us
    another operation x0 -> x3, other arithmetic: none -> 1.64 us  [the longest x1 1 us: local(): jnp.stack([keys, values]).reshape(2, block_count, BLOCK_TOKENS, head_dim)]
  transfers between devices with their start and end apart: 11 -> 11, of which waited for: 5 -> 5; matrix products, arithmetic and copies ran while one was open for 25% -> 26% of each run, Pallas kernels for 9% -> 9%
where the time goes in v8:
time: 139 us; the launch traced here: 138 us
  waiting for transfers between devices  51 us (37%)
  starting transfers between devices  19.3 us (14%)
  other arithmetic  14.9 us (11%)
  matrix products  14.4 us (10%)
  between operations  14.4 us (10%)
  Pallas kernels  12.3 us (9%)
  local copies, waits for them, and re-layouts  11.9 us (9%)
    ppermute x8, waiting for transfers between devices, ring(): lax.ppermute(block, axis, [(i, (i + distance) % size) for i in range(size)])  32.9 us
    all_gather x1, waiting for transfers between devices, local(): arrived = lax.all_gather(outgoing, SEQ, axis=1, tiled=True)  18.1 us
    pallas_call x1, Pallas kernels, vertical_attention(): pl.pallas_call(kernel, grid_spec=grid_spec, out_shape=jax.ShapeDtypeStruc...  12.3 us
    ppermute x8, starting transfers between devices, ring(): lax.ppermute(block, axis, [(i, (i + distance) % size) for i in range(size)])  11.2 us
    ppermute x2, starting transfers between devices, shift(): return lax.ppermute(block, axis, route)  8.08 us
    dot_general x1, matrix products, local(): jnp.einsum('htu,ud->htd', expo_diag.astype(jnp.bfloat16), context_v, pref...  5.65 us
    convert_element_type x1, other arithmetic, local(): expo_diag.astype(jnp.bfloat16)  5.59 us
    dot_general x1, matrix products, local(): jnp.einsum('htd,ud->htu', query_heads, context_k, preferred_element_type=...  3.4 us
  transfers between devices with their start and end apart: 11, of which 5 were waited for; matrix products, arithmetic and copies ran while one was open for 26% of the time, Pallas kernels for 9%

profile of v8, /device:TPU:1, one launch (start us, length us, event | category | flops | bytes accessed | tf_op | source)
XLA Modules:
  0.0 138.1 jit_solution(11704832113533222548)
XLA Ops:
  6.5 0.7 broadcast_multiply_fusion
  7.2 0.1 reshape.360
  7.4 0.1 fusion.35
  7.5 0.6 convert_reduce_fusion.2
  8.1 0.1 convert_reduce_fusion.1
  8.9 1.0 bitcast_convert_fusion
  9.9 0.1 select_reduce_fusion.1
  10.1 0.6 pad_maximum_fusion.2
  10.7 1.0 pad_maximum_fusion.1
  11.7 4.7 %collective-permute-start = (bf16[2,8,64,128]{3,2,1,0:T(8,128)(2,1)S(1)}, bf16[2,8,64,128]{3,2,1,0:T(8,128)(2,1)}, u32[]{:S(2)}, u32[]{:S(2)}) collective-permute-start(bf16[2,8,64,128]{3,2,1,0:T(8,128)(2,1)S(1)} %pad_maximum_fusion.1), channel_id=1, source_target_pairs={{0,2},{1,3},{2,4},{3,5},{4,6},{5,7},{6,8},{7,9},{8,10},{9,11},{10,... | collective-permute-start | bytes 786440 | tf_op jit(solution)/shard_map/ppermute | solution.py:21
  16.5 3.4 %collective-permute-start.1 = (bf16[2,8,64,128]{3,2,1,0:T(8,128)(2,1)S(1)}, bf16[2,8,64,128]{3,2,1,0:T(8,128)(2,1)}, u32[]{:S(2)}, u32[]{:S(2)}) collective-permute-start(bf16[2,8,64,128]{3,2,1,0:T(8,128)(2,1)S(1)} %pad_maximum_fusion.1), channel_id=1, source_target_pairs={{0,1},{1,2},{2,3},{3,4},{4,5},{5,6},{6,7},{7,8},{8,9},{9,10},{10,1... | collective-permute-start | bytes 786440 | tf_op jit(solution)/shard_map/ppermute | solution.py:21
  19.9 1.5 %fusion.47 = (bf16[256,1024]{1,0:T(8,128)(2,1)S(1)}, bf16[256,1024]{1,0:T(8,128)(2,1)S(1)}, bf16[256,1024]{1,0:T(8,128)(2,1)S(1)}) fusion(bf16[512,4096]{1,0:T(8,128)(2,1)} %param.11, s32[]{:T(128)S(6)} %select_n.105, s32[]{:T(128)S(6)} %select_n.107, s32[]{:T(128)S(6)} %select_n.111, s32[]{:T(128)S(6)} %select_n.109), kind=kLoop, calls=%fused_computation.99 | loop fusion | bytes 3145744 | tf_op jit(solution)/shard_map/dynamic_slice | solution.py:164
  21.4 1.3 collective-permute-start.3
  22.7 2.5 %collective-permute-start.4 = (bf16[256,1024]{1,0:T(8,128)(2,1)S(1)}, bf16[256,1024]{1,0:T(8,128)(2,1)S(1)}, u32[]{:S(2)}, u32[]{:S(2)}) collective-permute-start(bf16[256,1024]{1,0:T(8,128)(2,1)S(1)} %get-tuple-element.15), channel_id=1, source_target_pairs={{0,128},{64,192},{128,0},{192,64},{1,129},{65,193},{129,1},{193,65... | collective-permute-start | bytes 1572872 | tf_op jit(solution)/shard_map/ppermute | solution.py:25
  25.1 1.2 collective-permute-start.5
  26.3 0.1 constant_dynamic-slice_fusion
  26.3 0.1 copy.19
  26.4 0.2 convert_reduce_fusion
  26.6 0.1 reduce_sum.57
  26.7 0.1 broadcast_subtract_fusion
  26.8 0.1 compare_reduce_fusion
  26.9 0.1 compare_reduce_fusion.1
  27.0 0.1 subtract_compare_fusion.1
  27.1 0.6 fusion.39.slots_ref
  27.6 8.8 %collective-permute-done.3 = bf16[256,1024]{1,0:T(8,128)(2,1)S(1)} collective-permute-done((bf16[256,1024]{1,0:T(8,128)(2,1)S(1)}, bf16[256,1024]{1,0:T(8,128)(2,1)S(1)}, u32[]{:S(2)}, u32[]{:S(2)}) %collective-permute-start.3) | collective-permute-done | bytes 524320 | tf_op jit(solution)/shard_map/ppermute | solution.py:25
  36.5 12.2 %collective-permute-done.4 = bf16[256,1024]{1,0:T(8,128)(2,1)S(1)} collective-permute-done((bf16[256,1024]{1,0:T(8,128)(2,1)S(1)}, bf16[256,1024]{1,0:T(8,128)(2,1)S(1)}, u32[]{:S(2)}, u32[]{:S(2)}) %collective-permute-start.4) | collective-permute-done | bytes 524320 | tf_op jit(solution)/shard_map/ppermute | solution.py:25
  48.7 1.3 pad_maximum_fusion
  50.0 0.5 collective-permute-start.6
  50.6 0.7 iota_add_fusion.query_tok_ref
  51.3 0.1 copy.20
  51.4 0.2 broadcast_in_dim.85
  51.6 0.2 reshape.363
  51.8 0.1 copy.21
  51.9 0.2 broadcast_in_dim.87
  52.1 0.2 reshape.365
  52.3 0.7 tile.2
  53.0 2.1 %and.167 = pred[512,1536]{0,1:T(8,128)(4,1)S(1)} reshape(pred[8,64,24,64]{1,0,3,2:T(8,128)(4,1)S(1)} %tile.2) | data formatting | bytes 1572864 | tf_op jit(solution)/shard_map/and | solution.py:196
  55.1 1.3 copy.17
  56.4 0.3 copy.18
  56.6 0.1 add.155
  56.7 0.1 add.156
  56.8 0.1 add.158
  56.9 0.6 broadcast_add_fusion.key_tok_ref
  57.5 1.1 maximum_maximum_fusion
  58.6 0.1 fusion.48
  58.7 3.4 %fusion = (f32[4,512]{1,0:T(4,128)S(1)}, f32[1536,4,512]{2,0,1:T(8,128)S(1)}) fusion(pred[512,1536]{0,1:T(8,128)(4,1)S(1)} %and.167, pred[4,512,24]{1,2,0:T(8,128)(4,1)S(1)} %reshape.365, pred[4,512,24]{1,2,0:T(8,128)(4,1)S(1)} %reshape.363, bf16[1536,128,1]{1,0,2:T(8,128)(2,1)S(1)} %bitcast.96, bf16[512,4,128]{2,0,1:T(8,128)(2,1)S(1)} %copy.18), kind=kOutput, calls=%fused_computation.2 | convolution fusion | flops 821032960 | bytes 14393344 | tf_op jit(solution)/shard_map/htd,ud->htu/dot_general | solution.py:188
  62.1 5.6 %fusion.4 = (bf16[4,512,1536]{1,2,0:T(8,128)(2,1)}, f32[4,512]{1,0:T(4,128)S(1)}) fusion(f32[1536,4,512]{2,0,1:T(8,128)S(1)} %get-tuple-element.28, f32[4,512]{1,0:T(4,128)S(1)} %get-tuple-element.27, pred[512,1536]{0,1:T(8,128)(4,1)S(1)} %and.167, pred[4,512,24]{1,2,0:T(8,128)(4,1)S(1)} %reshape.365, pred[4,512,24]{1,2,0:T(8,128)(4,1)S(1)} %reshape.363), kind=kLoop, calls=%fused_computation.7 | loop fusion | flops 22018048 | bytes 19775488 | tf_op jit(solution)/shard_map/convert_element_type | solution.py:204
  67.7 1.3 copy.24.tot_ref
  69.1 1.3 copy.23.top_ref
  70.4 5.7 %fusion.49.acc_ref = f32[4,512,128]{2,1,0:T(8,128)} fusion(bf16[4,512,1536]{1,2,0:T(8,128)(2,1)} %get-tuple-element.11, bf16[1536,128,1]{1,0,2:T(8,128)(2,1)S(1)} %bitcast.95), kind=kOutput, calls=%fused_computation.101 | convolution fusion | flops 805306368 | bytes 7733248 | tf_op jit(solution)/shard_map/htu,ud->htd/dot_general | solution.py:202
  76.1 18.1 %all-gather.2.cloned.1.call-done = bf16[2,8192,128]{2,1,0:T(8,128)(2,1)} async-done(((bf16[2,128,128]{2,1,0:T(8,128)(2,1)}), bf16[2,8192,128]{2,1,0:T(8,128)(2,1)}) %all-gather.2.cloned.1.call-update) | async-done | bytes 4194320 | tf_op jit(solution)/shard_map/all_gather | solution.py:156
  94.2 12.3 %shard_map.64 = bf16[512,512]{1,0:T(8,128)(2,1)} custom-call(s32[4,16]{1,0:T(4,128)} %fusion.39.slots_ref, bf16[4,512,128]{2,1,0:T(8,128)(2,1)} %bitcast.91, bf16[2,128,64,128]{3,2,1,0:T(8,128)(2,1)} %bitcast.92, s32[4,1,1024]{2,1,0:T(1,128)} %broadcast_add_fusion.key_tok_ref, s32[512,1]{1,0:T(8,128)} %iota_add_fusion.query_tok_ref, ...), custom_call_target="tpu_custom_call" | custom-call | tf_op jit(solution)/shard_map/pallas_call | solution.py:102
  106.5 1.3 collective-permute-start.2
  107.7 1.5 %collective-permute-start.7 = (bf16[512,512]{1,0:T(8,128)(2,1)}, bf16[512,512]{1,0:T(8,128)(2,1)S(1)}, u32[]{:S(2)}, u32[]{:S(2)}) collective-permute-start(bf16[512,512]{1,0:T(8,128)(2,1)} %shard_map.64), channel_id=1, source_target_pairs={{0,192},{64,0},{128,64},{192,128},{1,193},{65,1},{129,65},{193,129... | collective-permute-start | bytes 1572872 | tf_op jit(solution)/shard_map/ppermute | solution.py:25
  109.2 1.5 %slice_bitcast_fusion = (bf16[256,1024]{1,0:T(8,128)(2,1)S(1)}, bf16[256,1024]{1,0:T(8,128)(2,1)S(1)}, bf16[256,1024]{1,0:T(8,128)(2,1)S(1)}) fusion(bf16[3,256,1024]{2,1,0:T(8,128)(2,1)} %collective-permute-done.6), kind=kLoop, calls=%fused_computation.38 | loop fusion | bytes 3145728 | tf_op jit(solution)/shard_map/squeeze | solution.py:226
  110.7 2.0 %fusion.24 = f32[512,1024]{1,0:T(8,128)S(1)} fusion(bf16[512,512]{1,0:T(8,128)(2,1)S(1)} %copy-done.2, bf16[512,4096]{1,0:T(8,128)(2,1)} %param.11, s32[]{:T(128)S(6)} %select_n.103), kind=kOutput, calls=%fused_computation.32 | convolution fusion | flops 536870912 | bytes 3670020 | tf_op jit(solution)/shard_map/dot_general | solution.py:236
  112.7 8.4 %collective-permute-done.2 = bf16[512,512]{1,0:T(8,128)(2,1)S(1)} collective-permute-done((bf16[512,512]{1,0:T(8,128)(2,1)}, bf16[512,512]{1,0:T(8,128)(2,1)S(1)}, u32[]{:S(2)}, u32[]{:S(2)}) %collective-permute-start.2) | collective-permute-done | bytes 524320 | tf_op jit(solution)/shard_map/ppermute | solution.py:25
  121.2 0.3 collective-permute-start.8
  121.5 2.7 %collective-permute-start.9 = (bf16[512,256]{1,0:T(8,128)(2,1)S(1)}, bf16[512,256]{1,0:T(8,128)(2,1)S(1)}, u32[]{:S(2)}, u32[]{:S(2)}) collective-permute-start(bf16[512,256]{1,0:T(8,128)(2,1)S(1)} %slice.33), channel_id=1, source_target_pairs={{0,192},{64,0},{128,64},{192,128},{1,193},{65,1},{129,65},{193,129... | collective-permute-start | bytes 786440 | tf_op jit(solution)/shard_map/ppermute | solution.py:25
  124.3 0.7 fusion.6
  125.0 0.3 copy-done.8
  125.3 0.7 fusion.12
  126.1 3.4 %collective-permute-done.8 = bf16[512,256]{1,0:T(8,128)(2,1)S(1)} collective-permute-done((bf16[512,256]{1,0:T(8,128)(2,1)S(1)}, bf16[512,256]{1,0:T(8,128)(2,1)S(1)}, u32[]{:S(2)}, u32[]{:S(2)}) %collective-permute-start.8) | collective-permute-done | bytes 262176 | tf_op jit(solution)/shard_map/ppermute | solution.py:25
  129.4 1.8 %add_convert_fusion = bf16[512,1024]{1,0:T(8,128)(2,1)} fusion(f32[512,1024]{1,0:T(8,128)S(1)} %fusion.12, f32[512,1024]{1,0:T(8,128)S(1)} %fusion.24, f32[512,1024]{1,0:T(8,128)S(1)} %fusion.6, bf16[256,1024]{1,0:T(8,128)(2,1)S(1)} %get-tuple-element.16, bf16[256,1024]{1,0:T(8,128)(2,1)S(1)} %collective-permute-done.4, pred[]{:T(512)S(6)} %eq.123, ...), kind=kOutput, calls=%fused_computation.9 | convolution fusion | flops 544735232 | bytes 8912897 | tf_op jit(solution)/shard_map/dot_general | solution.py:242
  (38 shorter events, 0.2 us)
Async XLA Ops:
  6.5 19.7 %copy-start = (s32[16,8]{0,1:T(8,128)S(1)}, s32[16,8]{0,1:T(8,128)}, u32[]{:S(2)}) copy-start(s32[16,8]{0,1:T(8,128)} %param.10) | copy-start | bytes 1540
  6.5 87.6 %all-gather.2.cloned.1.call-start = ((), (), s32[]{:S(2)}) async-start(), calls=%async_computation | async-start | bytes 4259840 | tf_op jit(solution)/shard_map/all_gather | solution.py:156
  11.7 45.8 %collective-permute-start = (bf16[2,8,64,128]{3,2,1,0:T(8,128)(2,1)S(1)}, bf16[2,8,64,128]{3,2,1,0:T(8,128)(2,1)}, u32[]{:S(2)}, u32[]{:S(2)}) collective-permute-start(bf16[2,8,64,128]{3,2,1,0:T(8,128)(2,1)S(1)} %pad_maximum_fusion.1), channel_id=1, source_target_pairs={{0,2},{1,3},{2,4},{3,5},{4,6},{5,7},{6,8},{7,9},{8,10},{9,11},{10,... | collective-permute-start | bytes 786440 | tf_op jit(solution)/shard_map/ppermute | solution.py:21
  16.5 41.0 %collective-permute-start.1 = (bf16[2,8,64,128]{3,2,1,0:T(8,128)(2,1)S(1)}, bf16[2,8,64,128]{3,2,1,0:T(8,128)(2,1)}, u32[]{:S(2)}, u32[]{:S(2)}) collective-permute-start(bf16[2,8,64,128]{3,2,1,0:T(8,128)(2,1)S(1)} %pad_maximum_fusion.1), channel_id=1, source_target_pairs={{0,1},{1,2},{2,3},{3,4},{4,5},{5,6},{6,7},{7,8},{8,9},{9,10},{10,1... | collective-permute-start | bytes 786440 | tf_op jit(solution)/shard_map/ppermute | solution.py:21
  21.4 15.1 %collective-permute-start.3 = (bf16[256,1024]{1,0:T(8,128)(2,1)S(1)}, bf16[256,1024]{1,0:T(8,128)(2,1)S(1)}, u32[]{:S(2)}, u32[]{:S(2)}) collective-permute-start(bf16[256,1024]{1,0:T(8,128)(2,1)S(1)} %get-tuple-element.13), channel_id=1, source_target_pairs={{0,64},{64,128},{128,192},{192,0},{1,65},{65,129},{129,193},{193,1... | collective-permute-start | bytes 1572872 | tf_op jit(solution)/shard_map/ppermute | solution.py:25
  22.7 26.0 %collective-permute-start.4 = (bf16[256,1024]{1,0:T(8,128)(2,1)S(1)}, bf16[256,1024]{1,0:T(8,128)(2,1)S(1)}, u32[]{:S(2)}, u32[]{:S(2)}) collective-permute-start(bf16[256,1024]{1,0:T(8,128)(2,1)S(1)} %get-tuple-element.15), channel_id=1, source_target_pairs={{0,128},{64,192},{128,0},{192,64},{1,129},{65,193},{129,1},{193,65... | collective-permute-start | bytes 1572872 | tf_op jit(solution)/shard_map/ppermute | solution.py:25
  25.1 23.6 %collective-permute-start.5 = (bf16[256,1024]{1,0:T(8,128)(2,1)S(1)}, bf16[256,1024]{1,0:T(8,128)(2,1)S(1)}, u32[]{:S(2)}, u32[]{:S(2)}) collective-permute-start(bf16[256,1024]{1,0:T(8,128)(2,1)S(1)} %get-tuple-element.14), channel_id=1, source_target_pairs={{0,192},{64,0},{128,64},{192,128},{1,193},{65,1},{129,65},{193,129... | collective-permute-start | bytes 1572872 | tf_op jit(solution)/shard_map/ppermute | solution.py:25
  36.5 15.8 %copy-start.5 = (bf16[256,1024]{1,0:T(8,128)(2,1)}, bf16[256,1024]{1,0:T(8,128)(2,1)S(1)}, u32[]{:S(2)}) copy-start(bf16[256,1024]{1,0:T(8,128)(2,1)S(1)} %collective-permute-done.3) | copy-start | bytes 1572868
  48.7 3.4 %copy-start.7 = (bf16[256,1024]{1,0:T(8,128)(2,1)}, bf16[256,1024]{1,0:T(8,128)(2,1)S(1)}, u32[]{:S(2)}) copy-start(bf16[256,1024]{1,0:T(8,128)(2,1)S(1)} %collective-permute-done.5) | copy-start | bytes 1572868
  50.0 59.2 %collective-permute-start.6 = (bf16[3,256,1024]{2,1,0:T(8,128)(2,1)}, bf16[3,256,1024]{2,1,0:T(8,128)(2,1)}, u32[]{:S(2)}, u32[]{:S(2)}) collective-permute-start(bf16[3,256,1024]{2,1,0:T(8,128)(2,1)} %pad_maximum_fusion), channel_id=1, source_target_pairs={{0,1},{1,0},{2,3},{3,2},{4,5},{5,4},{6,7},{7,6},{8,9},{9,8},{10,11... | collective-permute-start | bytes 4718600 | tf_op jit(solution)/shard_map/ppermute | solution.py:25
  52.9 4.6 %copy-start.3 = (bf16[512,128]{1,0:T(8,128)(2,1)S(1)}, bf16[512,128]{1,0:T(8,128)(2,1)}, u32[]{:S(2)}) copy-start(bf16[512,128]{1,0:T(8,128)(2,1)} %param.8) | copy-start | bytes 393220
  53.0 4.6 %copy-start.4 = (bf16[512,128]{1,0:T(8,128)(2,1)S(1)}, bf16[512,128]{1,0:T(8,128)(2,1)}, u32[]{:S(2)}) copy-start(bf16[512,128]{1,0:T(8,128)(2,1)} %param.7) | copy-start | bytes 393220
  56.6 5.5 %copy-start.1 = (bf16[512,4,128]{2,0,1:T(8,128)(2,1)}, bf16[512,4,128]{2,0,1:T(8,128)(2,1)S(1)}, u32[]{:S(2)}) copy-start(bf16[512,4,128]{2,0,1:T(8,128)(2,1)S(1)} %copy.18) | copy-start | bytes 1572868
  106.5 4.2 %copy-start.2 = (bf16[512,512]{1,0:T(8,128)(2,1)S(1)}, bf16[512,512]{1,0:T(8,128)(2,1)}, u32[]{:S(2)}) copy-start(bf16[512,512]{1,0:T(8,128)(2,1)} %shard_map.64) | copy-start | bytes 1572868
  106.5 14.7 %collective-permute-start.2 = (bf16[512,512]{1,0:T(8,128)(2,1)}, bf16[512,512]{1,0:T(8,128)(2,1)S(1)}, u32[]{:S(2)}, u32[]{:S(2)}) collective-permute-start(bf16[512,512]{1,0:T(8,128)(2,1)} %shard_map.64), channel_id=1, source_target_pairs={{0,64},{64,128},{128,192},{192,0},{1,65},{65,129},{129,193},{193,1... | collective-permute-start | bytes 1572872 | tf_op jit(solution)/shard_map/ppermute | solution.py:25
  107.7 13.8 %collective-permute-start.7 = (bf16[512,512]{1,0:T(8,128)(2,1)}, bf16[512,512]{1,0:T(8,128)(2,1)S(1)}, u32[]{:S(2)}, u32[]{:S(2)}) collective-permute-start(bf16[512,512]{1,0:T(8,128)(2,1)} %shard_map.64), channel_id=1, source_target_pairs={{0,192},{64,0},{128,64},{192,128},{1,193},{65,1},{129,65},{193,129... | collective-permute-start | bytes 1572872 | tf_op jit(solution)/shard_map/ppermute | solution.py:25
  110.7 13.6 %copy-start.6 = (bf16[256,1024]{1,0:T(8,128)(2,1)S(1)}, bf16[256,1024]{1,0:T(8,128)(2,1)}, u32[]{:S(2)}) copy-start(bf16[256,1024]{1,0:T(8,128)(2,1)} %copy-done.5) | copy-start | bytes 1572868
  121.2 8.2 %collective-permute-start.8 = (bf16[512,256]{1,0:T(8,128)(2,1)S(1)}, bf16[512,256]{1,0:T(8,128)(2,1)S(1)}, u32[]{:S(2)}, u32[]{:S(2)}) collective-permute-start(bf16[512,256]{1,0:T(8,128)(2,1)S(1)} %slice.32), channel_id=1, source_target_pairs={{0,64},{64,128},{128,192},{192,0},{1,65},{65,129},{129,193},{193,1... | collective-permute-start | bytes 786440 | tf_op jit(solution)/shard_map/ppermute | solution.py:25
  121.5 7.9 %collective-permute-start.9 = (bf16[512,256]{1,0:T(8,128)(2,1)S(1)}, bf16[512,256]{1,0:T(8,128)(2,1)S(1)}, u32[]{:S(2)}, u32[]{:S(2)}) collective-permute-start(bf16[512,256]{1,0:T(8,128)(2,1)S(1)} %slice.33), channel_id=1, source_target_pairs={{0,192},{64,0},{128,64},{192,128},{1,193},{65,1},{129,65},{193,129... | collective-permute-start | bytes 786440 | tf_op jit(solution)/shard_map/ppermute | solution.py:25
  124.3 1.0 copy-start.8
Sparse Core Ops, SparseCore 0:
  10.9 83.2 all-gather.1

commit v9 on v8

--- a/solution.py
+++ b/solution.py
@@ -29,7 +29,7 @@
     return jnp.repeat(jnp.repeat(table, rows, axis=-2), cols, axis=-1)
 
 
-def vertical_kernel(slots_ref, q_ref, kv_hbm, key_tok_ref, query_tok_ref, top_ref, tot_ref, acc_ref,
+def vertical_kernel(slots_ref, q_ref, kv_hbm, key_tok_ref, query_tok_ref, acc_ref,
                     o_ref, k_buf, v_buf, sems, *, scale):
     head = pl.program_id(0)
     heads = pl.num_programs(0)
@@ -67,16 +67,19 @@
         q_ref[0], k_buf[current], (((1,), (1,)), ((), ())), preferred_element_type=jnp.float32
     ) * scale
     s = jnp.where(key_tok_ref[0] <= query_tok_ref[...], s, -jnp.inf)
-    top_d = top_ref[0]
+    dim = q_ref.shape[-1]
+    top_d = acc_ref[0, :, dim:dim + 1]
     top = jnp.maximum(top_d, jnp.max(s, axis=1, keepdims=True))
     p = jnp.exp(s - top)
     sc = jnp.exp(top_d - top)
-    total = tot_ref[0] * sc + jnp.sum(p, axis=1, keepdims=True)
+    total = acc_ref[0, :, dim + 1:dim + 2] * sc + jnp.sum(p, axis=1, keepdims=True)
     acc = jnp.dot(p.astype(jnp.bfloat16), v_buf[current], preferred_element_type=jnp.float32)
-    o_ref[...] = ((acc_ref[0] * sc + acc) / total).astype(o_ref.dtype)
+    o_ref[...] = ((acc_ref[0, :, :dim] * sc + acc) / total).astype(o_ref.dtype)
 
 
 def vertical_attention(slots, q, kv, key_tok, query_tok, top_d, tot_d, acc_d, interpret=False):
+    spare = jnp.zeros(acc_d.shape[:-1] + (acc_d.shape[-1] - 2,), acc_d.dtype)
+    acc_d = jnp.concatenate([acc_d, top_d, tot_d, spare], axis=-1)
     heads, rows, dim = q.shape
     keys_n = key_tok.shape[-1]
     kernel = functools.partial(vertical_kernel, scale=1.0 / math.sqrt(dim))
@@ -88,9 +91,7 @@
             pl.BlockSpec(memory_space=pl.ANY),
             pl.BlockSpec((1, 1, keys_n), lambda i, t: (i, 0, 0)),
             pl.BlockSpec((rows, 1), lambda i, t: (0, 0)),
-            pl.BlockSpec((1, rows, 1), lambda i, t: (i, 0, 0)),
-            pl.BlockSpec((1, rows, 1), lambda i, t: (i, 0, 0)),
-            pl.BlockSpec((1, rows, dim), lambda i, t: (i, 0, 0)),
+            pl.BlockSpec((1, rows, 2 * dim), lambda i, t: (i, 0, 0)),
         ],
         out_specs=pl.BlockSpec((rows, dim), lambda i, t: (0, i)),
         scratch_shapes=[
@@ -104,7 +105,7 @@
         grid_spec=grid_spec,
         out_shape=jax.ShapeDtypeStruct((rows, heads * dim), jnp.bfloat16),
         interpret=interpret,
-    )(slots, q, kv, key_tok, query_tok, top_d, tot_d, acc_d)
+    )(slots, q, kv, key_tok, query_tok, acc_d)
 
 
 def make_local(sizes):

time: 139 us -> 139 us (level)
  local copies, waits for them, and re-layouts: 11.9 us -> 10 us
  other arithmetic: 14.9 us -> 16.6 us
    concatenate x0 -> x1, other arithmetic: none -> 1.71 us  [vertical_attention(): acc_d = jnp.concatenate([acc_d, top_d, tot_d, spare], axis=-1)]
  transfers between devices with their start and end apart: 11 -> 11, of which waited for: 5 -> 5; matrix products, arithmetic and copies ran while one was open for 26% -> 25% of each run, Pallas kernels for 9% -> 9%
where the time goes in v9:
time: 139 us; the launch traced here: 138 us
  waiting for transfers between devices  51.8 us (37%)
  starting transfers between devices  19.2 us (14%)
  other arithmetic  16.6 us (12%)
  between operations  14.4 us (10%)
  matrix products  13.6 us (10%)
  Pallas kernels  12.4 us (9%)
  local copies, waits for them, and re-layouts  10 us (7%)
    ppermute x8, waiting for transfers between devices, ring(): lax.ppermute(block, axis, [(i, (i + distance) % size) for i in range(size)])  32.7 us
    all_gather x1, waiting for transfers between devices, local(): arrived = lax.all_gather(outgoing, SEQ, axis=1, tiled=True)  19.1 us
    pallas_call x1, Pallas kernels, vertical_attention(): pl.pallas_call(kernel, grid_spec=grid_spec, out_shape=jax.ShapeDtypeStruc...  12.4 us
    ppermute x8, starting transfers between devices, ring(): lax.ppermute(block, axis, [(i, (i + distance) % size) for i in range(size)])  11.1 us
    ppermute x2, starting transfers between devices, shift(): return lax.ppermute(block, axis, route)  8.08 us
    convert_element_type x1, other arithmetic, local(): expo_diag.astype(jnp.bfloat16)  5.59 us
    dot_general x1, matrix products, local(): jnp.einsum('htu,ud->htd', expo_diag.astype(jnp.bfloat16), context_v, pref...  4.8 us
    dot_general x1, matrix products, local(): jnp.einsum('htd,ud->htu', query_heads, context_k, preferred_element_type=...  3.44 us
  transfers between devices with their start and end apart: 11, of which 5 were waited for; matrix products, arithmetic and copies ran while one was open for 25% of the time, Pallas kernels for 9%

profile of v9, /device:TPU:1, one launch (start us, length us, event | category | flops | bytes accessed | tf_op | source)
XLA Modules:
  0.0 138.0 jit_solution(1638606895258051294)
XLA Ops:
  6.5 0.7 broadcast_multiply_fusion
  7.2 0.1 reshape.360
  7.4 0.1 fusion.35
  7.5 0.6 convert_reduce_fusion.2
  8.1 0.1 convert_reduce_fusion.1
  8.9 1.0 bitcast_convert_fusion
  9.9 0.1 select_reduce_fusion.1
  10.1 0.6 pad_maximum_fusion.2
  10.8 1.0 pad_maximum_fusion.1
  11.8 4.7 %collective-permute-start = (bf16[2,8,64,128]{3,2,1,0:T(8,128)(2,1)S(1)}, bf16[2,8,64,128]{3,2,1,0:T(8,128)(2,1)}, u32[]{:S(2)}, u32[]{:S(2)}) collective-permute-start(bf16[2,8,64,128]{3,2,1,0:T(8,128)(2,1)S(1)} %pad_maximum_fusion.1), channel_id=1, source_target_pairs={{0,2},{1,3},{2,4},{3,5},{4,6},{5,7},{6,8},{7,9},{8,10},{9,11},{10,... | collective-permute-start | bytes 786440 | tf_op jit(solution)/shard_map/ppermute | solution.py:21
  16.5 3.3 %collective-permute-start.1 = (bf16[2,8,64,128]{3,2,1,0:T(8,128)(2,1)S(1)}, bf16[2,8,64,128]{3,2,1,0:T(8,128)(2,1)}, u32[]{:S(2)}, u32[]{:S(2)}) collective-permute-start(bf16[2,8,64,128]{3,2,1,0:T(8,128)(2,1)S(1)} %pad_maximum_fusion.1), channel_id=1, source_target_pairs={{0,1},{1,2},{2,3},{3,4},{4,5},{5,6},{6,7},{7,8},{8,9},{9,10},{10,1... | collective-permute-start | bytes 786440 | tf_op jit(solution)/shard_map/ppermute | solution.py:21
  19.9 1.5 %fusion.47 = (bf16[256,1024]{1,0:T(8,128)(2,1)S(1)}, bf16[256,1024]{1,0:T(8,128)(2,1)S(1)}, bf16[256,1024]{1,0:T(8,128)(2,1)S(1)}) fusion(bf16[512,4096]{1,0:T(8,128)(2,1)} %param.11, s32[]{:T(128)S(6)} %select_n.105, s32[]{:T(128)S(6)} %select_n.107, s32[]{:T(128)S(6)} %select_n.111, s32[]{:T(128)S(6)} %select_n.109), kind=kLoop, calls=%fused_computation.100 | loop fusion | bytes 3145744 | tf_op jit(solution)/shard_map/dynamic_slice | solution.py:165
  21.4 1.3 collective-permute-start.3
  22.7 2.5 %collective-permute-start.4 = (bf16[256,1024]{1,0:T(8,128)(2,1)S(1)}, bf16[256,1024]{1,0:T(8,128)(2,1)S(1)}, u32[]{:S(2)}, u32[]{:S(2)}) collective-permute-start(bf16[256,1024]{1,0:T(8,128)(2,1)S(1)} %get-tuple-element.15), channel_id=1, source_target_pairs={{0,128},{64,192},{128,0},{192,64},{1,129},{65,193},{129,1},{193,65... | collective-permute-start | bytes 1572872 | tf_op jit(solution)/shard_map/ppermute | solution.py:25
  25.1 1.2 collective-permute-start.5
  26.3 0.1 constant_dynamic-slice_fusion
  26.3 0.1 copy.23
  26.4 0.1 compare_reduce_fusion.1
  26.5 0.2 convert_reduce_fusion
  26.7 0.1 reduce_sum.57
  26.8 0.1 broadcast_subtract_fusion
  26.9 0.1 compare_reduce_fusion
  27.0 0.1 subtract_compare_fusion.1
  27.1 0.5 fusion.39.slots_ref
  27.6 8.8 %collective-permute-done.3 = bf16[256,1024]{1,0:T(8,128)(2,1)S(1)} collective-permute-done((bf16[256,1024]{1,0:T(8,128)(2,1)S(1)}, bf16[256,1024]{1,0:T(8,128)(2,1)S(1)}, u32[]{:S(2)}, u32[]{:S(2)}) %collective-permute-start.3) | collective-permute-done | bytes 524320 | tf_op jit(solution)/shard_map/ppermute | solution.py:25
  36.5 12.2 %collective-permute-done.4 = bf16[256,1024]{1,0:T(8,128)(2,1)S(1)} collective-permute-done((bf16[256,1024]{1,0:T(8,128)(2,1)S(1)}, bf16[256,1024]{1,0:T(8,128)(2,1)S(1)}, u32[]{:S(2)}, u32[]{:S(2)}) %collective-permute-start.4) | collective-permute-done | bytes 524320 | tf_op jit(solution)/shard_map/ppermute | solution.py:25
  48.7 1.3 pad_maximum_fusion
  50.0 0.5 collective-permute-start.6
  50.6 0.8 iota_add_fusion.query_tok_ref
  51.3 0.1 copy.24
  51.4 0.2 broadcast_in_dim.88
  51.6 0.2 reshape.363
  51.8 0.1 copy.25
  51.9 0.2 broadcast_in_dim.90
  52.1 0.2 reshape.365
  52.3 0.7 tile.2
  53.0 2.1 %and.167 = pred[512,1536]{0,1:T(8,128)(4,1)S(1)} reshape(pred[8,64,24,64]{1,0,3,2:T(8,128)(4,1)S(1)} %tile.2) | data formatting | bytes 1572864 | tf_op jit(solution)/shard_map/and | solution.py:197
  55.1 1.3 copy.21
  56.4 0.3 copy.22
  56.7 0.1 add.155
  56.7 0.1 add.156
  56.9 0.1 pad.20.clone
  57.0 0.6 broadcast_add_fusion.key_tok_ref
  57.6 1.1 maximum_maximum_fusion.1
  58.8 3.4 %fusion = (f32[4,512]{1,0:T(4,128)S(1)}, f32[1536,4,512]{2,0,1:T(8,128)S(1)}) fusion(pred[512,1536]{0,1:T(8,128)(4,1)S(1)} %and.167, pred[4,512,24]{1,2,0:T(8,128)(4,1)S(1)} %reshape.365, pred[4,512,24]{1,2,0:T(8,128)(4,1)S(1)} %reshape.363, bf16[1536,128,1]{1,0,2:T(8,128)(2,1)S(1)} %bitcast.96, bf16[512,4,128]{2,0,1:T(8,128)(2,1)S(1)} %copy.22), kind=kOutput, calls=%fused_computation.2 | convolution fusion | flops 821032960 | bytes 14393344 | tf_op jit(solution)/shard_map/htd,ud->htu/dot_general | solution.py:189
  62.3 5.6 %fusion.5 = (bf16[4,512,1536]{1,2,0:T(8,128)(2,1)}, f32[4,512]{1,0:T(4,128)S(1)}) fusion(f32[1536,4,512]{2,0,1:T(8,128)S(1)} %get-tuple-element.28, f32[4,512]{1,0:T(4,128)S(1)} %get-tuple-element.27, pred[512,1536]{0,1:T(8,128)(4,1)S(1)} %and.167, pred[4,512,24]{1,2,0:T(8,128)(4,1)S(1)} %reshape.365, pred[4,512,24]{1,2,0:T(8,128)(4,1)S(1)} %reshape.363), kind=kLoop, calls=%fused_computation.8 | loop fusion | flops 22018048 | bytes 19775488 | tf_op jit(solution)/shard_map/convert_element_type | solution.py:205
  67.8 0.4 copy.30
  68.2 0.4 copy.29
  68.6 4.8 %fusion.49 = f32[4,512,128]{2,1,0:T(8,128)S(1)} fusion(bf16[4,512,1536]{1,2,0:T(8,128)(2,1)} %get-tuple-element.11, bf16[1536,128,1]{1,0,2:T(8,128)(2,1)S(1)} %bitcast.95), kind=kOutput, calls=%fused_computation.102 | convolution fusion | flops 805306368 | bytes 7733248 | tf_op jit(solution)/shard_map/htu,ud->htd/dot_general | solution.py:203
  73.4 1.7 %maximum_maximum_fusion.acc_ref = f32[4,512,256]{2,1,0:T(8,128)} fusion(f32[4,512,1]{2,1,0:T(8,128)S(1)} %copy.30, f32[4,512,1]{2,1,0:T(8,128)S(1)} %copy.29, f32[4,512,128]{2,1,0:T(8,128)S(1)} %fusion.49, f32[256]{0:T(256)S(1)} %pad.20.clone), kind=kLoop, calls=%fused_computation.9 | loop fusion | flops 1572864 | bytes 3163136 | tf_op jit(solution)/shard_map/concatenate | solution.py:82
  75.1 19.1 %all-gather.2.cloned.1.call-done = bf16[2,8192,128]{2,1,0:T(8,128)(2,1)} async-done(((bf16[2,128,128]{2,1,0:T(8,128)(2,1)}), bf16[2,8192,128]{2,1,0:T(8,128)(2,1)}) %all-gather.2.cloned.1.call-update) | async-done | bytes 4194320 | tf_op jit(solution)/shard_map/all_gather | solution.py:157
  94.2 12.4 %shard_map.64 = bf16[512,512]{1,0:T(8,128)(2,1)} custom-call(s32[4,16]{1,0:T(4,128)} %fusion.39.slots_ref, bf16[4,512,128]{2,1,0:T(8,128)(2,1)} %bitcast.91, bf16[2,128,64,128]{3,2,1,0:T(8,128)(2,1)} %bitcast.92, s32[4,1,1024]{2,1,0:T(1,128)} %broadcast_add_fusion.key_tok_ref, s32[512,1]{1,0:T(8,128)} %iota_add_fusion.query_tok_ref, ...), custom_call_target="tpu_custom_call" | custom-call | tf_op jit(solution)/shard_map/pallas_call | solution.py:103
  106.6 1.3 collective-permute-start.2
  107.9 1.5 %collective-permute-start.7 = (bf16[512,512]{1,0:T(8,128)(2,1)}, bf16[512,512]{1,0:T(8,128)(2,1)S(1)}, u32[]{:S(2)}, u32[]{:S(2)}) collective-permute-start(bf16[512,512]{1,0:T(8,128)(2,1)} %shard_map.64), channel_id=1, source_target_pairs={{0,192},{64,0},{128,64},{192,128},{1,193},{65,1},{129,65},{193,129... | collective-permute-start | bytes 1572872 | tf_op jit(solution)/shard_map/ppermute | solution.py:25
  109.4 1.5 %slice_bitcast_fusion = (bf16[256,1024]{1,0:T(8,128)(2,1)S(1)}, bf16[256,1024]{1,0:T(8,128)(2,1)S(1)}, bf16[256,1024]{1,0:T(8,128)(2,1)S(1)}) fusion(bf16[3,256,1024]{2,1,0:T(8,128)(2,1)} %collective-permute-done.6), kind=kLoop, calls=%fused_computation.39 | loop fusion | bytes 3145728 | tf_op jit(solution)/shard_map/squeeze | solution.py:227
  110.9 2.0 %fusion.24 = f32[512,1024]{1,0:T(8,128)S(1)} fusion(bf16[512,512]{1,0:T(8,128)(2,1)S(1)} %copy-done.2, bf16[512,4096]{1,0:T(8,128)(2,1)} %param.11, s32[]{:T(128)S(6)} %select_n.103), kind=kOutput, calls=%fused_computation.33 | convolution fusion | flops 536870912 | bytes 3670020 | tf_op jit(solution)/shard_map/dot_general | solution.py:237
  112.9 8.4 %collective-permute-done.2 = bf16[512,512]{1,0:T(8,128)(2,1)S(1)} collective-permute-done((bf16[512,512]{1,0:T(8,128)(2,1)}, bf16[512,512]{1,0:T(8,128)(2,1)S(1)}, u32[]{:S(2)}, u32[]{:S(2)}) %collective-permute-start.2) | collective-permute-done | bytes 524320 | tf_op jit(solution)/shard_map/ppermute | solution.py:25
  121.3 0.1 collective-permute-start.8
  121.5 2.7 %collective-permute-start.9 = (bf16[512,256]{1,0:T(8,128)(2,1)S(1)}, bf16[512,256]{1,0:T(8,128)(2,1)S(1)}, u32[]{:S(2)}, u32[]{:S(2)}) collective-permute-start(bf16[512,256]{1,0:T(8,128)(2,1)S(1)} %slice.33), channel_id=1, source_target_pairs={{0,192},{64,0},{128,64},{192,128},{1,193},{65,1},{129,65},{193,129... | collective-permute-start | bytes 786440 | tf_op jit(solution)/shard_map/ppermute | solution.py:25
  124.2 0.7 fusion.6
  124.9 0.3 copy-done.8
  125.2 0.7 fusion.12
  126.0 3.3 %collective-permute-done.8 = bf16[512,256]{1,0:T(8,128)(2,1)S(1)} collective-permute-done((bf16[512,256]{1,0:T(8,128)(2,1)S(1)}, bf16[512,256]{1,0:T(8,128)(2,1)S(1)}, u32[]{:S(2)}, u32[]{:S(2)}) %collective-permute-start.8) | collective-permute-done | bytes 262176 | tf_op jit(solution)/shard_map/ppermute | solution.py:25
  129.3 1.8 %add_convert_fusion = bf16[512,1024]{1,0:T(8,128)(2,1)} fusion(f32[512,1024]{1,0:T(8,128)S(1)} %fusion.12, f32[512,1024]{1,0:T(8,128)S(1)} %fusion.24, f32[512,1024]{1,0:T(8,128)S(1)} %fusion.6, bf16[256,1024]{1,0:T(8,128)(2,1)S(1)} %get-tuple-element.16, bf16[256,1024]{1,0:T(8,128)(2,1)S(1)} %collective-permute-done.4, pred[]{:T(512)S(6)} %eq.123, ...), kind=kOutput, calls=%fused_computation.10 | convolution fusion | flops 544735232 | bytes 8912897 | tf_op jit(solution)/shard_map/dot_general | solution.py:243
  (41 shorter events, 0.3 us)
Async XLA Ops:
  6.5 19.7 %copy-start = (s32[16,8]{0,1:T(8,128)S(1)}, s32[16,8]{0,1:T(8,128)}, u32[]{:S(2)}) copy-start(s32[16,8]{0,1:T(8,128)} %param.10) | copy-start | bytes 1540
  6.5 87.6 %all-gather.2.cloned.1.call-start = ((), (), s32[]{:S(2)}) async-start(), calls=%async_computation | async-start | bytes 4259840 | tf_op jit(solution)/shard_map/all_gather | solution.py:157
  11.8 45.9 %collective-permute-start = (bf16[2,8,64,128]{3,2,1,0:T(8,128)(2,1)S(1)}, bf16[2,8,64,128]{3,2,1,0:T(8,128)(2,1)}, u32[]{:S(2)}, u32[]{:S(2)}) collective-permute-start(bf16[2,8,64,128]{3,2,1,0:T(8,128)(2,1)S(1)} %pad_maximum_fusion.1), channel_id=1, source_target_pairs={{0,2},{1,3},{2,4},{3,5},{4,6},{5,7},{6,8},{7,9},{8,10},{9,11},{10,... | collective-permute-start | bytes 786440 | tf_op jit(solution)/shard_map/ppermute | solution.py:21
  16.5 41.1 %collective-permute-start.1 = (bf16[2,8,64,128]{3,2,1,0:T(8,128)(2,1)S(1)}, bf16[2,8,64,128]{3,2,1,0:T(8,128)(2,1)}, u32[]{:S(2)}, u32[]{:S(2)}) collective-permute-start(bf16[2,8,64,128]{3,2,1,0:T(8,128)(2,1)S(1)} %pad_maximum_fusion.1), channel_id=1, source_target_pairs={{0,1},{1,2},{2,3},{3,4},{4,5},{5,6},{6,7},{7,8},{8,9},{9,10},{10,1... | collective-permute-start | bytes 786440 | tf_op jit(solution)/shard_map/ppermute | solution.py:21
  21.4 15.1 %collective-permute-start.3 = (bf16[256,1024]{1,0:T(8,128)(2,1)S(1)}, bf16[256,1024]{1,0:T(8,128)(2,1)S(1)}, u32[]{:S(2)}, u32[]{:S(2)}) collective-permute-start(bf16[256,1024]{1,0:T(8,128)(2,1)S(1)} %get-tuple-element.13), channel_id=1, source_target_pairs={{0,64},{64,128},{128,192},{192,0},{1,65},{65,129},{129,193},{193,1... | collective-permute-start | bytes 1572872 | tf_op jit(solution)/shard_map/ppermute | solution.py:25
  22.7 26.0 %collective-permute-start.4 = (bf16[256,1024]{1,0:T(8,128)(2,1)S(1)}, bf16[256,1024]{1,0:T(8,128)(2,1)S(1)}, u32[]{:S(2)}, u32[]{:S(2)}) collective-permute-start(bf16[256,1024]{1,0:T(8,128)(2,1)S(1)} %get-tuple-element.15), channel_id=1, source_target_pairs={{0,128},{64,192},{128,0},{192,64},{1,129},{65,193},{129,1},{193,65... | collective-permute-start | bytes 1572872 | tf_op jit(solution)/shard_map/ppermute | solution.py:25
  25.1 23.6 %collective-permute-start.5 = (bf16[256,1024]{1,0:T(8,128)(2,1)S(1)}, bf16[256,1024]{1,0:T(8,128)(2,1)S(1)}, u32[]{:S(2)}, u32[]{:S(2)}) collective-permute-start(bf16[256,1024]{1,0:T(8,128)(2,1)S(1)} %get-tuple-element.14), channel_id=1, source_target_pairs={{0,192},{64,0},{128,64},{192,128},{1,193},{65,1},{129,65},{193,129... | collective-permute-start | bytes 1572872 | tf_op jit(solution)/shard_map/ppermute | solution.py:25
  36.5 15.8 %copy-start.5 = (bf16[256,1024]{1,0:T(8,128)(2,1)}, bf16[256,1024]{1,0:T(8,128)(2,1)S(1)}, u32[]{:S(2)}) copy-start(bf16[256,1024]{1,0:T(8,128)(2,1)S(1)} %collective-permute-done.3) | copy-start | bytes 1572868
  48.7 3.4 %copy-start.7 = (bf16[256,1024]{1,0:T(8,128)(2,1)}, bf16[256,1024]{1,0:T(8,128)(2,1)S(1)}, u32[]{:S(2)}) copy-start(bf16[256,1024]{1,0:T(8,128)(2,1)S(1)} %collective-permute-done.5) | copy-start | bytes 1572868
  50.0 59.4 %collective-permute-start.6 = (bf16[3,256,1024]{2,1,0:T(8,128)(2,1)}, bf16[3,256,1024]{2,1,0:T(8,128)(2,1)}, u32[]{:S(2)}, u32[]{:S(2)}) collective-permute-start(bf16[3,256,1024]{2,1,0:T(8,128)(2,1)} %pad_maximum_fusion), channel_id=1, source_target_pairs={{0,1},{1,0},{2,3},{3,2},{4,5},{5,4},{6,7},{7,6},{8,9},{9,8},{10,11... | collective-permute-start | bytes 4718600 | tf_op jit(solution)/shard_map/ppermute | solution.py:25
  53.0 4.6 %copy-start.3 = (bf16[512,128]{1,0:T(8,128)(2,1)S(1)}, bf16[512,128]{1,0:T(8,128)(2,1)}, u32[]{:S(2)}) copy-start(bf16[512,128]{1,0:T(8,128)(2,1)} %param.8) | copy-start | bytes 393220
  53.0 4.6 %copy-start.4 = (bf16[512,128]{1,0:T(8,128)(2,1)S(1)}, bf16[512,128]{1,0:T(8,128)(2,1)}, u32[]{:S(2)}) copy-start(bf16[512,128]{1,0:T(8,128)(2,1)} %param.7) | copy-start | bytes 393220
  56.7 5.6 %copy-start.1 = (bf16[512,4,128]{2,0,1:T(8,128)(2,1)}, bf16[512,4,128]{2,0,1:T(8,128)(2,1)S(1)}, u32[]{:S(2)}) copy-start(bf16[512,4,128]{2,0,1:T(8,128)(2,1)S(1)} %copy.22) | copy-start | bytes 1572868
  106.6 4.3 %copy-start.2 = (bf16[512,512]{1,0:T(8,128)(2,1)S(1)}, bf16[512,512]{1,0:T(8,128)(2,1)}, u32[]{:S(2)}) copy-start(bf16[512,512]{1,0:T(8,128)(2,1)} %shard_map.64) | copy-start | bytes 1572868
  106.6 14.7 %collective-permute-start.2 = (bf16[512,512]{1,0:T(8,128)(2,1)}, bf16[512,512]{1,0:T(8,128)(2,1)S(1)}, u32[]{:S(2)}, u32[]{:S(2)}) collective-permute-start(bf16[512,512]{1,0:T(8,128)(2,1)} %shard_map.64), channel_id=1, source_target_pairs={{0,64},{64,128},{128,192},{192,0},{1,65},{65,129},{129,193},{193,1... | collective-permute-start | bytes 1572872 | tf_op jit(solution)/shard_map/ppermute | solution.py:25
  107.9 13.5 %collective-permute-start.7 = (bf16[512,512]{1,0:T(8,128)(2,1)}, bf16[512,512]{1,0:T(8,128)(2,1)S(1)}, u32[]{:S(2)}, u32[]{:S(2)}) collective-permute-start(bf16[512,512]{1,0:T(8,128)(2,1)} %shard_map.64), channel_id=1, source_target_pairs={{0,192},{64,0},{128,64},{192,128},{1,193},{65,1},{129,65},{193,129... | collective-permute-start | bytes 1572872 | tf_op jit(solution)/shard_map/ppermute | solution.py:25
  110.9 13.3 %copy-start.6 = (bf16[256,1024]{1,0:T(8,128)(2,1)S(1)}, bf16[256,1024]{1,0:T(8,128)(2,1)}, u32[]{:S(2)}) copy-start(bf16[256,1024]{1,0:T(8,128)(2,1)} %copy-done.5) | copy-start | bytes 1572868
  121.3 8.0 %collective-permute-start.8 = (bf16[512,256]{1,0:T(8,128)(2,1)S(1)}, bf16[512,256]{1,0:T(8,128)(2,1)S(1)}, u32[]{:S(2)}, u32[]{:S(2)}) collective-permute-start(bf16[512,256]{1,0:T(8,128)(2,1)S(1)} %slice.32), channel_id=1, source_target_pairs={{0,64},{64,128},{128,192},{192,0},{1,65},{65,129},{129,193},{193,1... | collective-permute-start | bytes 786440 | tf_op jit(solution)/shard_map/ppermute | solution.py:25
  121.5 7.8 %collective-permute-start.9 = (bf16[512,256]{1,0:T(8,128)(2,1)S(1)}, bf16[512,256]{1,0:T(8,128)(2,1)S(1)}, u32[]{:S(2)}, u32[]{:S(2)}) collective-permute-start(bf16[512,256]{1,0:T(8,128)(2,1)S(1)} %slice.33), channel_id=1, source_target_pairs={{0,192},{64,0},{128,64},{192,128},{1,193},{65,1},{129,65},{193,129... | collective-permute-start | bytes 786440 | tf_op jit(solution)/shard_map/ppermute | solution.py:25
  124.2 1.0 copy-start.8
Sparse Core Ops, SparseCore 0:
  10.9 83.2 all-gather.1

commit v10 on v9

--- a/solution.py
+++ b/solution.py
@@ -29,7 +29,7 @@
     return jnp.repeat(jnp.repeat(table, rows, axis=-2), cols, axis=-1)
 
 
-def vertical_kernel(slots_ref, q_ref, kv_hbm, key_tok_ref, query_tok_ref, acc_ref,
+def vertical_kernel(slots_ref, first_ref, q_ref, kv_hbm, key_tok_ref, acc_ref,
                     o_ref, k_buf, v_buf, sems, *, scale):
     head = pl.program_id(0)
     heads = pl.num_programs(0)
@@ -66,7 +66,8 @@
     s = lax.dot_general(
         q_ref[0], k_buf[current], (((1,), (1,)), ((), ())), preferred_element_type=jnp.float32
     ) * scale
-    s = jnp.where(key_tok_ref[0] <= query_tok_ref[...], s, -jnp.inf)
+    query_tok = first_ref[0] + lax.broadcasted_iota(jnp.int32, (s.shape[0], 1), 0)
+    s = jnp.where(key_tok_ref[0] <= query_tok, s, -jnp.inf)
     dim = q_ref.shape[-1]
     top_d = acc_ref[0, :, dim:dim + 1]
     top = jnp.maximum(top_d, jnp.max(s, axis=1, keepdims=True))
@@ -84,16 +85,15 @@
     keys_n = key_tok.shape[-1]
     kernel = functools.partial(vertical_kernel, scale=1.0 / math.sqrt(dim))
     grid_spec = pltpu.PrefetchScalarGridSpec(
-        num_scalar_prefetch=1,
+        num_scalar_prefetch=2,
         grid=(heads,),
         in_specs=[
-            pl.BlockSpec((1, rows, dim), lambda i, t: (i, 0, 0)),
+            pl.BlockSpec((1, rows, dim), lambda i, t, f: (i, 0, 0)),
             pl.BlockSpec(memory_space=pl.ANY),
-            pl.BlockSpec((1, 1, keys_n), lambda i, t: (i, 0, 0)),
-            pl.BlockSpec((rows, 1), lambda i, t: (0, 0)),
-            pl.BlockSpec((1, rows, 2 * dim), lambda i, t: (i, 0, 0)),
+            pl.BlockSpec((1, 1, keys_n), lambda i, t, f: (i, 0, 0)),
+            pl.BlockSpec((1, rows, 2 * dim), lambda i, t, f: (i, 0, 0)),
         ],
-        out_specs=pl.BlockSpec((rows, dim), lambda i, t: (0, i)),
+        out_specs=pl.BlockSpec((rows, dim), lambda i, t, f: (0, i)),
         scratch_shapes=[
             pltpu.VMEM((2, keys_n, dim), kv.dtype),
             pltpu.VMEM((2, keys_n, dim), kv.dtype),
@@ -105,7 +105,7 @@
         grid_spec=grid_spec,
         out_shape=jax.ShapeDtypeStruct((rows, heads * dim), jnp.bfloat16),
         interpret=interpret,
-    )(slots, q, kv, key_tok, query_tok, acc_d)
+    )(slots, query_tok[:1, 0], q, kv, key_tok, acc_d)
 
 
 def make_local(sizes):

time: 139 us -> 140 us (level)
  no operation moved by 1% of the time
where the time goes in v10:
time: 140 us; the launch traced here: 139 us
  waiting for transfers between devices  52 us (37%)
  starting transfers between devices  19.1 us (14%)
  other arithmetic  15.9 us (11%)
  between operations  14.4 us (10%)
  matrix products  13.6 us (10%)
  Pallas kernels  12.9 us (9%)
  local copies, waits for them, and re-layouts  10.5 us (8%)
    ppermute x8, waiting for transfers between devices, ring(): lax.ppermute(block, axis, [(i, (i + distance) % size) for i in range(size)])  32.7 us
    all_gather x1, waiting for transfers between devices, local(): arrived = lax.all_gather(outgoing, SEQ, axis=1, tiled=True)  19.2 us
    pallas_call x1, Pallas kernels, vertical_attention(): pl.pallas_call(kernel, grid_spec=grid_spec, out_shape=jax.ShapeDtypeStruc...  12.9 us
    ppermute x8, starting transfers between devices, ring(): lax.ppermute(block, axis, [(i, (i + distance) % size) for i in range(size)])  11 us
    ppermute x2, starting transfers between devices, shift(): return lax.ppermute(block, axis, route)  8.08 us
    convert_element_type x1, other arithmetic, local(): expo_diag.astype(jnp.bfloat16)  5.59 us
    dot_general x1, matrix products, local(): jnp.einsum('htu,ud->htd', expo_diag.astype(jnp.bfloat16), context_v, pref...  4.86 us
    dot_general x1, matrix products, local(): jnp.einsum('htd,ud->htu', query_heads, context_k, preferred_element_type=...  3.45 us
  transfers between devices with their start and end apart: 11, of which 5 were waited for; matrix products, arithmetic and copies ran while one was open for 25% of the time, Pallas kernels for 9%

profile of v10, /device:TPU:1, one launch (start us, length us, event | category | flops | bytes accessed | tf_op | source)
XLA Modules:
  0.0 138.5 jit_solution(8814700541629852022)
XLA Ops:
  6.5 0.7 broadcast_multiply_fusion
  7.2 0.1 reshape.355
  7.4 0.1 fusion.35
  7.5 0.6 convert_reduce_fusion.2
  8.1 0.1 convert_reduce_fusion.1
  8.9 1.0 bitcast_convert_fusion
  9.9 0.1 select_reduce_fusion.1
  10.1 0.6 pad_maximum_fusion.2
  10.8 1.0 pad_maximum_fusion.1
  11.8 4.7 %collective-permute-start = (bf16[2,8,64,128]{3,2,1,0:T(8,128)(2,1)S(1)}, bf16[2,8,64,128]{3,2,1,0:T(8,128)(2,1)}, u32[]{:S(2)}, u32[]{:S(2)}) collective-permute-start(bf16[2,8,64,128]{3,2,1,0:T(8,128)(2,1)S(1)} %pad_maximum_fusion.1), channel_id=1, source_target_pairs={{0,2},{1,3},{2,4},{3,5},{4,6},{5,7},{6,8},{7,9},{8,10},{9,11},{10,... | collective-permute-start | bytes 786440 | tf_op jit(solution)/shard_map/ppermute | solution.py:21
  16.5 3.3 %collective-permute-start.1 = (bf16[2,8,64,128]{3,2,1,0:T(8,128)(2,1)S(1)}, bf16[2,8,64,128]{3,2,1,0:T(8,128)(2,1)}, u32[]{:S(2)}, u32[]{:S(2)}) collective-permute-start(bf16[2,8,64,128]{3,2,1,0:T(8,128)(2,1)S(1)} %pad_maximum_fusion.1), channel_id=1, source_target_pairs={{0,1},{1,2},{2,3},{3,4},{4,5},{5,6},{6,7},{7,8},{8,9},{9,10},{10,1... | collective-permute-start | bytes 786440 | tf_op jit(solution)/shard_map/ppermute | solution.py:21
  19.9 1.5 %fusion.47 = (bf16[256,1024]{1,0:T(8,128)(2,1)S(1)}, bf16[256,1024]{1,0:T(8,128)(2,1)S(1)}, bf16[256,1024]{1,0:T(8,128)(2,1)S(1)}) fusion(bf16[512,4096]{1,0:T(8,128)(2,1)} %param.11, s32[]{:T(128)S(6)} %select_n.105, s32[]{:T(128)S(6)} %select_n.107, s32[]{:T(128)S(6)} %select_n.111, s32[]{:T(128)S(6)} %select_n.109), kind=kLoop, calls=%fused_computation.100 | loop fusion | bytes 3145744 | tf_op jit(solution)/shard_map/dynamic_slice | solution.py:165
  21.4 1.3 collective-permute-start.3
  22.7 2.5 %collective-permute-start.4 = (bf16[256,1024]{1,0:T(8,128)(2,1)S(1)}, bf16[256,1024]{1,0:T(8,128)(2,1)S(1)}, u32[]{:S(2)}, u32[]{:S(2)}) collective-permute-start(bf16[256,1024]{1,0:T(8,128)(2,1)S(1)} %get-tuple-element.15), channel_id=1, source_target_pairs={{0,128},{64,192},{128,0},{192,64},{1,129},{65,193},{129,1},{193,65... | collective-permute-start | bytes 1572872 | tf_op jit(solution)/shard_map/ppermute | solution.py:25
  25.1 1.2 collective-permute-start.5
  26.3 0.1 constant_dynamic-slice_fusion
  26.3 0.1 copy.23
  26.4 0.1 compare_reduce_fusion.1
  26.5 0.2 convert_reduce_fusion
  26.7 0.1 reduce_sum.57
  26.8 0.1 broadcast_subtract_fusion
  26.9 0.1 compare_reduce_fusion
  27.0 0.1 subtract_compare_fusion.1
  27.1 0.6 fusion.39.slots_ref
  27.7 8.8 %collective-permute-done.3 = bf16[256,1024]{1,0:T(8,128)(2,1)S(1)} collective-permute-done((bf16[256,1024]{1,0:T(8,128)(2,1)S(1)}, bf16[256,1024]{1,0:T(8,128)(2,1)S(1)}, u32[]{:S(2)}, u32[]{:S(2)}) %collective-permute-start.3) | collective-permute-done | bytes 524320 | tf_op jit(solution)/shard_map/ppermute | solution.py:25
  36.5 12.2 %collective-permute-done.4 = bf16[256,1024]{1,0:T(8,128)(2,1)S(1)} collective-permute-done((bf16[256,1024]{1,0:T(8,128)(2,1)S(1)}, bf16[256,1024]{1,0:T(8,128)(2,1)S(1)}, u32[]{:S(2)}, u32[]{:S(2)}) %collective-permute-start.4) | collective-permute-done | bytes 524320 | tf_op jit(solution)/shard_map/ppermute | solution.py:25
  48.7 1.3 pad_maximum_fusion
  50.0 0.5 collective-permute-start.6
  50.6 0.1 copy.24
  50.7 0.2 broadcast_in_dim.88
  50.9 0.2 reshape.358
  51.1 0.1 copy.25
  51.2 0.2 broadcast_in_dim.90
  51.3 0.2 reshape.360
  51.6 0.7 tile.2
  52.3 2.1 %and.167 = pred[512,1536]{0,1:T(8,128)(4,1)S(1)} reshape(pred[8,64,24,64]{1,0,3,2:T(8,128)(4,1)S(1)} %tile.2) | data formatting | bytes 1572864 | tf_op jit(solution)/shard_map/and | solution.py:197
  54.4 1.3 copy.21
  55.6 0.3 copy.22
  55.9 0.1 add.150
  56.0 0.1 add.151
  56.2 0.5 slice.25.first_ref
  56.7 0.1 pad.20.clone
  56.8 0.6 broadcast_add_fusion.key_tok_ref
  57.4 1.1 maximum_maximum_fusion.1
  58.6 3.4 %fusion = (f32[4,512]{1,0:T(4,128)S(1)}, f32[1536,4,512]{2,0,1:T(8,128)S(1)}) fusion(pred[512,1536]{0,1:T(8,128)(4,1)S(1)} %and.167, pred[4,512,24]{1,2,0:T(8,128)(4,1)S(1)} %reshape.360, pred[4,512,24]{1,2,0:T(8,128)(4,1)S(1)} %reshape.358, bf16[1536,128,1]{1,0,2:T(8,128)(2,1)S(1)} %bitcast.96, bf16[512,4,128]{2,0,1:T(8,128)(2,1)S(1)} %copy.22), kind=kOutput, calls=%fused_computation.2 | convolution fusion | flops 821032960 | bytes 14393344 | tf_op jit(solution)/shard_map/htd,ud->htu/dot_general | solution.py:189
  62.0 5.6 %fusion.5 = (bf16[4,512,1536]{1,2,0:T(8,128)(2,1)}, f32[4,512]{1,0:T(4,128)S(1)}) fusion(f32[1536,4,512]{2,0,1:T(8,128)S(1)} %get-tuple-element.28, f32[4,512]{1,0:T(4,128)S(1)} %get-tuple-element.27, pred[512,1536]{0,1:T(8,128)(4,1)S(1)} %and.167, pred[4,512,24]{1,2,0:T(8,128)(4,1)S(1)} %reshape.360, pred[4,512,24]{1,2,0:T(8,128)(4,1)S(1)} %reshape.358), kind=kLoop, calls=%fused_computation.8 | loop fusion | flops 22018048 | bytes 19775488 | tf_op jit(solution)/shard_map/convert_element_type | solution.py:205
  67.6 0.4 copy.30
  68.0 0.4 copy.29
  68.4 4.9 %fusion.49 = f32[4,512,128]{2,1,0:T(8,128)S(1)} fusion(bf16[4,512,1536]{1,2,0:T(8,128)(2,1)} %get-tuple-element.11, bf16[1536,128,1]{1,0,2:T(8,128)(2,1)S(1)} %bitcast.95), kind=kOutput, calls=%fused_computation.102 | convolution fusion | flops 805306368 | bytes 7733248 | tf_op jit(solution)/shard_map/htu,ud->htd/dot_general | solution.py:203
  73.2 1.7 %maximum_maximum_fusion.acc_ref = f32[4,512,256]{2,1,0:T(8,128)} fusion(f32[4,512,1]{2,1,0:T(8,128)S(1)} %copy.30, f32[4,512,1]{2,1,0:T(8,128)S(1)} %copy.29, f32[4,512,128]{2,1,0:T(8,128)S(1)} %fusion.49, f32[256]{0:T(256)S(1)} %pad.20.clone), kind=kLoop, calls=%fused_computation.9 | loop fusion | flops 1572864 | bytes 3163136 | tf_op jit(solution)/shard_map/concatenate | solution.py:83
  74.9 19.2 %all-gather.2.cloned.1.call-done = bf16[2,8192,128]{2,1,0:T(8,128)(2,1)} async-done(((bf16[2,128,128]{2,1,0:T(8,128)(2,1)}), bf16[2,8192,128]{2,1,0:T(8,128)(2,1)}) %all-gather.2.cloned.1.call-update) | async-done | bytes 4194320 | tf_op jit(solution)/shard_map/all_gather | solution.py:157
  94.2 12.9 %shard_map.64 = bf16[512,512]{1,0:T(8,128)(2,1)} custom-call(s32[4,16]{1,0:T(4,128)} %fusion.39.slots_ref, s32[1]{0:T(128)} %slice.25.first_ref, bf16[4,512,128]{2,1,0:T(8,128)(2,1)} %bitcast.91, bf16[2,128,64,128]{3,2,1,0:T(8,128)(2,1)} %bitcast.92, s32[4,1,1024]{2,1,0:T(1,128)} %broadcast_add_fusion.key_tok_ref, f32[4,512,256]{2,1,0:T(8,128)} %maximum_maximum_fusion.acc_ref), custom_call_target="tpu_custom_call" | custom-call | tf_op jit(solution)/shard_map/pallas_call | solution.py:103
  107.1 1.3 collective-permute-start.2
  108.4 1.5 %collective-permute-start.7 = (bf16[512,512]{1,0:T(8,128)(2,1)}, bf16[512,512]{1,0:T(8,128)(2,1)S(1)}, u32[]{:S(2)}, u32[]{:S(2)}) collective-permute-start(bf16[512,512]{1,0:T(8,128)(2,1)} %shard_map.64), channel_id=1, source_target_pairs={{0,192},{64,0},{128,64},{192,128},{1,193},{65,1},{129,65},{193,129... | collective-permute-start | bytes 1572872 | tf_op jit(solution)/shard_map/ppermute | solution.py:25
  109.9 1.5 %slice_bitcast_fusion = (bf16[256,1024]{1,0:T(8,128)(2,1)S(1)}, bf16[256,1024]{1,0:T(8,128)(2,1)S(1)}, bf16[256,1024]{1,0:T(8,128)(2,1)S(1)}) fusion(bf16[3,256,1024]{2,1,0:T(8,128)(2,1)} %collective-permute-done.6), kind=kLoop, calls=%fused_computation.39 | loop fusion | bytes 3145728 | tf_op jit(solution)/shard_map/squeeze | solution.py:227
  111.4 2.0 %fusion.24 = f32[512,1024]{1,0:T(8,128)S(1)} fusion(bf16[512,512]{1,0:T(8,128)(2,1)S(1)} %copy-done.2, bf16[512,4096]{1,0:T(8,128)(2,1)} %param.11, s32[]{:T(128)S(6)} %select_n.103), kind=kOutput, calls=%fused_computation.33 | convolution fusion | flops 536870912 | bytes 3670020 | tf_op jit(solution)/shard_map/dot_general | solution.py:237
  113.4 8.4 %collective-permute-done.2 = bf16[512,512]{1,0:T(8,128)(2,1)S(1)} collective-permute-done((bf16[512,512]{1,0:T(8,128)(2,1)}, bf16[512,512]{1,0:T(8,128)(2,1)S(1)}, u32[]{:S(2)}, u32[]{:S(2)}) %collective-permute-start.2) | collective-permute-done | bytes 524320 | tf_op jit(solution)/shard_map/ppermute | solution.py:25
  121.8 0.1 collective-permute-start.8
  122.0 2.7 %collective-permute-start.9 = (bf16[512,256]{1,0:T(8,128)(2,1)S(1)}, bf16[512,256]{1,0:T(8,128)(2,1)S(1)}, u32[]{:S(2)}, u32[]{:S(2)}) collective-permute-start(bf16[512,256]{1,0:T(8,128)(2,1)S(1)} %slice.38), channel_id=1, source_target_pairs={{0,192},{64,0},{128,64},{192,128},{1,193},{65,1},{129,65},{193,129... | collective-permute-start | bytes 786440 | tf_op jit(solution)/shard_map/ppermute | solution.py:25
  124.7 0.7 fusion.6
  125.4 0.3 copy-done.8
  125.7 0.7 fusion.12
  126.5 3.4 %collective-permute-done.8 = bf16[512,256]{1,0:T(8,128)(2,1)S(1)} collective-permute-done((bf16[512,256]{1,0:T(8,128)(2,1)S(1)}, bf16[512,256]{1,0:T(8,128)(2,1)S(1)}, u32[]{:S(2)}, u32[]{:S(2)}) %collective-permute-start.8) | collective-permute-done | bytes 262176 | tf_op jit(solution)/shard_map/ppermute | solution.py:25
  129.8 1.8 %add_convert_fusion = bf16[512,1024]{1,0:T(8,128)(2,1)} fusion(f32[512,1024]{1,0:T(8,128)S(1)} %fusion.12, f32[512,1024]{1,0:T(8,128)S(1)} %fusion.24, f32[512,1024]{1,0:T(8,128)S(1)} %fusion.6, bf16[256,1024]{1,0:T(8,128)(2,1)S(1)} %get-tuple-element.16, bf16[256,1024]{1,0:T(8,128)(2,1)S(1)} %collective-permute-done.4, pred[]{:T(512)S(6)} %eq.123, ...), kind=kOutput, calls=%fused_computation.10 | convolution fusion | flops 544735232 | bytes 8912897 | tf_op jit(solution)/shard_map/dot_general | solution.py:243
  (42 shorter events, 0.3 us)
Async XLA Ops:
  6.5 19.7 %copy-start = (s32[16,8]{0,1:T(8,128)S(1)}, s32[16,8]{0,1:T(8,128)}, u32[]{:S(2)}) copy-start(s32[16,8]{0,1:T(8,128)} %param.10) | copy-start | bytes 1540
  6.5 87.6 %all-gather.2.cloned.1.call-start = ((), (), s32[]{:S(2)}) async-start(), calls=%async_computation | async-start | bytes 4259840 | tf_op jit(solution)/shard_map/all_gather | solution.py:157
  11.8 45.6 %collective-permute-start = (bf16[2,8,64,128]{3,2,1,0:T(8,128)(2,1)S(1)}, bf16[2,8,64,128]{3,2,1,0:T(8,128)(2,1)}, u32[]{:S(2)}, u32[]{:S(2)}) collective-permute-start(bf16[2,8,64,128]{3,2,1,0:T(8,128)(2,1)S(1)} %pad_maximum_fusion.1), channel_id=1, source_target_pairs={{0,2},{1,3},{2,4},{3,5},{4,6},{5,7},{6,8},{7,9},{8,10},{9,11},{10,... | collective-permute-start | bytes 786440 | tf_op jit(solution)/shard_map/ppermute | solution.py:21
  16.5 40.9 %collective-permute-start.1 = (bf16[2,8,64,128]{3,2,1,0:T(8,128)(2,1)S(1)}, bf16[2,8,64,128]{3,2,1,0:T(8,128)(2,1)}, u32[]{:S(2)}, u32[]{:S(2)}) collective-permute-start(bf16[2,8,64,128]{3,2,1,0:T(8,128)(2,1)S(1)} %pad_maximum_fusion.1), channel_id=1, source_target_pairs={{0,1},{1,2},{2,3},{3,4},{4,5},{5,6},{6,7},{7,8},{8,9},{9,10},{10,1... | collective-permute-start | bytes 786440 | tf_op jit(solution)/shard_map/ppermute | solution.py:21
  21.4 15.1 %collective-permute-start.3 = (bf16[256,1024]{1,0:T(8,128)(2,1)S(1)}, bf16[256,1024]{1,0:T(8,128)(2,1)S(1)}, u32[]{:S(2)}, u32[]{:S(2)}) collective-permute-start(bf16[256,1024]{1,0:T(8,128)(2,1)S(1)} %get-tuple-element.13), channel_id=1, source_target_pairs={{0,64},{64,128},{128,192},{192,0},{1,65},{65,129},{129,193},{193,1... | collective-permute-start | bytes 1572872 | tf_op jit(solution)/shard_map/ppermute | solution.py:25
  22.7 26.0 %collective-permute-start.4 = (bf16[256,1024]{1,0:T(8,128)(2,1)S(1)}, bf16[256,1024]{1,0:T(8,128)(2,1)S(1)}, u32[]{:S(2)}, u32[]{:S(2)}) collective-permute-start(bf16[256,1024]{1,0:T(8,128)(2,1)S(1)} %get-tuple-element.15), channel_id=1, source_target_pairs={{0,128},{64,192},{128,0},{192,64},{1,129},{65,193},{129,1},{193,65... | collective-permute-start | bytes 1572872 | tf_op jit(solution)/shard_map/ppermute | solution.py:25
  25.1 23.6 %collective-permute-start.5 = (bf16[256,1024]{1,0:T(8,128)(2,1)S(1)}, bf16[256,1024]{1,0:T(8,128)(2,1)S(1)}, u32[]{:S(2)}, u32[]{:S(2)}) collective-permute-start(bf16[256,1024]{1,0:T(8,128)(2,1)S(1)} %get-tuple-element.14), channel_id=1, source_target_pairs={{0,192},{64,0},{128,64},{192,128},{1,193},{65,1},{129,65},{193,129... | collective-permute-start | bytes 1572872 | tf_op jit(solution)/shard_map/ppermute | solution.py:25
  36.5 15.1 %copy-start.5 = (bf16[256,1024]{1,0:T(8,128)(2,1)}, bf16[256,1024]{1,0:T(8,128)(2,1)S(1)}, u32[]{:S(2)}) copy-start(bf16[256,1024]{1,0:T(8,128)(2,1)S(1)} %collective-permute-done.3) | copy-start | bytes 1572868
  48.7 2.6 %copy-start.7 = (bf16[256,1024]{1,0:T(8,128)(2,1)}, bf16[256,1024]{1,0:T(8,128)(2,1)S(1)}, u32[]{:S(2)}) copy-start(bf16[256,1024]{1,0:T(8,128)(2,1)S(1)} %collective-permute-done.5) | copy-start | bytes 1572868
  50.0 59.9 %collective-permute-start.6 = (bf16[3,256,1024]{2,1,0:T(8,128)(2,1)}, bf16[3,256,1024]{2,1,0:T(8,128)(2,1)}, u32[]{:S(2)}, u32[]{:S(2)}) collective-permute-start(bf16[3,256,1024]{2,1,0:T(8,128)(2,1)} %pad_maximum_fusion), channel_id=1, source_target_pairs={{0,1},{1,0},{2,3},{3,2},{4,5},{5,4},{6,7},{7,6},{8,9},{9,8},{10,11... | collective-permute-start | bytes 4718600 | tf_op jit(solution)/shard_map/ppermute | solution.py:25
  52.2 5.1 %copy-start.3 = (bf16[512,128]{1,0:T(8,128)(2,1)S(1)}, bf16[512,128]{1,0:T(8,128)(2,1)}, u32[]{:S(2)}) copy-start(bf16[512,128]{1,0:T(8,128)(2,1)} %param.8) | copy-start | bytes 393220
  52.2 5.1 %copy-start.4 = (bf16[512,128]{1,0:T(8,128)(2,1)S(1)}, bf16[512,128]{1,0:T(8,128)(2,1)}, u32[]{:S(2)}) copy-start(bf16[512,128]{1,0:T(8,128)(2,1)} %param.7) | copy-start | bytes 393220
  55.9 6.1 %copy-start.1 = (bf16[512,4,128]{2,0,1:T(8,128)(2,1)}, bf16[512,4,128]{2,0,1:T(8,128)(2,1)S(1)}, u32[]{:S(2)}) copy-start(bf16[512,4,128]{2,0,1:T(8,128)(2,1)S(1)} %copy.22) | copy-start | bytes 1572868
  107.1 4.3 %copy-start.2 = (bf16[512,512]{1,0:T(8,128)(2,1)S(1)}, bf16[512,512]{1,0:T(8,128)(2,1)}, u32[]{:S(2)}) copy-start(bf16[512,512]{1,0:T(8,128)(2,1)} %shard_map.64) | copy-start | bytes 1572868
  107.1 14.7 %collective-permute-start.2 = (bf16[512,512]{1,0:T(8,128)(2,1)}, bf16[512,512]{1,0:T(8,128)(2,1)S(1)}, u32[]{:S(2)}, u32[]{:S(2)}) collective-permute-start(bf16[512,512]{1,0:T(8,128)(2,1)} %shard_map.64), channel_id=1, source_target_pairs={{0,64},{64,128},{128,192},{192,0},{1,65},{65,129},{129,193},{193,1... | collective-permute-start | bytes 1572872 | tf_op jit(solution)/shard_map/ppermute | solution.py:25
  108.4 13.5 %collective-permute-start.7 = (bf16[512,512]{1,0:T(8,128)(2,1)}, bf16[512,512]{1,0:T(8,128)(2,1)S(1)}, u32[]{:S(2)}, u32[]{:S(2)}) collective-permute-start(bf16[512,512]{1,0:T(8,128)(2,1)} %shard_map.64), channel_id=1, source_target_pairs={{0,192},{64,0},{128,64},{192,128},{1,193},{65,1},{129,65},{193,129... | collective-permute-start | bytes 1572872 | tf_op jit(solution)/shard_map/ppermute | solution.py:25
  111.4 13.3 %copy-start.6 = (bf16[256,1024]{1,0:T(8,128)(2,1)S(1)}, bf16[256,1024]{1,0:T(8,128)(2,1)}, u32[]{:S(2)}) copy-start(bf16[256,1024]{1,0:T(8,128)(2,1)} %copy-done.5) | copy-start | bytes 1572868
  121.8 8.0 %collective-permute-start.8 = (bf16[512,256]{1,0:T(8,128)(2,1)S(1)}, bf16[512,256]{1,0:T(8,128)(2,1)S(1)}, u32[]{:S(2)}, u32[]{:S(2)}) collective-permute-start(bf16[512,256]{1,0:T(8,128)(2,1)S(1)} %slice.37), channel_id=1, source_target_pairs={{0,64},{64,128},{128,192},{192,0},{1,65},{65,129},{129,193},{193,1... | collective-permute-start | bytes 786440 | tf_op jit(solution)/shard_map/ppermute | solution.py:25
  122.0 7.9 %collective-permute-start.9 = (bf16[512,256]{1,0:T(8,128)(2,1)S(1)}, bf16[512,256]{1,0:T(8,128)(2,1)S(1)}, u32[]{:S(2)}, u32[]{:S(2)}) collective-permute-start(bf16[512,256]{1,0:T(8,128)(2,1)S(1)} %slice.38), channel_id=1, source_target_pairs={{0,192},{64,0},{128,64},{192,128},{1,193},{65,1},{129,65},{193,129... | collective-permute-start | bytes 786440 | tf_op jit(solution)/shard_map/ppermute | solution.py:25
  124.7 1.0 copy-start.8
Sparse Core Ops, SparseCore 0:
  10.9 83.2 all-gather.1

commit v11 on v9

--- a/solution.py
+++ b/solution.py
@@ -74,7 +74,7 @@
     sc = jnp.exp(top_d - top)
     total = acc_ref[0, :, dim + 1:dim + 2] * sc + jnp.sum(p, axis=1, keepdims=True)
     acc = jnp.dot(p.astype(jnp.bfloat16), v_buf[current], preferred_element_type=jnp.float32)
-    o_ref[...] = ((acc_ref[0, :, :dim] * sc + acc) / total).astype(o_ref.dtype)
+    o_ref[...] = ((acc_ref[0, :, :dim] * sc + acc) * (1.0 / total)).astype(o_ref.dtype)
 
 
 def vertical_attention(slots, q, kv, key_tok, query_tok, top_d, tot_d, acc_d, interpret=False):

time: 139 us -> 139 us (level)
  no operation moved by 1% of the time
where the time goes in v11:
time: 139 us; the launch traced here: 138 us
  waiting for transfers between devices  51.9 us (37%)
  starting transfers between devices  19.1 us (14%)
  other arithmetic  16.6 us (12%)
  between operations  14.4 us (10%)
  matrix products  13.6 us (10%)
  Pallas kernels  12.3 us (9%)
  local copies, waits for them, and re-layouts  9.99 us (7%)
    ppermute x8, waiting for transfers between devices, ring(): lax.ppermute(block, axis, [(i, (i + distance) % size) for i in range(size)])  32.8 us
    all_gather x1, waiting for transfers between devices, local(): arrived = lax.all_gather(outgoing, SEQ, axis=1, tiled=True)  19.1 us
    pallas_call x1, Pallas kernels, vertical_attention(): pl.pallas_call(kernel, grid_spec=grid_spec, out_shape=jax.ShapeDtypeStruc...  12.3 us
    ppermute x8, starting transfers between devices, ring(): lax.ppermute(block, axis, [(i, (i + distance) % size) for i in range(size)])  11 us
    ppermute x2, starting transfers between devices, shift(): return lax.ppermute(block, axis, route)  8.08 us
    convert_element_type x1, other arithmetic, local(): expo_diag.astype(jnp.bfloat16)  5.59 us
    dot_general x1, matrix products, local(): jnp.einsum('htu,ud->htd', expo_diag.astype(jnp.bfloat16), context_v, pref...  4.8 us
    dot_general x1, matrix products, local(): jnp.einsum('htd,ud->htu', query_heads, context_k, preferred_element_type=...  3.44 us
  transfers between devices with their start and end apart: 11, of which 5 were waited for; matrix products, arithmetic and copies ran while one was open for 25% of the time, Pallas kernels for 9%

profile of v11, /device:TPU:1, one launch (start us, length us, event | category | flops | bytes accessed | tf_op | source)
XLA Modules:
  0.0 137.9 jit_solution(7938782110093865468)
XLA Ops:
  6.5 0.7 broadcast_multiply_fusion
  7.2 0.1 reshape.360
  7.4 0.1 fusion.35
  7.5 0.6 convert_reduce_fusion.2
  8.1 0.1 convert_reduce_fusion.1
  8.9 1.0 bitcast_convert_fusion
  9.9 0.1 select_reduce_fusion.1
  10.1 0.6 pad_maximum_fusion.2
  10.8 1.0 pad_maximum_fusion.1
  11.8 4.7 %collective-permute-start = (bf16[2,8,64,128]{3,2,1,0:T(8,128)(2,1)S(1)}, bf16[2,8,64,128]{3,2,1,0:T(8,128)(2,1)}, u32[]{:S(2)}, u32[]{:S(2)}) collective-permute-start(bf16[2,8,64,128]{3,2,1,0:T(8,128)(2,1)S(1)} %pad_maximum_fusion.1), channel_id=1, source_target_pairs={{0,2},{1,3},{2,4},{3,5},{4,6},{5,7},{6,8},{7,9},{8,10},{9,11},{10,... | collective-permute-start | bytes 786440 | tf_op jit(solution)/shard_map/ppermute | solution.py:21
  16.5 3.3 %collective-permute-start.1 = (bf16[2,8,64,128]{3,2,1,0:T(8,128)(2,1)S(1)}, bf16[2,8,64,128]{3,2,1,0:T(8,128)(2,1)}, u32[]{:S(2)}, u32[]{:S(2)}) collective-permute-start(bf16[2,8,64,128]{3,2,1,0:T(8,128)(2,1)S(1)} %pad_maximum_fusion.1), channel_id=1, source_target_pairs={{0,1},{1,2},{2,3},{3,4},{4,5},{5,6},{6,7},{7,8},{8,9},{9,10},{10,1... | collective-permute-start | bytes 786440 | tf_op jit(solution)/shard_map/ppermute | solution.py:21
  19.9 1.5 %fusion.47 = (bf16[256,1024]{1,0:T(8,128)(2,1)S(1)}, bf16[256,1024]{1,0:T(8,128)(2,1)S(1)}, bf16[256,1024]{1,0:T(8,128)(2,1)S(1)}) fusion(bf16[512,4096]{1,0:T(8,128)(2,1)} %param.11, s32[]{:T(128)S(6)} %select_n.105, s32[]{:T(128)S(6)} %select_n.107, s32[]{:T(128)S(6)} %select_n.111, s32[]{:T(128)S(6)} %select_n.109), kind=kLoop, calls=%fused_computation.100 | loop fusion | bytes 3145744 | tf_op jit(solution)/shard_map/dynamic_slice | solution.py:165
  21.4 1.3 collective-permute-start.3
  22.7 2.5 %collective-permute-start.4 = (bf16[256,1024]{1,0:T(8,128)(2,1)S(1)}, bf16[256,1024]{1,0:T(8,128)(2,1)S(1)}, u32[]{:S(2)}, u32[]{:S(2)}) collective-permute-start(bf16[256,1024]{1,0:T(8,128)(2,1)S(1)} %get-tuple-element.15), channel_id=1, source_target_pairs={{0,128},{64,192},{128,0},{192,64},{1,129},{65,193},{129,1},{193,65... | collective-permute-start | bytes 1572872 | tf_op jit(solution)/shard_map/ppermute | solution.py:25
  25.1 1.2 collective-permute-start.5
  26.3 0.1 constant_dynamic-slice_fusion
  26.3 0.1 copy.23
  26.4 0.1 compare_reduce_fusion.1
  26.5 0.2 convert_reduce_fusion
  26.7 0.1 reduce_sum.57
  26.8 0.1 broadcast_subtract_fusion
  26.9 0.1 compare_reduce_fusion
  27.0 0.1 subtract_compare_fusion.1
  27.1 0.5 fusion.39.slots_ref
  27.6 8.8 %collective-permute-done.3 = bf16[256,1024]{1,0:T(8,128)(2,1)S(1)} collective-permute-done((bf16[256,1024]{1,0:T(8,128)(2,1)S(1)}, bf16[256,1024]{1,0:T(8,128)(2,1)S(1)}, u32[]{:S(2)}, u32[]{:S(2)}) %collective-permute-start.3) | collective-permute-done | bytes 524320 | tf_op jit(solution)/shard_map/ppermute | solution.py:25
  36.5 12.2 %collective-permute-done.4 = bf16[256,1024]{1,0:T(8,128)(2,1)S(1)} collective-permute-done((bf16[256,1024]{1,0:T(8,128)(2,1)S(1)}, bf16[256,1024]{1,0:T(8,128)(2,1)S(1)}, u32[]{:S(2)}, u32[]{:S(2)}) %collective-permute-start.4) | collective-permute-done | bytes 524320 | tf_op jit(solution)/shard_map/ppermute | solution.py:25
  48.7 1.3 pad_maximum_fusion
  50.0 0.5 collective-permute-start.6
  50.6 0.8 iota_add_fusion.query_tok_ref
  51.3 0.1 copy.24
  51.4 0.2 broadcast_in_dim.88
  51.6 0.2 reshape.363
  51.8 0.1 copy.25
  51.9 0.2 broadcast_in_dim.90
  52.1 0.2 reshape.365
  52.3 0.7 tile.2
  53.0 2.1 %and.167 = pred[512,1536]{0,1:T(8,128)(4,1)S(1)} reshape(pred[8,64,24,64]{1,0,3,2:T(8,128)(4,1)S(1)} %tile.2) | data formatting | bytes 1572864 | tf_op jit(solution)/shard_map/and | solution.py:197
  55.1 1.3 copy.21
  56.4 0.3 copy.22
  56.7 0.1 add.155
  56.7 0.1 add.156
  56.9 0.1 pad.20.clone
  57.0 0.6 broadcast_add_fusion.key_tok_ref
  57.6 1.1 maximum_maximum_fusion.1
  58.8 3.4 %fusion = (f32[4,512]{1,0:T(4,128)S(1)}, f32[1536,4,512]{2,0,1:T(8,128)S(1)}) fusion(pred[512,1536]{0,1:T(8,128)(4,1)S(1)} %and.167, pred[4,512,24]{1,2,0:T(8,128)(4,1)S(1)} %reshape.365, pred[4,512,24]{1,2,0:T(8,128)(4,1)S(1)} %reshape.363, bf16[1536,128,1]{1,0,2:T(8,128)(2,1)S(1)} %bitcast.96, bf16[512,4,128]{2,0,1:T(8,128)(2,1)S(1)} %copy.22), kind=kOutput, calls=%fused_computation.2 | convolution fusion | flops 821032960 | bytes 14393344 | tf_op jit(solution)/shard_map/htd,ud->htu/dot_general | solution.py:189
  62.3 5.6 %fusion.5 = (bf16[4,512,1536]{1,2,0:T(8,128)(2,1)}, f32[4,512]{1,0:T(4,128)S(1)}) fusion(f32[1536,4,512]{2,0,1:T(8,128)S(1)} %get-tuple-element.28, f32[4,512]{1,0:T(4,128)S(1)} %get-tuple-element.27, pred[512,1536]{0,1:T(8,128)(4,1)S(1)} %and.167, pred[4,512,24]{1,2,0:T(8,128)(4,1)S(1)} %reshape.365, pred[4,512,24]{1,2,0:T(8,128)(4,1)S(1)} %reshape.363), kind=kLoop, calls=%fused_computation.8 | loop fusion | flops 22018048 | bytes 19775488 | tf_op jit(solution)/shard_map/convert_element_type | solution.py:205
  67.8 0.4 copy.30
  68.2 0.4 copy.29
  68.6 4.8 %fusion.49 = f32[4,512,128]{2,1,0:T(8,128)S(1)} fusion(bf16[4,512,1536]{1,2,0:T(8,128)(2,1)} %get-tuple-element.11, bf16[1536,128,1]{1,0,2:T(8,128)(2,1)S(1)} %bitcast.95), kind=kOutput, calls=%fused_computation.102 | convolution fusion | flops 805306368 | bytes 7733248 | tf_op jit(solution)/shard_map/htu,ud->htd/dot_general | solution.py:203
  73.4 1.7 %maximum_maximum_fusion.acc_ref = f32[4,512,256]{2,1,0:T(8,128)} fusion(f32[4,512,1]{2,1,0:T(8,128)S(1)} %copy.30, f32[4,512,1]{2,1,0:T(8,128)S(1)} %copy.29, f32[4,512,128]{2,1,0:T(8,128)S(1)} %fusion.49, f32[256]{0:T(256)S(1)} %pad.20.clone), kind=kLoop, calls=%fused_computation.9 | loop fusion | flops 1572864 | bytes 3163136 | tf_op jit(solution)/shard_map/concatenate | solution.py:82
  75.1 19.1 %all-gather.2.cloned.1.call-done = bf16[2,8192,128]{2,1,0:T(8,128)(2,1)} async-done(((bf16[2,128,128]{2,1,0:T(8,128)(2,1)}), bf16[2,8192,128]{2,1,0:T(8,128)(2,1)}) %all-gather.2.cloned.1.call-update) | async-done | bytes 4194320 | tf_op jit(solution)/shard_map/all_gather | solution.py:157
  94.2 12.3 %shard_map.64 = bf16[512,512]{1,0:T(8,128)(2,1)} custom-call(s32[4,16]{1,0:T(4,128)} %fusion.39.slots_ref, bf16[4,512,128]{2,1,0:T(8,128)(2,1)} %bitcast.91, bf16[2,128,64,128]{3,2,1,0:T(8,128)(2,1)} %bitcast.92, s32[4,1,1024]{2,1,0:T(1,128)} %broadcast_add_fusion.key_tok_ref, s32[512,1]{1,0:T(8,128)} %iota_add_fusion.query_tok_ref, ...), custom_call_target="tpu_custom_call" | custom-call | tf_op jit(solution)/shard_map/pallas_call | solution.py:103
  106.5 1.3 collective-permute-start.2
  107.7 1.5 %collective-permute-start.7 = (bf16[512,512]{1,0:T(8,128)(2,1)}, bf16[512,512]{1,0:T(8,128)(2,1)S(1)}, u32[]{:S(2)}, u32[]{:S(2)}) collective-permute-start(bf16[512,512]{1,0:T(8,128)(2,1)} %shard_map.64), channel_id=1, source_target_pairs={{0,192},{64,0},{128,64},{192,128},{1,193},{65,1},{129,65},{193,129... | collective-permute-start | bytes 1572872 | tf_op jit(solution)/shard_map/ppermute | solution.py:25
  109.3 1.5 %slice_bitcast_fusion = (bf16[256,1024]{1,0:T(8,128)(2,1)S(1)}, bf16[256,1024]{1,0:T(8,128)(2,1)S(1)}, bf16[256,1024]{1,0:T(8,128)(2,1)S(1)}) fusion(bf16[3,256,1024]{2,1,0:T(8,128)(2,1)} %collective-permute-done.6), kind=kLoop, calls=%fused_computation.39 | loop fusion | bytes 3145728 | tf_op jit(solution)/shard_map/squeeze | solution.py:227
  110.8 2.0 %fusion.24 = f32[512,1024]{1,0:T(8,128)S(1)} fusion(bf16[512,512]{1,0:T(8,128)(2,1)S(1)} %copy-done.2, bf16[512,4096]{1,0:T(8,128)(2,1)} %param.11, s32[]{:T(128)S(6)} %select_n.103), kind=kOutput, calls=%fused_computation.33 | convolution fusion | flops 536870912 | bytes 3670020 | tf_op jit(solution)/shard_map/dot_general | solution.py:237
  112.8 8.4 %collective-permute-done.2 = bf16[512,512]{1,0:T(8,128)(2,1)S(1)} collective-permute-done((bf16[512,512]{1,0:T(8,128)(2,1)}, bf16[512,512]{1,0:T(8,128)(2,1)S(1)}, u32[]{:S(2)}, u32[]{:S(2)}) %collective-permute-start.2) | collective-permute-done | bytes 524320 | tf_op jit(solution)/shard_map/ppermute | solution.py:25
  121.2 0.1 collective-permute-start.8
  121.3 2.7 %collective-permute-start.9 = (bf16[512,256]{1,0:T(8,128)(2,1)S(1)}, bf16[512,256]{1,0:T(8,128)(2,1)S(1)}, u32[]{:S(2)}, u32[]{:S(2)}) collective-permute-start(bf16[512,256]{1,0:T(8,128)(2,1)S(1)} %slice.33), channel_id=1, source_target_pairs={{0,192},{64,0},{128,64},{192,128},{1,193},{65,1},{129,65},{193,129... | collective-permute-start | bytes 786440 | tf_op jit(solution)/shard_map/ppermute | solution.py:25
  124.1 0.7 fusion.6
  124.8 0.3 copy-done.8
  125.1 0.7 fusion.12
  125.8 3.4 %collective-permute-done.8 = bf16[512,256]{1,0:T(8,128)(2,1)S(1)} collective-permute-done((bf16[512,256]{1,0:T(8,128)(2,1)S(1)}, bf16[512,256]{1,0:T(8,128)(2,1)S(1)}, u32[]{:S(2)}, u32[]{:S(2)}) %collective-permute-start.8) | collective-permute-done | bytes 262176 | tf_op jit(solution)/shard_map/ppermute | solution.py:25
  129.2 1.8 %add_convert_fusion = bf16[512,1024]{1,0:T(8,128)(2,1)} fusion(f32[512,1024]{1,0:T(8,128)S(1)} %fusion.12, f32[512,1024]{1,0:T(8,128)S(1)} %fusion.24, f32[512,1024]{1,0:T(8,128)S(1)} %fusion.6, bf16[256,1024]{1,0:T(8,128)(2,1)S(1)} %get-tuple-element.16, bf16[256,1024]{1,0:T(8,128)(2,1)S(1)} %collective-permute-done.4, pred[]{:T(512)S(6)} %eq.123, ...), kind=kOutput, calls=%fused_computation.10 | convolution fusion | flops 544735232 | bytes 8912897 | tf_op jit(solution)/shard_map/dot_general | solution.py:243
  (41 shorter events, 0.3 us)
Async XLA Ops:
  6.5 19.7 %copy-start = (s32[16,8]{0,1:T(8,128)S(1)}, s32[16,8]{0,1:T(8,128)}, u32[]{:S(2)}) copy-start(s32[16,8]{0,1:T(8,128)} %param.10) | copy-start | bytes 1540
  6.5 87.6 %all-gather.2.cloned.1.call-start = ((), (), s32[]{:S(2)}) async-start(), calls=%async_computation | async-start | bytes 4259840 | tf_op jit(solution)/shard_map/all_gather | solution.py:157
  11.8 45.9 %collective-permute-start = (bf16[2,8,64,128]{3,2,1,0:T(8,128)(2,1)S(1)}, bf16[2,8,64,128]{3,2,1,0:T(8,128)(2,1)}, u32[]{:S(2)}, u32[]{:S(2)}) collective-permute-start(bf16[2,8,64,128]{3,2,1,0:T(8,128)(2,1)S(1)} %pad_maximum_fusion.1), channel_id=1, source_target_pairs={{0,2},{1,3},{2,4},{3,5},{4,6},{5,7},{6,8},{7,9},{8,10},{9,11},{10,... | collective-permute-start | bytes 786440 | tf_op jit(solution)/shard_map/ppermute | solution.py:21
  16.5 41.1 %collective-permute-start.1 = (bf16[2,8,64,128]{3,2,1,0:T(8,128)(2,1)S(1)}, bf16[2,8,64,128]{3,2,1,0:T(8,128)(2,1)}, u32[]{:S(2)}, u32[]{:S(2)}) collective-permute-start(bf16[2,8,64,128]{3,2,1,0:T(8,128)(2,1)S(1)} %pad_maximum_fusion.1), channel_id=1, source_target_pairs={{0,1},{1,2},{2,3},{3,4},{4,5},{5,6},{6,7},{7,8},{8,9},{9,10},{10,1... | collective-permute-start | bytes 786440 | tf_op jit(solution)/shard_map/ppermute | solution.py:21
  21.4 15.1 %collective-permute-start.3 = (bf16[256,1024]{1,0:T(8,128)(2,1)S(1)}, bf16[256,1024]{1,0:T(8,128)(2,1)S(1)}, u32[]{:S(2)}, u32[]{:S(2)}) collective-permute-start(bf16[256,1024]{1,0:T(8,128)(2,1)S(1)} %get-tuple-element.13), channel_id=1, source_target_pairs={{0,64},{64,128},{128,192},{192,0},{1,65},{65,129},{129,193},{193,1... | collective-permute-start | bytes 1572872 | tf_op jit(solution)/shard_map/ppermute | solution.py:25
  22.7 26.0 %collective-permute-start.4 = (bf16[256,1024]{1,0:T(8,128)(2,1)S(1)}, bf16[256,1024]{1,0:T(8,128)(2,1)S(1)}, u32[]{:S(2)}, u32[]{:S(2)}) collective-permute-start(bf16[256,1024]{1,0:T(8,128)(2,1)S(1)} %get-tuple-element.15), channel_id=1, source_target_pairs={{0,128},{64,192},{128,0},{192,64},{1,129},{65,193},{129,1},{193,65... | collective-permute-start | bytes 1572872 | tf_op jit(solution)/shard_map/ppermute | solution.py:25
  25.1 23.6 %collective-permute-start.5 = (bf16[256,1024]{1,0:T(8,128)(2,1)S(1)}, bf16[256,1024]{1,0:T(8,128)(2,1)S(1)}, u32[]{:S(2)}, u32[]{:S(2)}) collective-permute-start(bf16[256,1024]{1,0:T(8,128)(2,1)S(1)} %get-tuple-element.14), channel_id=1, source_target_pairs={{0,192},{64,0},{128,64},{192,128},{1,193},{65,1},{129,65},{193,129... | collective-permute-start | bytes 1572872 | tf_op jit(solution)/shard_map/ppermute | solution.py:25
  36.5 15.8 %copy-start.5 = (bf16[256,1024]{1,0:T(8,128)(2,1)}, bf16[256,1024]{1,0:T(8,128)(2,1)S(1)}, u32[]{:S(2)}) copy-start(bf16[256,1024]{1,0:T(8,128)(2,1)S(1)} %collective-permute-done.3) | copy-start | bytes 1572868
  48.7 3.4 %copy-start.7 = (bf16[256,1024]{1,0:T(8,128)(2,1)}, bf16[256,1024]{1,0:T(8,128)(2,1)S(1)}, u32[]{:S(2)}) copy-start(bf16[256,1024]{1,0:T(8,128)(2,1)S(1)} %collective-permute-done.5) | copy-start | bytes 1572868
  50.0 59.3 %collective-permute-start.6 = (bf16[3,256,1024]{2,1,0:T(8,128)(2,1)}, bf16[3,256,1024]{2,1,0:T(8,128)(2,1)}, u32[]{:S(2)}, u32[]{:S(2)}) collective-permute-start(bf16[3,256,1024]{2,1,0:T(8,128)(2,1)} %pad_maximum_fusion), channel_id=1, source_target_pairs={{0,1},{1,0},{2,3},{3,2},{4,5},{5,4},{6,7},{7,6},{8,9},{9,8},{10,11... | collective-permute-start | bytes 4718600 | tf_op jit(solution)/shard_map/ppermute | solution.py:25
  53.0 4.6 %copy-start.3 = (bf16[512,128]{1,0:T(8,128)(2,1)S(1)}, bf16[512,128]{1,0:T(8,128)(2,1)}, u32[]{:S(2)}) copy-start(bf16[512,128]{1,0:T(8,128)(2,1)} %param.8) | copy-start | bytes 393220
  53.0 4.6 %copy-start.4 = (bf16[512,128]{1,0:T(8,128)(2,1)S(1)}, bf16[512,128]{1,0:T(8,128)(2,1)}, u32[]{:S(2)}) copy-start(bf16[512,128]{1,0:T(8,128)(2,1)} %param.7) | copy-start | bytes 393220
  56.7 5.6 %copy-start.1 = (bf16[512,4,128]{2,0,1:T(8,128)(2,1)}, bf16[512,4,128]{2,0,1:T(8,128)(2,1)S(1)}, u32[]{:S(2)}) copy-start(bf16[512,4,128]{2,0,1:T(8,128)(2,1)S(1)} %copy.22) | copy-start | bytes 1572868
  106.5 4.3 %copy-start.2 = (bf16[512,512]{1,0:T(8,128)(2,1)S(1)}, bf16[512,512]{1,0:T(8,128)(2,1)}, u32[]{:S(2)}) copy-start(bf16[512,512]{1,0:T(8,128)(2,1)} %shard_map.64) | copy-start | bytes 1572868
  106.5 14.7 %collective-permute-start.2 = (bf16[512,512]{1,0:T(8,128)(2,1)}, bf16[512,512]{1,0:T(8,128)(2,1)S(1)}, u32[]{:S(2)}, u32[]{:S(2)}) collective-permute-start(bf16[512,512]{1,0:T(8,128)(2,1)} %shard_map.64), channel_id=1, source_target_pairs={{0,64},{64,128},{128,192},{192,0},{1,65},{65,129},{129,193},{193,1... | collective-permute-start | bytes 1572872 | tf_op jit(solution)/shard_map/ppermute | solution.py:25
  107.7 13.5 %collective-permute-start.7 = (bf16[512,512]{1,0:T(8,128)(2,1)}, bf16[512,512]{1,0:T(8,128)(2,1)S(1)}, u32[]{:S(2)}, u32[]{:S(2)}) collective-permute-start(bf16[512,512]{1,0:T(8,128)(2,1)} %shard_map.64), channel_id=1, source_target_pairs={{0,192},{64,0},{128,64},{192,128},{1,193},{65,1},{129,65},{193,129... | collective-permute-start | bytes 1572872 | tf_op jit(solution)/shard_map/ppermute | solution.py:25
  110.8 13.3 %copy-start.6 = (bf16[256,1024]{1,0:T(8,128)(2,1)S(1)}, bf16[256,1024]{1,0:T(8,128)(2,1)}, u32[]{:S(2)}) copy-start(bf16[256,1024]{1,0:T(8,128)(2,1)} %copy-done.5) | copy-start | bytes 1572868
  121.2 8.0 %collective-permute-start.8 = (bf16[512,256]{1,0:T(8,128)(2,1)S(1)}, bf16[512,256]{1,0:T(8,128)(2,1)S(1)}, u32[]{:S(2)}, u32[]{:S(2)}) collective-permute-start(bf16[512,256]{1,0:T(8,128)(2,1)S(1)} %slice.32), channel_id=1, source_target_pairs={{0,64},{64,128},{128,192},{192,0},{1,65},{65,129},{129,193},{193,1... | collective-permute-start | bytes 786440 | tf_op jit(solution)/shard_map/ppermute | solution.py:25
  121.3 7.9 %collective-permute-start.9 = (bf16[512,256]{1,0:T(8,128)(2,1)S(1)}, bf16[512,256]{1,0:T(8,128)(2,1)S(1)}, u32[]{:S(2)}, u32[]{:S(2)}) collective-permute-start(bf16[512,256]{1,0:T(8,128)(2,1)S(1)} %slice.33), channel_id=1, source_target_pairs={{0,192},{64,0},{128,64},{192,128},{1,193},{65,1},{129,65},{193,129... | collective-permute-start | bytes 786440 | tf_op jit(solution)/shard_map/ppermute | solution.py:25
  124.1 1.0 copy-start.8
Sparse Core Ops, SparseCore 0:
  10.9 83.2 all-gather.1
